TPU v7x, 256 devices: a whole 4x4x8 slice. The times are simulated.
256 devices in a mesh: tm: 16 (over z, core), row: 2 (over x_hi), col: 8 (over y, x_lo).
Axes of the slice: x: 4 (x_hi: 2, x_lo: 2; x = x_hi * 2 + x_lo), y: 4, z: 8, core: 2. Of those that a mesh axis runs over, the one named last changes fastest.
Arguments:
- latents: bfloat16 [32, 64, 40960], P('tm', 'row', 'col'), may hold values from -6 to 6
- w_qkv: bfloat16 [320, 960], replicated, may hold values from -4 to 4
- w_out: bfloat16 [320, 320], replicated, may hold values from -0.3125 to 0.3125
- conv_weight: float32 [9, 320], replicated, may hold values from -1.8 to 1.8
Outputs:
- result: bfloat16 [32, 64, 40960], P('tm', 'row', 'col')
All inputs are finite; a program needn't handle non-finite values.
Results may differ from a plain program's by a relative error of at most 0.013.
Values may be sent and summed in bfloat16 or wider, within the bound.
No kernel may reach another device: no remote copies, remote signals or barrier semaphores. Data moves between devices by JAX's collectives and lax.ppermute only.
A program may use at most 64 MiB of HBM per device.

v0:
```python
import jax
import jax.numpy as jnp
from jax import lax
from jax.sharding import PartitionSpec as P

HEAD_DIM = 64


def padded_2(cells, sides, width):
    for axis, dim in sides:
        count = lax.axis_size(axis)
        ends = count - 1
        head = lax.slice_in_dim(cells, 0, width, axis=dim)
        tail = lax.slice_in_dim(cells, cells.shape[dim] - width, cells.shape[dim], axis=dim)
        cells = jnp.concatenate(
            [
                lax.ppermute(tail, axis, [(i, (i + 1) % count) for i in range(ends)]),
                cells,
                lax.ppermute(head, axis, [((i + 1) % count, i) for i in range(ends)]),
            ],
            axis=dim,
        )
    return cells


def layer_norm(flat):
    mean = jnp.mean(flat, axis=-1, keepdims=True)
    cent = flat - mean
    var = jnp.mean(cent * cent, axis=-1, keepdims=True)
    return (cent * lax.rsqrt(var + 1e-05)).astype(jnp.bfloat16)


def body(latents, w_qkv, w_out, conv_weight):
    frames, rows, merged = latents.shape
    chans = w_out.shape[0]
    cols = merged // chans
    points = rows * cols
    flat = latents.reshape(frames * points, chans).astype(jnp.float32)
    normed = layer_norm(flat)
    query = jnp.dot(normed, w_qkv[:, :chans], preferred_element_type=jnp.float32).astype(
        jnp.bfloat16
    )
    query = query.reshape(frames, points, chans)
    keys_own = jnp.dot(
        normed, w_qkv[:, chans : 2 * chans], preferred_element_type=jnp.float32
    ).astype(jnp.bfloat16)
    vals_own = jnp.dot(normed, w_qkv[:, 2 * chans :], preferred_element_type=jnp.float32).astype(
        jnp.bfloat16
    )
    stacked_kv = jnp.stack(
        [keys_own.reshape(frames, points, chans), vals_own.reshape(frames, points, chans)], 0
    )
    wide = padded_2(stacked_kv, (("tm", 1),), 2)
    first = lax.axis_index("tm") * frames
    total = lax.axis_size("tm") * frames
    group = jnp.arange(chans, dtype=jnp.int32) // HEAD_DIM
    head_sum = (group[:, None] == group[None, :]).astype(jnp.float32)
    scale = HEAD_DIM ** (-0.5)
    q_wide = query.astype(jnp.float32)
    scores = []
    for shift_d in range(5):
        prod = q_wide * wide[0, shift_d : shift_d + frames].astype(jnp.float32)
        score = jnp.dot(
            prod.reshape(frames * points, chans), head_sum, precision=lax.Precision.HIGHEST
        )
        score = score.reshape(frames, points, chans) * scale
        where_t = first + jnp.arange(frames, dtype=jnp.int32) + (shift_d - 2)
        valid = (where_t >= 0) & (where_t < total)
        scores.append(jnp.where(valid[:, None, None], score, jnp.float32(-1e30)))
    stacked = jnp.stack(scores, 0)
    top = jnp.max(stacked, axis=0, keepdims=True)
    expo = jnp.exp(stacked - top)
    weights = (expo / jnp.sum(expo, axis=0, keepdims=True)).astype(jnp.bfloat16)
    mixed = jnp.zeros((frames, points, chans), jnp.float32)
    for shift_d in range(5):
        mixed = mixed + weights[shift_d].astype(jnp.float32) * wide[
            1, shift_d : shift_d + frames
        ].astype(jnp.float32)
    attended = mixed.astype(jnp.bfloat16).reshape(frames * points, chans)
    proj = jnp.dot(attended, w_out, preferred_element_type=jnp.float32)
    hidden = (flat + proj).astype(jnp.bfloat16).reshape(frames, rows, cols * chans)
    tall = padded_2(hidden, (("row", 1),), 1)
    padded = padded_2(tall, (("col", 2),), chans)
    taps = jnp.tile(conv_weight, (1, cols))
    acc = hidden.astype(jnp.float32)
    span = cols * chans
    for tap_a in range(3):
        for tap_b in range(3):
            acc = (
                acc
                + padded[:, tap_a : tap_a + rows, tap_b * chans : tap_b * chans + span].astype(
                    jnp.float32
                )
                * taps[3 * tap_a + tap_b]
            )
    return acc.astype(jnp.bfloat16)


def solution(mesh):
    placed = (P("tm", "row", "col"), P(), P(), P())
    return jax.shard_map(
        body, mesh=mesh, in_specs=placed, out_specs=P("tm", "row", "col"), check_vma=False
    )
```

profile of v0, /device:TPU:111, one launch (start us, length us, event | category | flops | bytes accessed | tf_op | source)
XLA Modules:
  0.0 93.2 jit_solution(8871701909744382278)
XLA Ops:
  0.0 1.7 %reshape.198 = f32[1024,320]{1,0:T(8,128)S(1)} reshape(bf16[2,32,5120]{2,1,0:T(8,128)(2,1)} %param.4) | data formatting | bytes 1966080 | tf_op jit(solution)/shard_map/convert_element_type | solution.py:38
  1.9 0.4 multiply_reduce_fusion
  2.3 0.3 multiply_convert_fusion
  2.7 0.7 copy-done.4
  3.4 0.6 convolution_convert_fusion.1
  4.0 1.4 %convolution_convert_fusion = bf16[1024,320]{0,1:T(8,128)(2,1)} fusion(bf16[1024,320]{1,0:T(8,128)(2,1)S(1)} %multiply_convert_fusion, bf16[320,960]{1,0:T(8,128)(2,1)S(1)} %copy-done.4), kind=kOutput, calls=%fused_computation.24 | convolution fusion | flops 210042880 | bytes 1687552 | tf_op jit(solution)/shard_map/dot_general | solution.py:47
  5.5 1.3 %stack_reshape.6 = bf16[1,2,512,320]{2,1,3,0:T(2,128)(2,1)} reshape(bf16[1024,320]{0,1:T(8,128)(2,1)S(1)} %convolution_convert_fusion.1) | data formatting | bytes 1310720 | tf_op jit(solution)/shard_map/stack;reshape | solution.py:50
  6.8 2.0 %copy_dynamic-update-slice_fusion.1 = bf16[2,2,512,320]{2,3,1,0:T(8,128)(2,1)} fusion(bf16[1,2,512,320]{2,1,3,0:T(2,128)(2,1)} %stack_reshape.6), kind=kLoop, calls=%fused_computation.68 | loop fusion | bytes 1310720
  8.8 3.0 %stack_reshape.7 = bf16[1,2,512,320]{2,1,3,0:T(2,128)(2,1)} reshape(bf16[1024,320]{0,1:T(8,128)(2,1)} %convolution_convert_fusion) | data formatting | bytes 1310720 | tf_op jit(solution)/shard_map/stack;reshape | solution.py:50
  11.7 2.0 %copy_dynamic-update-slice_fusion = bf16[2,2,512,320]{2,3,1,0:T(8,128)(2,1)} fusion(bf16[2,2,512,320]{2,3,1,0:T(8,128)(2,1)} %copy_dynamic-update-slice_fusion.1, bf16[1,2,512,320]{2,1,3,0:T(2,128)(2,1)} %stack_reshape.7), kind=kLoop, calls=%fused_computation.67 | loop fusion | bytes 1310720 | tf_op jit(solution)/shard_map/stack | solution.py:50
  13.7 5.3 %collective-permute-start = (bf16[2,2,512,320]{2,3,1,0:T(8,128)(2,1)}, bf16[2,2,512,320]{2,3,1,0:T(8,128)(2,1)}, u32[]{:S(2)}, u32[]{:S(2)}) collective-permute-start(bf16[2,2,512,320]{2,3,1,0:T(8,128)(2,1)} %copy_dynamic-update-slice_fusion), channel_id=1, source_target_pairs={{0,16},{16,32},{32,48},{48,64},{64,80},{80,96},{96,112},{112,128},... | collective-permute-start | bytes 3932168 | tf_op jit(solution)/shard_map/ppermute | solution.py:17
  19.1 2.1 %collective-permute-start.1 = (bf16[2,2,512,320]{2,3,1,0:T(8,128)(2,1)}, bf16[2,2,512,320]{2,3,1,0:T(8,128)(2,1)}, u32[]{:S(2)}, u32[]{:S(2)}) collective-permute-start(bf16[2,2,512,320]{2,3,1,0:T(8,128)(2,1)} %copy_dynamic-update-slice_fusion), channel_id=1, source_target_pairs={{16,0},{32,16},{48,32},{64,48},{80,64},{96,80},{112,96},{128,112},... | collective-permute-start | bytes 3932168 | tf_op jit(solution)/shard_map/ppermute | solution.py:19
  21.2 1.5 %copy.35 = f32[1024,320]{0,1:T(8,128)} copy(f32[1024,320]{1,0:T(8,128)S(1)} %reshape.198) | data formatting | bytes 2621440 | tf_op jit(solution)/shard_map/convert_element_type | solution.py:38
  22.7 11.2 %collective-permute-done = bf16[2,2,512,320]{2,3,1,0:T(8,128)(2,1)} collective-permute-done((bf16[2,2,512,320]{2,3,1,0:T(8,128)(2,1)}, bf16[2,2,512,320]{2,3,1,0:T(8,128)(2,1)}, u32[]{:S(2)}, u32[]{:S(2)}) %collective-permute-start) | collective-permute-done | bytes 1310752 | tf_op jit(solution)/shard_map/ppermute | solution.py:17
  33.9 5.6 %collective-permute-done.1 = bf16[2,2,512,320]{2,3,1,0:T(8,128)(2,1)} collective-permute-done((bf16[2,2,512,320]{2,3,1,0:T(8,128)(2,1)}, bf16[2,2,512,320]{2,3,1,0:T(8,128)(2,1)}, u32[]{:S(2)}, u32[]{:S(2)}) %collective-permute-start.1) | collective-permute-done | bytes 1310752 | tf_op jit(solution)/shard_map/ppermute | solution.py:19
  39.5 2.4 %slice_convert_fusion.1 = (f32[1,2,512,320]{2,3,1,0:T(8,128)S(1)}, f32[1,2,512,320]{2,3,1,0:T(8,128)S(1)}, f32[1,2,512,320]{2,3,1,0:T(8,128)S(1)}, f32[1,2,512,320]{2,3,1,0:T(8,128)S(1)}) fusion(bf16[2,2,512,320]{2,3,1,0:T(8,128)(2,1)} %collective-permute-done.1, bf16[2,2,512,320]{2,3,1,0:T(8,128)(2,1)} %copy_dynamic-update-slice_fusion, ...), kind=kLoop, calls=%fused_computation.63 | loop fusion | flops 1966080 | bytes 10485760 | tf_op jit(solution)/shard_map/convert_element_type | solution.py:62
  41.9 1.0 %copy.29 = f32[1,2,512,320]{2,1,3,0:T(2,128)S(1)} copy(f32[1,2,512,320]{2,3,1,0:T(8,128)S(1)} %get-tuple-element.17) | data formatting | bytes 2621440 | tf_op jit(solution)/shard_map/convert_element_type | solution.py:62
  43.2 1.0 %copy.24 = f32[1,2,512,320]{2,1,3,0:T(2,128)S(1)} copy(f32[1,2,512,320]{2,3,1,0:T(8,128)S(1)} %get-tuple-element.19) | data formatting | bytes 2621440 | tf_op jit(solution)/shard_map/convert_element_type | solution.py:62
  44.5 1.0 %copy.27 = f32[1,2,512,320]{2,1,3,0:T(2,128)S(1)} copy(f32[1,2,512,320]{2,3,1,0:T(8,128)S(1)} %get-tuple-element.18) | data formatting | bytes 2621440 | tf_op jit(solution)/shard_map/convert_element_type | solution.py:62
  45.8 1.0 %copy.22 = f32[1,2,512,320]{2,1,3,0:T(2,128)S(1)} copy(f32[1,2,512,320]{2,3,1,0:T(8,128)S(1)} %get-tuple-element.20) | data formatting | bytes 2621440 | tf_op jit(solution)/shard_map/convert_element_type | solution.py:62
  47.1 1.8 %convert_multiply_fusion = (f32[1024,320]{0,1:T(8,128)S(1)}, f32[1024,320]{0,1:T(8,128)S(1)}, f32[1024,320]{0,1:T(8,128)S(1)}, f32[1024,320]{0,1:T(8,128)S(1)}, f32[1024,320]{0,1:T(8,128)S(1)}) fusion(f32[1024,320]{0,1:T(8,128)S(1)} %bitcast.114, f32[1024,320]{0,1:T(8,128)S(1)} %bitcast.115, bf16[1024,320]{0,1:T(8,128)(2,1)S(1)} %convolution_convert_fusion.1, ...), kind=kOutput, calls=%fused_computation.3 | convolution fusion | flops 212336640 | bytes 13352960 | tf_op jit(solution)/shard_map/dot_general | solution.py:40
  48.9 1.4 %bitcast_dynamic-update-slice_fusion.4 = (f32[5,2,512,320]{2,3,1,0:T(8,128)S(1)}, f32[2,512,320]{1,2,0:T(8,128)S(1)}) fusion(s32[320]{0:T(512)S(1)} %add_select_fusion, f32[40,2,8,512]{3,2,1,0:T(8,128)S(1)} %bitcast.113, pred[2]{0:T(512)(128)(4,1)S(1)} %compare_and_fusion.4), kind=kOutput, calls=%fused_computation.50 | convolution fusion | flops 1259048960 | bytes 3936768 | tf_op jit(solution)/shard_map/dot_general | solution.py:63
  50.3 1.3 %bitcast_dynamic-update-slice_fusion.3 = (f32[5,2,512,320]{2,3,1,0:T(8,128)S(1)}, f32[2,512,320]{1,2,0:T(8,128)S(1)}) fusion(f32[5,2,512,320]{2,3,1,0:T(8,128)S(1)} %get-tuple-element.32, s32[320]{0:T(512)S(1)} %add_select_fusion, f32[40,2,8,512]{3,2,1,0:T(8,128)S(1)} %bitcast.112, pred[2]{0:T(512)(128)(4,1)S(1)} %get-tuple-element.45), kind=kOutput, calls=%fused_computation.49 | convolution fusion | flops 1259048960 | bytes 3936768 | tf_op jit(solution)/shard_map/dot_general | solution.py:63
  51.7 1.3 %bitcast_dynamic-update-slice_fusion.2 = (f32[5,2,512,320]{2,3,1,0:T(8,128)S(1)}, f32[2,512,320]{1,2,0:T(8,128)S(1)}) fusion(f32[5,2,512,320]{2,3,1,0:T(8,128)S(1)} %get-tuple-element.34, s32[320]{0:T(512)S(1)} %add_select_fusion, f32[40,2,8,512]{3,2,1,0:T(8,128)S(1)} %bitcast.111, pred[2]{0:T(512)(128)(4,1)S(1)} %get-tuple-element.44), kind=kOutput, calls=%fused_computation.48 | convolution fusion | flops 1259048960 | bytes 3936768 | tf_op jit(solution)/shard_map/dot_general | solution.py:63
  53.0 1.6 %bitcast_dynamic-update-slice_fusion.1 = (f32[5,2,512,320]{2,3,1,0:T(8,128)S(1)}, f32[2,512,320]{1,2,0:T(8,128)S(1)}) fusion(f32[5,2,512,320]{2,3,1,0:T(8,128)S(1)} %get-tuple-element.36, s32[320]{0:T(512)S(1)} %add_select_fusion, f32[40,2,8,512]{3,2,1,0:T(8,128)S(1)} %bitcast.110, pred[2]{0:T(512)(128)(4,1)S(1)} %get-tuple-element.43), kind=kOutput, calls=%fused_computation.47 | convolution fusion | flops 1259048960 | bytes 3936768 | tf_op jit(solution)/shard_map/dot_general | solution.py:63
  54.6 1.3 %bitcast_dynamic-update-slice_fusion = (f32[5,2,512,320]{2,3,1,0:T(8,128)S(1)}, f32[2,512,320]{1,2,0:T(8,128)S(1)}) fusion(f32[5,2,512,320]{2,3,1,0:T(8,128)S(1)} %get-tuple-element.38, s32[320]{0:T(512)S(1)} %add_select_fusion, f32[40,2,8,512]{3,2,1,0:T(8,128)S(1)} %bitcast.109, pred[2]{0:T(512)(128)(4,1)S(1)} %get-tuple-element.42), kind=kOutput, calls=%fused_computation.46 | convolution fusion | flops 1259048960 | bytes 3936768 | tf_op jit(solution)/shard_map/dot_general | solution.py:63
  55.9 0.8 maximum_maximum_fusion
  56.7 1.4 %fusion = f32[2,512,320]{1,2,0:T(8,128)S(1)} fusion(f32[5,2,512,320]{2,3,1,0:T(8,128)S(1)} %get-tuple-element.40, f32[2,512,320]{1,2,0:T(8,128)S(1)} %maximum_maximum_fusion), kind=kLoop, calls=%fused_computation.2 | loop fusion | flops 2949120 | bytes 9175040 | tf_op jit(solution)/shard_map/reduce_sum | solution.py:73
  58.1 1.7 %divide_convert_fusion = bf16[5,2,512,320]{2,3,1,0:T(8,128)(2,1)S(1)} fusion(f32[5,2,512,320]{2,3,1,0:T(8,128)S(1)} %get-tuple-element.40, f32[2,512,320]{1,2,0:T(8,128)S(1)} %fusion, f32[2,512,320]{1,2,0:T(8,128)S(1)} %maximum_maximum_fusion), kind=kLoop, calls=%fused_computation | loop fusion | flops 4915200 | bytes 12451840 | tf_op jit(solution)/shard_map/convert_element_type | solution.py:73
  60.0 1.1 %copy-done.1 = bf16[2,2,512,320]{2,3,1,0:T(8,128)(2,1)S(1)} copy-done((bf16[2,2,512,320]{2,3,1,0:T(8,128)(2,1)S(1)}, bf16[2,2,512,320]{2,3,1,0:T(8,128)(2,1)}, u32[]{:S(2)}) %copy-start.1) | copy-done | bytes 1310744
  61.2 2.1 %multiply_add_fusion = (f32[1,2,512,320]{2,3,1,0:T(8,128)S(1)}, f32[1,2,512,320]{2,3,1,0:T(8,128)S(1)}, f32[1,2,512,320]{2,3,1,0:T(8,128)S(1)}) fusion(bf16[2,2,512,320]{2,3,1,0:T(8,128)(2,1)S(1)} %copy-done.1, bf16[2,2,512,320]{2,3,1,0:T(8,128)(2,1)} %collective-permute-done, bf16[5,2,512,320]{2,3,1,0:T(8,128)(2,1)S(1)} %divide_convert_fusion, ...), kind=kLoop, calls=%fused_computation.54 | loop fusion | flops 4915200 | bytes 11796480 | tf_op jit(solution)/shard_map/add | solution.py:76
  63.3 1.0 %copy.34 = f32[1,2,512,320]{2,1,3,0:T(2,128)S(1)} copy(f32[1,2,512,320]{2,3,1,0:T(8,128)S(1)} %get-tuple-element.16) | data formatting | bytes 2621440 | tf_op jit(solution)/shard_map/mul | solution.py:76
  64.6 1.0 %copy.33 = f32[1,2,512,320]{2,1,3,0:T(2,128)S(1)} copy(f32[1,2,512,320]{2,3,1,0:T(8,128)S(1)} %get-tuple-element.15) | data formatting | bytes 2621440 | tf_op jit(solution)/shard_map/mul | solution.py:76
  65.9 1.0 %copy.31 = f32[1,2,512,320]{2,1,3,0:T(2,128)S(1)} copy(f32[1,2,512,320]{2,3,1,0:T(8,128)S(1)} %get-tuple-element.14) | data formatting | bytes 2621440 | tf_op jit(solution)/shard_map/add | solution.py:76
  67.2 1.0 %copy.32 = f32[1,2,512,320]{2,1,3,0:T(2,128)S(1)} copy(f32[1,2,512,320]{2,3,1,0:T(8,128)S(1)} %slice_convert_fusion) | data formatting | bytes 2621440 | tf_op jit(solution)/shard_map/convert_element_type | solution.py:76
  68.5 0.8 copy-done.2
  69.3 0.4 copy-done.3
  69.7 0.9 %fusion.6 = bf16[1024,320]{0,1:T(8,128)(2,1)S(1)} fusion(f32[1024,320]{0,1:T(8,128)S(1)} %copy-done.3, bf16[320,320]{1,0:T(8,128)(2,1)S(1)} %copy-done, f32[1024,320]{0,1:T(8,128)S(1)} %bitcast.126, f32[1024,320]{0,1:T(8,128)S(1)} %bitcast.127, f32[1024,320]{0,1:T(8,128)S(1)} %bitcast.128, f32[1024,320]{0,1:T(8,128)S(1)} %bitcast.129, ...), kind=kOutput, calls=%fused_computation.23 | convolution fusion | flops 212336640 | bytes 8069120 | tf_op jit(solution)/shard_map/dot_general | solution.py:80
  70.7 0.4 copy.36
  71.0 0.6 reshape.197
  71.7 3.0 %collective-permute-start.3 = (bf16[2,1,5120]{2,1,0:T(2,128)(2,1)S(1)}, bf16[2,1,5120]{2,1,0:T(2,128)(2,1)S(1)}, u32[]{:S(2)}, u32[]{:S(2)}) collective-permute-start(bf16[2,1,5120]{2,1,0:T(2,128)(2,1)S(1)} %get-tuple-element.26), channel_id=1, source_target_pairs={{8,0},{9,1},{10,2},{11,3},{12,4},{13,5},{14,6},{15,7},{24,16},{25,... | collective-permute-start | bytes 61448 | tf_op jit(solution)/shard_map/ppermute | solution.py:19
  74.8 1.3 %collective-permute-start.2 = (bf16[2,1,5120]{2,1,0:T(2,128)(2,1)S(1)}, bf16[2,1,5120]{2,1,0:T(2,128)(2,1)S(1)}, u32[]{:S(2)}, u32[]{:S(2)}) collective-permute-start(bf16[2,1,5120]{2,1,0:T(2,128)(2,1)S(1)} %get-tuple-element.25), channel_id=1, source_target_pairs={{0,8},{1,9},{2,10},{3,11},{4,12},{5,13},{6,14},{7,15},{16,24},{17,... | collective-permute-start | bytes 61448 | tf_op jit(solution)/shard_map/ppermute | solution.py:17
  76.1 4.9 %collective-permute-done.2 = bf16[2,1,5120]{2,1,0:T(2,128)(2,1)S(1)} collective-permute-done((bf16[2,1,5120]{2,1,0:T(2,128)(2,1)S(1)}, bf16[2,1,5120]{2,1,0:T(2,128)(2,1)S(1)}, u32[]{:S(2)}, u32[]{:S(2)}) %collective-permute-start.2) | collective-permute-done | bytes 20512 | tf_op jit(solution)/shard_map/ppermute | solution.py:17
  81.2 2.6 %collective-permute-start.4 = (bf16[2,34,320]{2,1,0:T(8,128)(2,1)S(1)}, bf16[2,34,320]{2,1,0:T(8,128)(2,1)S(1)}, u32[]{:S(2)}, u32[]{:S(2)}) collective-permute-start(bf16[2,34,320]{2,1,0:T(8,128)(2,1)S(1)} %get-tuple-element.23), channel_id=1, source_target_pairs={{0,1},{1,2},{2,3},{3,4},{4,5},{5,6},{6,7},{8,9},{9,10},{10,11},{11... | collective-permute-start | bytes 130568 | tf_op jit(solution)/shard_map/ppermute | solution.py:17
  83.7 2.7 %collective-permute-start.5 = (bf16[2,34,320]{2,1,0:T(8,128)(2,1)S(1)}, bf16[2,34,320]{2,1,0:T(8,128)(2,1)S(1)}, u32[]{:S(2)}, u32[]{:S(2)}) collective-permute-start(bf16[2,34,320]{2,1,0:T(8,128)(2,1)S(1)} %get-tuple-element.24), channel_id=1, source_target_pairs={{1,0},{2,1},{3,2},{4,3},{5,4},{6,5},{7,6},{9,8},{10,9},{11,10},{12... | collective-permute-start | bytes 130568 | tf_op jit(solution)/shard_map/ppermute | solution.py:19
  87.3 2.3 %collective-permute-done.5 = bf16[2,34,320]{2,1,0:T(8,128)(2,1)S(1)} collective-permute-done((bf16[2,34,320]{2,1,0:T(8,128)(2,1)S(1)}, bf16[2,34,320]{2,1,0:T(8,128)(2,1)S(1)}, u32[]{:S(2)}, u32[]{:S(2)}) %collective-permute-start.5) | collective-permute-done | bytes 43552 | tf_op jit(solution)/shard_map/ppermute | solution.py:19
  89.6 0.8 maximum_maximum_fusion.1
  90.4 2.8 %fusion.15 = bf16[2,32,5120]{2,1,0:T(8,128)(2,1)} fusion(bf16[2,32,5120]{2,1,0:T(8,128)(2,1)S(1)} %reshape.197, bf16[2,34,5440]{2,1,0:T(8,128)(2,1)S(1)} %get-tuple-element.22, bf16[2,1,5120]{2,1,0:T(2,128)(2,1)S(1)} %collective-permute-done.3, bf16[2,34,5440]{2,1,0:T(8,128)(2,1)S(1)} %get-tuple-element.21, ...), kind=kLoop, calls=%fused_computation.35 | loop fusion | flops 11141120 | bytes 5468160 | tf_op jit(solution)/shard_map/convert_element_type | solution.py:96
  (47 shorter events, 3.5 us)
Async XLA Ops:
  0.0 68.5 %copy-start = (bf16[320,320]{1,0:T(8,128)(2,1)S(1)}, bf16[320,320]{1,0:T(8,128)(2,1)}, u32[]{:S(2)}) copy-start(bf16[320,320]{1,0:T(8,128)(2,1)} %param.6) | copy-start | bytes 614404
  2.3 1.1 %copy-start.4 = (bf16[320,960]{1,0:T(8,128)(2,1)S(1)}, bf16[320,960]{1,0:T(8,128)(2,1)}, u32[]{:S(2)}) copy-start(bf16[320,960]{1,0:T(8,128)(2,1)} %param.5) | copy-start | bytes 1843204
  13.7 20.2 %collective-permute-start = (bf16[2,2,512,320]{2,3,1,0:T(8,128)(2,1)}, bf16[2,2,512,320]{2,3,1,0:T(8,128)(2,1)}, u32[]{:S(2)}, u32[]{:S(2)}) collective-permute-start(bf16[2,2,512,320]{2,3,1,0:T(8,128)(2,1)} %copy_dynamic-update-slice_fusion), channel_id=1, source_target_pairs={{0,16},{16,32},{32,48},{48,64},{64,80},{80,96},{96,112},{112,128},... | collective-permute-start | bytes 3932168 | tf_op jit(solution)/shard_map/ppermute | solution.py:17
  19.1 20.5 %collective-permute-start.1 = (bf16[2,2,512,320]{2,3,1,0:T(8,128)(2,1)}, bf16[2,2,512,320]{2,3,1,0:T(8,128)(2,1)}, u32[]{:S(2)}, u32[]{:S(2)}) collective-permute-start(bf16[2,2,512,320]{2,3,1,0:T(8,128)(2,1)} %copy_dynamic-update-slice_fusion), channel_id=1, source_target_pairs={{16,0},{32,16},{48,32},{64,48},{80,64},{96,80},{112,96},{128,112},... | collective-permute-start | bytes 3932168 | tf_op jit(solution)/shard_map/ppermute | solution.py:19
  59.8 1.3 %copy-start.1 = (bf16[2,2,512,320]{2,3,1,0:T(8,128)(2,1)S(1)}, bf16[2,2,512,320]{2,3,1,0:T(8,128)(2,1)}, u32[]{:S(2)}) copy-start(bf16[2,2,512,320]{2,3,1,0:T(8,128)(2,1)} %copy_dynamic-update-slice_fusion) | copy-start | bytes 3932164
  68.2 1.1 %copy-start.2 = (bf16[1024,320]{0,1:T(8,128)(2,1)S(1)}, bf16[1024,320]{0,1:T(8,128)(2,1)}, u32[]{:S(2)}) copy-start(bf16[1024,320]{0,1:T(8,128)(2,1)} %convolution_convert_fusion) | copy-start | bytes 1966084
  68.2 1.5 %copy-start.3 = (f32[1024,320]{0,1:T(8,128)S(1)}, f32[1024,320]{0,1:T(8,128)}, u32[]{:S(2)}) copy-start(f32[1024,320]{0,1:T(8,128)} %copy.35) | copy-start | bytes 3932164
  71.0 15.4 %copy-start.5 = (f32[9,320]{1,0:T(8,128)S(1)}, f32[9,320]{1,0:T(8,128)}, u32[]{:S(2)}) copy-start(f32[9,320]{1,0:T(8,128)} %param.7) | copy-start | bytes 34564
  71.7 4.3 %collective-permute-start.3 = (bf16[2,1,5120]{2,1,0:T(2,128)(2,1)S(1)}, bf16[2,1,5120]{2,1,0:T(2,128)(2,1)S(1)}, u32[]{:S(2)}, u32[]{:S(2)}) collective-permute-start(bf16[2,1,5120]{2,1,0:T(2,128)(2,1)S(1)} %get-tuple-element.26), channel_id=1, source_target_pairs={{8,0},{9,1},{10,2},{11,3},{12,4},{13,5},{14,6},{15,7},{24,16},{25,... | collective-permute-start | bytes 61448 | tf_op jit(solution)/shard_map/ppermute | solution.py:19
  74.8 6.3 %collective-permute-start.2 = (bf16[2,1,5120]{2,1,0:T(2,128)(2,1)S(1)}, bf16[2,1,5120]{2,1,0:T(2,128)(2,1)S(1)}, u32[]{:S(2)}, u32[]{:S(2)}) collective-permute-start(bf16[2,1,5120]{2,1,0:T(2,128)(2,1)S(1)} %get-tuple-element.25), channel_id=1, source_target_pairs={{0,8},{1,9},{2,10},{3,11},{4,12},{5,13},{6,14},{7,15},{16,24},{17,... | collective-permute-start | bytes 61448 | tf_op jit(solution)/shard_map/ppermute | solution.py:17
  81.2 6.1 %collective-permute-start.4 = (bf16[2,34,320]{2,1,0:T(8,128)(2,1)S(1)}, bf16[2,34,320]{2,1,0:T(8,128)(2,1)S(1)}, u32[]{:S(2)}, u32[]{:S(2)}) collective-permute-start(bf16[2,34,320]{2,1,0:T(8,128)(2,1)S(1)} %get-tuple-element.23), channel_id=1, source_target_pairs={{0,1},{1,2},{2,3},{3,4},{4,5},{5,6},{6,7},{8,9},{9,10},{10,11},{11... | collective-permute-start | bytes 130568 | tf_op jit(solution)/shard_map/ppermute | solution.py:17
  83.7 5.9 %collective-permute-start.5 = (bf16[2,34,320]{2,1,0:T(8,128)(2,1)S(1)}, bf16[2,34,320]{2,1,0:T(8,128)(2,1)S(1)}, u32[]{:S(2)}, u32[]{:S(2)}) collective-permute-start(bf16[2,34,320]{2,1,0:T(8,128)(2,1)S(1)} %get-tuple-element.24), channel_id=1, source_target_pairs={{1,0},{2,1},{3,2},{4,3},{5,4},{6,5},{7,6},{9,8},{10,9},{11,10},{12... | collective-permute-start | bytes 130568 | tf_op jit(solution)/shard_map/ppermute | solution.py:19
where the time goes:
time: 93.7 us; the launch traced here: 93.2 us
  local copies, waits for them, and re-layouts  26.7 us (28%)
  waiting for transfers between devices  24 us (26%)
  starting transfers between devices  17 us (18%)
  other arithmetic  13.3 us (14%)
  matrix products  11.8 us (13%)
    ppermute x3, waiting for transfers between devices, padded_2(): lax.ppermute(tail, axis, [(i, (i + 1) % count) for i in range(ends)])  16.1 us
    ppermute x3, starting transfers between devices, padded_2(): lax.ppermute(tail, axis, [(i, (i + 1) % count) for i in range(ends)])  9.17 us
    ppermute x3, waiting for transfers between devices, padded_2(): lax.ppermute(head, axis, [((i + 1) % count, i) for i in range(ends)])  7.93 us
    ppermute x3, starting transfers between devices, padded_2(): lax.ppermute(head, axis, [((i + 1) % count, i) for i in range(ends)])  7.84 us
    unnamed x21, local copies, waits for them, and re-layouts  7.24 us
    dot_general x5, matrix products, body(): jnp.dot(prod.reshape(frames * points, chans), head_sum, precision=lax.Pre...  6.96 us
    another operation x3, local copies, waits for them, and re-layouts, body(): jnp.stack([keys_own.reshape(frames, points, chans), vals_own.reshape(fram...  6.27 us
    convert_element_type x4, local copies, waits for them, and re-layouts, body(): prod = q_wide * wide[0, shift_d:shift_d + frames].astype(jnp.float32)  4.05 us
  transfers between devices with their start and end apart: 6, of which 4 were waited for; matrix products, arithmetic and copies ran while one was open for 3% of the time, Pallas kernels for 0%

commit v1 on v0

v1 whole, which is shorter than its diff:
```python
import functools

import jax
import jax.numpy as jnp
from jax import lax
from jax.experimental import pallas as pl
from jax.experimental.pallas import tpu as pltpu
from jax.sharding import PartitionSpec as P

HEAD_DIM = 64
BLOCK = 128


def layer_norm(flat):
    mean = jnp.mean(flat, axis=-1, keepdims=True)
    cent = flat - mean
    var = jnp.mean(cent * cent, axis=-1, keepdims=True)
    return (cent * lax.rsqrt(var + 1e-05)).astype(jnp.bfloat16)


def attend_kernel(valid_ref, prev_ref, own_ref, next_ref, wqkv_ref, wout_ref, hsum_ref, out_ref):
    chans = wout_ref.shape[0]
    block = own_ref.shape[1]
    frames = [prev_ref[0], prev_ref[1], own_ref[0], own_ref[1], next_ref[0], next_ref[1]]
    normed = [layer_norm(f.astype(jnp.float32)) for f in frames]
    own_n = jnp.concatenate([normed[2], normed[3]], axis=0)
    qkv = jnp.dot(own_n, wqkv_ref[...], preferred_element_type=jnp.float32).astype(jnp.bfloat16)
    nb_n = jnp.concatenate([normed[0], normed[1], normed[4], normed[5]], axis=0)
    kv_nb = jnp.dot(
        nb_n, wqkv_ref[:, chans:], preferred_element_type=jnp.float32
    ).astype(jnp.bfloat16)
    keys = [None] * 6
    vals = [None] * 6
    for w, slot in ((0, 0), (1, 1), (4, 2), (5, 3)):
        keys[w] = kv_nb[slot * block : (slot + 1) * block, :chans]
        vals[w] = kv_nb[slot * block : (slot + 1) * block, chans:]
    for t in range(2):
        keys[2 + t] = qkv[t * block : (t + 1) * block, chans : 2 * chans]
        vals[2 + t] = qkv[t * block : (t + 1) * block, 2 * chans :]
    hsum = hsum_ref[...]
    outs = []
    for t in range(2):
        q = qkv[t * block : (t + 1) * block, :chans].astype(jnp.float32)
        scores = []
        for d in range(5):
            w = t + d
            prod = q * keys[w].astype(jnp.float32)
            hi = prod.astype(jnp.bfloat16)
            lo = (prod - hi.astype(jnp.float32)).astype(jnp.bfloat16)
            score = jnp.dot(hi, hsum, preferred_element_type=jnp.float32) + jnp.dot(
                lo, hsum, preferred_element_type=jnp.float32
            )
            score = score * (HEAD_DIM ** (-0.5))
            score = jnp.where(valid_ref[w] > 0, score, jnp.float32(-1e30))
            scores.append(score)
        top = scores[0]
        for s in scores[1:]:
            top = jnp.maximum(top, s)
        expo = [jnp.exp(s - top) for s in scores]
        denom = expo[0]
        for e in expo[1:]:
            denom = denom + e
        mixed = None
        for d in range(5):
            weight = (expo[d] / denom).astype(jnp.bfloat16).astype(jnp.float32)
            term = weight * vals[t + d].astype(jnp.float32)
            mixed = term if mixed is None else mixed + term
        outs.append(mixed.astype(jnp.bfloat16))
    attended = jnp.concatenate(outs, axis=0)
    proj = jnp.dot(attended, wout_ref[...], preferred_element_type=jnp.float32)
    xown = jnp.concatenate([own_ref[0], own_ref[1]], axis=0).astype(jnp.float32)
    hidden = (xown + proj).astype(jnp.bfloat16)
    out_ref[0] = hidden[:block]
    out_ref[1] = hidden[block:]


def attend(valid, prev, own, nxt, w_qkv, w_out, hsum):
    frames, points, chans = own.shape
    grid = (points // BLOCK,)
    cell_spec = pl.BlockSpec((frames, BLOCK, chans), lambda i: (0, i, 0))
    full = lambda shape: pl.BlockSpec(shape, lambda i: (0, 0))
    return pl.pallas_call(
        attend_kernel,
        grid=grid,
        in_specs=[
            pl.BlockSpec(memory_space=pltpu.SMEM),
            cell_spec,
            cell_spec,
            cell_spec,
            full(w_qkv.shape),
            full(w_out.shape),
            full(hsum.shape),
        ],
        out_specs=cell_spec,
        out_shape=jax.ShapeDtypeStruct(own.shape, jnp.bfloat16),
    )(valid, prev, own, nxt, w_qkv, w_out, hsum)


def shift(x, axis, step):
    count = lax.axis_size(axis)
    if step > 0:
        pairs = [(i, i + 1) for i in range(count - 1)]
    else:
        pairs = [(i + 1, i) for i in range(count - 1)]
    return lax.ppermute(x, axis, pairs)


def shift2(x, rstep, cstep):
    rows = lax.axis_size("row")
    cols = lax.axis_size("col")
    pairs = []
    for r in range(rows):
        for c in range(cols):
            rr, cc = r + rstep, c + cstep
            if 0 <= rr < rows and 0 <= cc < cols:
                pairs.append((r * cols + c, rr * cols + cc))
    return lax.ppermute(x, ("row", "col"), pairs)


def body(latents, w_qkv, w_out, conv_weight):
    frames, rows, merged = latents.shape
    chans = w_out.shape[0]
    cols = merged // chans
    points = rows * cols
    x_prev = shift(latents, "tm", 1)
    x_next = shift(latents, "tm", -1)
    first = lax.axis_index("tm") * frames
    total = lax.axis_size("tm") * frames
    where_t = first + jnp.arange(6, dtype=jnp.int32) - 2
    valid = ((where_t >= 0) & (where_t < total)).astype(jnp.int32)
    group = jnp.arange(chans, dtype=jnp.int32) // HEAD_DIM
    hsum = (group[:, None] == group[None, :]).astype(jnp.bfloat16)
    cells = lambda a: a.reshape(frames, points, chans)
    hidden = attend(valid, cells(x_prev), cells(latents), cells(x_next), w_qkv, w_out, hsum)
    hid = hidden.reshape(frames, rows, merged)

    top_row = hid[:, :1, :]
    bot_row = hid[:, rows - 1 :, :]
    left_col = hid[:, :, :chans]
    right_col = hid[:, :, merged - chans :]
    halo_top = shift(bot_row, "row", 1)
    halo_bot = shift(top_row, "row", -1)
    halo_left = shift(right_col, "col", 1)
    halo_right = shift(left_col, "col", -1)
    c_tl = shift2(hid[:, rows - 1 :, merged - chans :], 1, 1)
    c_tr = shift2(hid[:, rows - 1 :, :chans], 1, -1)
    c_bl = shift2(hid[:, :1, merged - chans :], -1, 1)
    c_br = shift2(hid[:, :1, :chans], -1, -1)
    padded = jnp.concatenate(
        [
            jnp.concatenate([c_tl, halo_top, c_tr], axis=2),
            jnp.concatenate([halo_left, hid, halo_right], axis=2),
            jnp.concatenate([c_bl, halo_bot, c_br], axis=2),
        ],
        axis=1,
    )
    taps = jnp.tile(conv_weight, (1, cols))
    acc = hid.astype(jnp.float32)
    for tap_a in range(3):
        for tap_b in range(3):
            acc = (
                acc
                + padded[:, tap_a : tap_a + rows, tap_b * chans : tap_b * chans + merged].astype(
                    jnp.float32
                )
                * taps[3 * tap_a + tap_b]
            )
    return acc.astype(jnp.bfloat16)


def solution(mesh):
    placed = (P("tm", "row", "col"), P(), P(), P())
    return jax.shard_map(
        body, mesh=mesh, in_specs=placed, out_specs=P("tm", "row", "col"), check_vma=False
    )
```

time: 93.7 us -> 66.4 us (0.71)
  the two profiles are of different devices: /device:TPU:111 before, /device:TPU:105 now
where the time goes in v1:
time: 66.4 us; the launch traced here: 66 us
  starting transfers between devices  24.5 us (37%)
  Pallas kernels  15.3 us (23%)
  waiting for transfers between devices  10.5 us (16%)
  local copies, waits for them, and re-layouts  9.54 us (14%)
  other arithmetic  5.95 us (9%)
    ppermute x6, starting transfers between devices, shift(): return lax.ppermute(x, axis, pairs)  16.3 us
    pallas_call x1, Pallas kernels, attend(): pl.pallas_call(attend_kernel, grid=grid, in_specs=[pl.BlockSpec(memory_sp...  15.3 us
    ppermute x4, starting transfers between devices, shift2(): return lax.ppermute(x, ('row', 'col'), pairs)  8.25 us
    ppermute x6, waiting for transfers between devices, shift(): return lax.ppermute(x, axis, pairs)  6.15 us
    reshape x3, local copies, waits for them, and re-layouts, body(): cells = lambda a: a.reshape(frames, points, chans)  5.48 us
    convert_element_type x1, other arithmetic, body(): return acc.astype(jnp.bfloat16)  4.66 us
    ppermute x4, waiting for transfers between devices, shift2(): return lax.ppermute(x, ('row', 'col'), pairs)  4.36 us
    reshape x1, local copies, waits for them, and re-layouts, body(): hid = hidden.reshape(frames, rows, merged)  1.78 us
  transfers between devices with their start and end apart: 10, of which 4 were waited for; matrix products, arithmetic and copies ran while one was open for 10% of the time, Pallas kernels for 0%

profile of v1, /device:TPU:105, one launch (start us, length us, event | category | flops | bytes accessed | tf_op | source)
XLA Modules:
  0.0 66.0 jit_solution(5103111512437723593)
XLA Ops:
  0.0 5.3 %collective-permute-start = (bf16[2,32,5120]{2,1,0:T(8,128)(2,1)}, bf16[2,32,5120]{2,1,0:T(8,128)(2,1)S(1)}, u32[]{:S(2)}, u32[]{:S(2)}) collective-permute-start(bf16[2,32,5120]{2,1,0:T(8,128)(2,1)} %param.4), channel_id=1, source_target_pairs={{0,16},{16,32},{32,48},{48,64},{64,80},{80,96},{96,112},{112,128},... | collective-permute-start | bytes 1966088 | tf_op jit(solution)/shard_map/ppermute | solution.py:105
  5.3 1.9 %collective-permute-start.1 = (bf16[2,32,5120]{2,1,0:T(8,128)(2,1)}, bf16[2,32,5120]{2,1,0:T(8,128)(2,1)S(1)}, u32[]{:S(2)}, u32[]{:S(2)}) collective-permute-start(bf16[2,32,5120]{2,1,0:T(8,128)(2,1)} %param.4), channel_id=1, source_target_pairs={{16,0},{32,16},{48,32},{64,48},{80,64},{96,80},{112,96},{128,112},... | collective-permute-start | bytes 1966088 | tf_op jit(solution)/shard_map/ppermute | solution.py:105
  7.2 2.4 %reshape.87.own_ref = bf16[2,512,320]{2,1,0:T(8,128)(2,1)} reshape(bf16[2,32,5120]{2,1,0:T(8,128)(2,1)} %param.4) | data formatting | bytes 1310720 | tf_op jit(solution)/shard_map/reshape | solution.py:133
  9.7 0.5 and_convert_fusion.valid_ref
  10.2 0.8 %compare_convert_fusion.hsum_ref = bf16[320,320]{1,0:T(8,128)(2,1)} fusion(s32[320]{0:T(512)S(1)} %add_select_fusion), kind=kLoop, calls=%fused_computation.27 | loop fusion | flops 204800 | bytes 206080 | tf_op jit(solution)/shard_map/convert_element_type | solution.py:132
  11.0 2.2 %collective-permute-done = bf16[2,32,5120]{2,1,0:T(8,128)(2,1)S(1)} collective-permute-done((bf16[2,32,5120]{2,1,0:T(8,128)(2,1)}, bf16[2,32,5120]{2,1,0:T(8,128)(2,1)S(1)}, u32[]{:S(2)}, u32[]{:S(2)}) %collective-permute-start) | collective-permute-done | bytes 655392 | tf_op jit(solution)/shard_map/ppermute | solution.py:105
  13.1 1.5 %reshape.86.prev_ref = bf16[2,512,320]{2,1,0:T(8,128)(2,1)} reshape(bf16[2,32,5120]{2,1,0:T(8,128)(2,1)S(1)} %collective-permute-done) | data formatting | bytes 1310720 | tf_op jit(solution)/shard_map/reshape | solution.py:133
  14.6 4.0 %collective-permute-done.1 = bf16[2,32,5120]{2,1,0:T(8,128)(2,1)S(1)} collective-permute-done((bf16[2,32,5120]{2,1,0:T(8,128)(2,1)}, bf16[2,32,5120]{2,1,0:T(8,128)(2,1)S(1)}, u32[]{:S(2)}, u32[]{:S(2)}) %collective-permute-start.1) | collective-permute-done | bytes 655392 | tf_op jit(solution)/shard_map/ppermute | solution.py:105
  18.6 1.5 %reshape.88.next_ref = bf16[2,512,320]{2,1,0:T(8,128)(2,1)} reshape(bf16[2,32,5120]{2,1,0:T(8,128)(2,1)S(1)} %collective-permute-done.1) | data formatting | bytes 1310720 | tf_op jit(solution)/shard_map/reshape | solution.py:133
  20.2 15.3 %shard_map.46 = bf16[2,512,320]{2,1,0:T(8,128)(2,1)} custom-call(s32[6]{0:T(128)} %and_convert_fusion.valid_ref, bf16[2,512,320]{2,1,0:T(8,128)(2,1)} %reshape.86.prev_ref, bf16[2,512,320]{2,1,0:T(8,128)(2,1)} %reshape.87.own_ref, bf16[2,512,320]{2,1,0:T(8,128)(2,1)} %reshape.88.next_ref, bf16[320,960]{1,0:T(8,128)(2,1)} %wqkv_ref.1, ...), custom_call_target="tpu_custom_call" | custom-call | tf_op jit(solution)/shard_map/pallas_call | solution.py:82
  35.5 0.0 copy-start
  35.5 1.8 %reshape.89 = bf16[2,32,5120]{2,1,0:T(8,128)(2,1)S(1)} reshape(bf16[2,512,320]{2,1,0:T(8,128)(2,1)} %shard_map.46) | data formatting | bytes 1310720 | tf_op jit(solution)/shard_map/reshape | solution.py:135
  37.3 0.1 fusion.16
  37.4 0.1 fusion.17
  37.4 4.4 %collective-permute-start.2 = (bf16[2,1,320]{2,1,0:T(2,128)(2,1)S(1)}, bf16[2,1,320]{2,1,0:T(2,128)(2,1)S(1)}, u32[]{:S(2)}, u32[]{:S(2)}) collective-permute-start(bf16[2,1,320]{2,1,0:T(2,128)(2,1)S(1)} %get-tuple-element.17), channel_id=1, source_target_pairs={{0,9},{1,10},{2,11},{3,12},{4,13},{5,14},{6,15},{16,25},{17,26},{1... | collective-permute-start | bytes 3848 | tf_op jit(solution)/shard_map/ppermute | solution.py:117
  41.8 0.1 fusion.18
  41.9 1.3 %collective-permute-start.4 = (bf16[2,1,320]{2,1,0:T(2,128)(2,1)S(1)}, bf16[2,1,320]{2,1,0:T(2,128)(2,1)S(1)}, u32[]{:S(2)}, u32[]{:S(2)}) collective-permute-start(bf16[2,1,320]{2,1,0:T(2,128)(2,1)S(1)} %get-tuple-element.14), channel_id=1, source_target_pairs={{1,8},{2,9},{3,10},{4,11},{5,12},{6,13},{7,14},{17,24},{18,25},{19... | collective-permute-start | bytes 3848 | tf_op jit(solution)/shard_map/ppermute | solution.py:117
  43.2 1.6 %collective-permute-start.3 = (bf16[2,1,5120]{2,1,0:T(2,128)(2,1)S(1)}, bf16[2,1,5120]{2,1,0:T(2,128)(2,1)S(1)}, u32[]{:S(2)}, u32[]{:S(2)}) collective-permute-start(bf16[2,1,5120]{2,1,0:T(2,128)(2,1)S(1)} %get-tuple-element.18), channel_id=1, source_target_pairs={{0,8},{1,9},{2,10},{3,11},{4,12},{5,13},{6,14},{7,15},{16,24},{17,... | collective-permute-start | bytes 61448 | tf_op jit(solution)/shard_map/ppermute | solution.py:105
  44.8 1.3 %collective-permute-start.8 = (bf16[2,1,5120]{2,1,0:T(2,128)(2,1)S(1)}, bf16[2,1,5120]{2,1,0:T(2,128)(2,1)S(1)}, u32[]{:S(2)}, u32[]{:S(2)}) collective-permute-start(bf16[2,1,5120]{2,1,0:T(2,128)(2,1)S(1)} %get-tuple-element.19), channel_id=1, source_target_pairs={{8,0},{9,1},{10,2},{11,3},{12,4},{13,5},{14,6},{15,7},{24,16},{25,... | collective-permute-start | bytes 61448 | tf_op jit(solution)/shard_map/ppermute | solution.py:105
  46.1 2.6 %collective-permute-start.5 = (bf16[2,32,320]{2,1,0:T(8,128)(2,1)S(1)}, bf16[2,32,320]{2,1,0:T(8,128)(2,1)S(1)}, u32[]{:S(2)}, u32[]{:S(2)}) collective-permute-start(bf16[2,32,320]{2,1,0:T(8,128)(2,1)S(1)} %get-tuple-element.21), channel_id=1, source_target_pairs={{0,1},{1,2},{2,3},{3,4},{4,5},{5,6},{6,7},{8,9},{9,10},{10,11},{11... | collective-permute-start | bytes 122888 | tf_op jit(solution)/shard_map/ppermute | solution.py:105
  48.7 0.0 collective-permute-done.2
  48.7 3.6 %collective-permute-start.6 = (bf16[2,32,320]{2,1,0:T(8,128)(2,1)S(1)}, bf16[2,32,320]{2,1,0:T(8,128)(2,1)S(1)}, u32[]{:S(2)}, u32[]{:S(2)}) collective-permute-start(bf16[2,32,320]{2,1,0:T(8,128)(2,1)S(1)} %get-tuple-element.20), channel_id=1, source_target_pairs={{1,0},{2,1},{3,2},{4,3},{5,4},{6,5},{7,6},{9,8},{10,9},{11,10},{12... | collective-permute-start | bytes 122888 | tf_op jit(solution)/shard_map/ppermute | solution.py:105
  52.3 0.0 copy-done
  52.3 0.1 slice_reduce_fusion.8
  52.4 0.1 tile.42
  52.4 0.0 collective-permute-done.4
  52.4 1.3 %collective-permute-start.7 = (bf16[2,1,320]{2,1,0:T(2,128)(2,1)S(1)}, bf16[2,1,320]{2,1,0:T(2,128)(2,1)S(1)}, u32[]{:S(2)}, u32[]{:S(2)}) collective-permute-start(bf16[2,1,320]{2,1,0:T(2,128)(2,1)S(1)} %get-tuple-element.15), channel_id=1, source_target_pairs={{8,1},{9,2},{10,3},{11,4},{12,5},{13,6},{14,7},{24,17},{25,18},{26... | collective-permute-start | bytes 3848 | tf_op jit(solution)/shard_map/ppermute | solution.py:117
  53.7 0.0 collective-permute-done.3
  53.7 1.3 %collective-permute-start.9 = (bf16[2,1,320]{2,1,0:T(2,128)(2,1)S(1)}, bf16[2,1,320]{2,1,0:T(2,128)(2,1)S(1)}, u32[]{:S(2)}, u32[]{:S(2)}) collective-permute-start(bf16[2,1,320]{2,1,0:T(2,128)(2,1)S(1)} %get-tuple-element.16), channel_id=1, source_target_pairs={{9,0},{10,1},{11,2},{12,3},{13,4},{14,5},{15,6},{25,16},{26,17},{2... | collective-permute-start | bytes 3848 | tf_op jit(solution)/shard_map/ppermute | solution.py:117
  55.1 0.1 tile.44
  55.1 0.1 tile.46
  55.2 0.1 tile.48
  55.3 0.1 tile.50
  55.4 0.1 tile.52
  55.5 0.1 tile.54
  55.6 0.1 tile.56
  55.6 0.1 tile.58
  55.7 0.2 concatenate.26
  56.0 2.9 %collective-permute-done.7 = bf16[2,1,320]{2,1,0:T(2,128)(2,1)S(1)} collective-permute-done((bf16[2,1,320]{2,1,0:T(2,128)(2,1)S(1)}, bf16[2,1,320]{2,1,0:T(2,128)(2,1)S(1)}, u32[]{:S(2)}, u32[]{:S(2)}) %collective-permute-start.7) | collective-permute-done | bytes 1312 | tf_op jit(solution)/shard_map/ppermute | solution.py:117
  58.9 1.4 %collective-permute-done.9 = bf16[2,1,320]{2,1,0:T(2,128)(2,1)S(1)} collective-permute-done((bf16[2,1,320]{2,1,0:T(2,128)(2,1)S(1)}, bf16[2,1,320]{2,1,0:T(2,128)(2,1)S(1)}, u32[]{:S(2)}, u32[]{:S(2)}) %collective-permute-start.9) | collective-permute-done | bytes 1312 | tf_op jit(solution)/shard_map/ppermute | solution.py:117
  60.3 0.0 collective-permute-done.8
  60.3 0.2 concatenate.31
  60.5 0.0 collective-permute-done.5
  60.6 0.0 collective-permute-done.6
  60.6 0.8 %concatenate.27 = bf16[2,32,5760]{2,1,0:T(8,128)(2,1)S(1)} concatenate(bf16[2,32,320]{2,1,0:T(8,128)(2,1)S(1)} %collective-permute-done.5, bf16[2,32,5120]{2,1,0:T(8,128)(2,1)S(1)} %reshape.89, bf16[2,32,320]{2,1,0:T(8,128)(2,1)S(1)} %collective-permute-done.6), dimensions={2} | concatenate | bytes 1474560 | tf_op jit(solution)/shard_map/concatenate | solution.py:152
  61.4 4.7 %fusion.8 = bf16[2,32,5120]{2,1,0:T(8,128)(2,1)} fusion(bf16[2,32,5120]{2,1,0:T(8,128)(2,1)S(1)} %reshape.89, bf16[2,32,5760]{2,1,0:T(8,128)(2,1)S(1)} %concatenate.27, bf16[2,1,5760]{2,1,0:T(2,128)(2,1)S(1)} %concatenate.31, bf16[2,1,5760]{2,1,0:T(2,128)(2,1)S(1)} %concatenate.26, bf16[2,32,320]{2,1,0:T(8,128)(2,1)S(1)} %collective-permute-done.6, ...), kind=kLoop, calls=%fused_computation.10 | loop fusion | flops 17039360 | bytes 2360320 | tf_op jit(solution)/shard_map/convert_element_type | solution.py:168
  (10 shorter events, 0.0 us)
Async XLA Ops:
  0.0 13.1 %collective-permute-start = (bf16[2,32,5120]{2,1,0:T(8,128)(2,1)}, bf16[2,32,5120]{2,1,0:T(8,128)(2,1)S(1)}, u32[]{:S(2)}, u32[]{:S(2)}) collective-permute-start(bf16[2,32,5120]{2,1,0:T(8,128)(2,1)} %param.4), channel_id=1, source_target_pairs={{0,16},{16,32},{32,48},{48,64},{64,80},{80,96},{96,112},{112,128},... | collective-permute-start | bytes 1966088 | tf_op jit(solution)/shard_map/ppermute | solution.py:105
  5.3 13.3 %collective-permute-start.1 = (bf16[2,32,5120]{2,1,0:T(8,128)(2,1)}, bf16[2,32,5120]{2,1,0:T(8,128)(2,1)S(1)}, u32[]{:S(2)}, u32[]{:S(2)}) collective-permute-start(bf16[2,32,5120]{2,1,0:T(8,128)(2,1)} %param.4), channel_id=1, source_target_pairs={{16,0},{32,16},{48,32},{64,48},{80,64},{96,80},{112,96},{128,112},... | collective-permute-start | bytes 1966088 | tf_op jit(solution)/shard_map/ppermute | solution.py:105
  35.5 16.8 %copy-start = (f32[9,320]{1,0:T(8,128)S(1)}, f32[9,320]{1,0:T(8,128)}, u32[]{:S(2)}) copy-start(f32[9,320]{1,0:T(8,128)} %param.7) | copy-start | bytes 34564
  37.4 11.3 %collective-permute-start.2 = (bf16[2,1,320]{2,1,0:T(2,128)(2,1)S(1)}, bf16[2,1,320]{2,1,0:T(2,128)(2,1)S(1)}, u32[]{:S(2)}, u32[]{:S(2)}) collective-permute-start(bf16[2,1,320]{2,1,0:T(2,128)(2,1)S(1)} %get-tuple-element.17), channel_id=1, source_target_pairs={{0,9},{1,10},{2,11},{3,12},{4,13},{5,14},{6,15},{16,25},{17,26},{1... | collective-permute-start | bytes 3848 | tf_op jit(solution)/shard_map/ppermute | solution.py:117
  41.9 10.5 %collective-permute-start.4 = (bf16[2,1,320]{2,1,0:T(2,128)(2,1)S(1)}, bf16[2,1,320]{2,1,0:T(2,128)(2,1)S(1)}, u32[]{:S(2)}, u32[]{:S(2)}) collective-permute-start(bf16[2,1,320]{2,1,0:T(2,128)(2,1)S(1)} %get-tuple-element.14), channel_id=1, source_target_pairs={{1,8},{2,9},{3,10},{4,11},{5,12},{6,13},{7,14},{17,24},{18,25},{19... | collective-permute-start | bytes 3848 | tf_op jit(solution)/shard_map/ppermute | solution.py:117
  43.2 10.5 %collective-permute-start.3 = (bf16[2,1,5120]{2,1,0:T(2,128)(2,1)S(1)}, bf16[2,1,5120]{2,1,0:T(2,128)(2,1)S(1)}, u32[]{:S(2)}, u32[]{:S(2)}) collective-permute-start(bf16[2,1,5120]{2,1,0:T(2,128)(2,1)S(1)} %get-tuple-element.18), channel_id=1, source_target_pairs={{0,8},{1,9},{2,10},{3,11},{4,12},{5,13},{6,14},{7,15},{16,24},{17,... | collective-permute-start | bytes 61448 | tf_op jit(solution)/shard_map/ppermute | solution.py:105
  44.8 15.5 %collective-permute-start.8 = (bf16[2,1,5120]{2,1,0:T(2,128)(2,1)S(1)}, bf16[2,1,5120]{2,1,0:T(2,128)(2,1)S(1)}, u32[]{:S(2)}, u32[]{:S(2)}) collective-permute-start(bf16[2,1,5120]{2,1,0:T(2,128)(2,1)S(1)} %get-tuple-element.19), channel_id=1, source_target_pairs={{8,0},{9,1},{10,2},{11,3},{12,4},{13,5},{14,6},{15,7},{24,16},{25,... | collective-permute-start | bytes 61448 | tf_op jit(solution)/shard_map/ppermute | solution.py:105
  46.1 14.5 %collective-permute-start.5 = (bf16[2,32,320]{2,1,0:T(8,128)(2,1)S(1)}, bf16[2,32,320]{2,1,0:T(8,128)(2,1)S(1)}, u32[]{:S(2)}, u32[]{:S(2)}) collective-permute-start(bf16[2,32,320]{2,1,0:T(8,128)(2,1)S(1)} %get-tuple-element.21), channel_id=1, source_target_pairs={{0,1},{1,2},{2,3},{3,4},{4,5},{5,6},{6,7},{8,9},{9,10},{10,11},{11... | collective-permute-start | bytes 122888 | tf_op jit(solution)/shard_map/ppermute | solution.py:105
  48.7 11.9 %collective-permute-start.6 = (bf16[2,32,320]{2,1,0:T(8,128)(2,1)S(1)}, bf16[2,32,320]{2,1,0:T(8,128)(2,1)S(1)}, u32[]{:S(2)}, u32[]{:S(2)}) collective-permute-start(bf16[2,32,320]{2,1,0:T(8,128)(2,1)S(1)} %get-tuple-element.20), channel_id=1, source_target_pairs={{1,0},{2,1},{3,2},{4,3},{5,4},{6,5},{7,6},{9,8},{10,9},{11,10},{12... | collective-permute-start | bytes 122888 | tf_op jit(solution)/shard_map/ppermute | solution.py:105
  52.4 6.4 %collective-permute-start.7 = (bf16[2,1,320]{2,1,0:T(2,128)(2,1)S(1)}, bf16[2,1,320]{2,1,0:T(2,128)(2,1)S(1)}, u32[]{:S(2)}, u32[]{:S(2)}) collective-permute-start(bf16[2,1,320]{2,1,0:T(2,128)(2,1)S(1)} %get-tuple-element.15), channel_id=1, source_target_pairs={{8,1},{9,2},{10,3},{11,4},{12,5},{13,6},{14,7},{24,17},{25,18},{26... | collective-permute-start | bytes 3848 | tf_op jit(solution)/shard_map/ppermute | solution.py:117
  53.7 6.6 %collective-permute-start.9 = (bf16[2,1,320]{2,1,0:T(2,128)(2,1)S(1)}, bf16[2,1,320]{2,1,0:T(2,128)(2,1)S(1)}, u32[]{:S(2)}, u32[]{:S(2)}) collective-permute-start(bf16[2,1,320]{2,1,0:T(2,128)(2,1)S(1)} %get-tuple-element.16), channel_id=1, source_target_pairs={{9,0},{10,1},{11,2},{12,3},{13,4},{14,5},{15,6},{25,16},{26,17},{2... | collective-permute-start | bytes 3848 | tf_op jit(solution)/shard_map/ppermute | solution.py:117

commit v2 on v1

v2 whole, which is shorter than its diff:
```python
import functools

import jax
import jax.numpy as jnp
from jax import lax
from jax.experimental import pallas as pl
from jax.experimental.pallas import tpu as pltpu
from jax.sharding import PartitionSpec as P

HEAD_DIM = 64
BLOCK = 128


def layer_norm(flat):
    mean = jnp.mean(flat, axis=-1, keepdims=True)
    cent = flat - mean
    var = jnp.mean(cent * cent, axis=-1, keepdims=True)
    return (cent * lax.rsqrt(var + 1e-05)).astype(jnp.bfloat16)


def attend_kernel(valid_ref, prev_ref, own_ref, next_ref, wqkv_ref, wout_ref, out_ref):
    chans = wout_ref.shape[0]
    heads = chans // HEAD_DIM
    block = own_ref.shape[1]
    frames = [prev_ref[0], prev_ref[1], own_ref[0], own_ref[1], next_ref[0], next_ref[1]]
    normed = [layer_norm(f.astype(jnp.float32)) for f in frames]
    nt = (((1,), (1,)), ((), ()))
    own_n = jnp.concatenate([normed[2], normed[3]], axis=0)
    qkv = lax.dot_general(
        wqkv_ref[...], own_n, nt, preferred_element_type=jnp.float32
    ).astype(jnp.bfloat16)
    nb_n = jnp.concatenate([normed[0], normed[1], normed[4], normed[5]], axis=0)
    kv_nb = lax.dot_general(
        wqkv_ref[chans:, :], nb_n, nt, preferred_element_type=jnp.float32
    ).astype(jnp.bfloat16)
    keys = [None] * 6
    vals = [None] * 6
    for w, slot in ((0, 0), (1, 1), (4, 2), (5, 3)):
        keys[w] = kv_nb[:chans, slot * block : (slot + 1) * block]
        vals[w] = kv_nb[chans:, slot * block : (slot + 1) * block]
    for t in range(2):
        keys[2 + t] = qkv[chans : 2 * chans, t * block : (t + 1) * block]
        vals[2 + t] = qkv[2 * chans :, t * block : (t + 1) * block]
    outs = []
    for t in range(2):
        q = qkv[:chans, t * block : (t + 1) * block].astype(jnp.float32)
        scores = []
        for d in range(5):
            w = t + d
            prod = q * keys[w].astype(jnp.float32)
            score = jnp.sum(prod.reshape(heads, HEAD_DIM, block), axis=1)
            score = score * (HEAD_DIM ** (-0.5))
            score = jnp.where(valid_ref[w] > 0, score, jnp.float32(-1e30))
            scores.append(score)
        top = scores[0]
        for s in scores[1:]:
            top = jnp.maximum(top, s)
        expo = [jnp.exp(s - top) for s in scores]
        denom = expo[0]
        for e in expo[1:]:
            denom = denom + e
        mixed = None
        for d in range(5):
            weight = (expo[d] / denom).astype(jnp.bfloat16).astype(jnp.float32)
            wide = jnp.broadcast_to(weight[:, None, :], (heads, HEAD_DIM, block)).reshape(chans, block)
            term = wide * vals[t + d].astype(jnp.float32)
            mixed = term if mixed is None else mixed + term
        outs.append(mixed.astype(jnp.bfloat16))
    attended = jnp.concatenate(outs, axis=1)
    tn = (((0,), (0,)), ((), ()))
    proj = lax.dot_general(attended, wout_ref[...], tn, preferred_element_type=jnp.float32)
    xown = jnp.concatenate([own_ref[0], own_ref[1]], axis=0).astype(jnp.float32)
    hidden = (xown + proj).astype(jnp.bfloat16)
    out_ref[0] = hidden[:block]
    out_ref[1] = hidden[block:]


def attend(valid, prev, own, nxt, w_qkv, w_out):
    frames, points, chans = own.shape
    w_qkv = w_qkv.T
    grid = (points // BLOCK,)
    cell_spec = pl.BlockSpec((frames, BLOCK, chans), lambda i: (0, i, 0))
    full = lambda shape: pl.BlockSpec(shape, lambda i: (0, 0))
    return pl.pallas_call(
        attend_kernel,
        grid=grid,
        in_specs=[
            pl.BlockSpec(memory_space=pltpu.SMEM),
            cell_spec,
            cell_spec,
            cell_spec,
            full(w_qkv.shape),
            full(w_out.shape),
        ],
        out_specs=cell_spec,
        out_shape=jax.ShapeDtypeStruct(own.shape, jnp.bfloat16),
    )(valid, prev, own, nxt, w_qkv, w_out)


def shift(x, axis, step):
    count = lax.axis_size(axis)
    if step > 0:
        pairs = [(i, i + 1) for i in range(count - 1)]
    else:
        pairs = [(i + 1, i) for i in range(count - 1)]
    return lax.ppermute(x, axis, pairs)


def body(latents, w_qkv, w_out, conv_weight):
    frames, rows, merged = latents.shape
    chans = w_out.shape[0]
    cols = merged // chans
    points = rows * cols
    x_prev = shift(latents, "tm", 1)
    x_next = shift(latents, "tm", -1)
    first = lax.axis_index("tm") * frames
    total = lax.axis_size("tm") * frames
    where_t = first + jnp.arange(6, dtype=jnp.int32) - 2
    valid = ((where_t >= 0) & (where_t < total)).astype(jnp.int32)
    cells = lambda a: a.reshape(frames, points, chans)
    hidden = attend(valid, cells(x_prev), cells(latents), cells(x_next), w_qkv, w_out)
    hid = hidden.reshape(frames, rows, merged)

    halo_top = shift(hid[:, rows - 1 :, :], "row", 1)
    halo_bot = shift(hid[:, :1, :], "row", -1)
    tall = jnp.concatenate([halo_top, hid, halo_bot], axis=1)
    halo_left = shift(tall[:, :, merged - chans :], "col", 1)
    halo_right = shift(tall[:, :, :chans], "col", -1)
    padded = jnp.concatenate([halo_left, tall, halo_right], axis=2)
    taps = jnp.tile(conv_weight, (1, cols))
    acc = hid.astype(jnp.float32)
    for tap_a in range(3):
        for tap_b in range(3):
            acc = (
                acc
                + padded[:, tap_a : tap_a + rows, tap_b * chans : tap_b * chans + merged].astype(
                    jnp.float32
                )
                * taps[3 * tap_a + tap_b]
            )
    return acc.astype(jnp.bfloat16)


def solution(mesh):
    placed = (P("tm", "row", "col"), P(), P(), P())
    return jax.shard_map(
        body, mesh=mesh, in_specs=placed, out_specs=P("tm", "row", "col"), check_vma=False
    )
```

time: 66.4 us -> 55 us (0.83)
  the two profiles are of different devices: /device:TPU:105 before, /device:TPU:99 now
where the time goes in v2:
time: 55 us; the launch traced here: 54.7 us
  starting transfers between devices  18.4 us (33%)
  waiting for transfers between devices  13.8 us (25%)
  local copies, waits for them, and re-layouts  9.3 us (17%)
  Pallas kernels  8.85 us (16%)
  other arithmetic  4.23 us (8%)
    ppermute x6, starting transfers between devices, shift(): return lax.ppermute(x, axis, pairs)  18.4 us
    ppermute x6, waiting for transfers between devices, shift(): return lax.ppermute(x, axis, pairs)  13.8 us
    pallas_call x1, Pallas kernels, attend(): pl.pallas_call(attend_kernel, grid=grid, in_specs=[pl.BlockSpec(memory_sp...  8.85 us
    reshape x3, local copies, waits for them, and re-layouts, body(): cells = lambda a: a.reshape(frames, points, chans)  5.48 us
    convert_element_type x1, other arithmetic, body(): return acc.astype(jnp.bfloat16)  2.85 us
    reshape x1, local copies, waits for them, and re-layouts, body(): hid = hidden.reshape(frames, rows, merged)  1.78 us
    unnamed x5, local copies, waits for them, and re-layouts  1.18 us
  transfers between devices with their start and end apart: 6, of which 4 were waited for; matrix products, arithmetic and copies ran while one was open for 12% of the time, Pallas kernels for 0%

profile of v2, /device:TPU:99, one launch (start us, length us, event | category | flops | bytes accessed | tf_op | source)
XLA Modules:
  0.0 54.7 jit_solution(2064001835454762121)
XLA Ops:
  0.0 0.0 copy-start
  0.0 5.4 %collective-permute-start = (bf16[2,32,5120]{2,1,0:T(8,128)(2,1)}, bf16[2,32,5120]{2,1,0:T(8,128)(2,1)S(1)}, u32[]{:S(2)}, u32[]{:S(2)}) collective-permute-start(bf16[2,32,5120]{2,1,0:T(8,128)(2,1)} %param.4), channel_id=1, source_target_pairs={{0,16},{16,32},{32,48},{48,64},{64,80},{80,96},{96,112},{112,128},... | collective-permute-start | bytes 1966088 | tf_op jit(solution)/shard_map/ppermute | solution.py:106
  5.4 1.9 %collective-permute-start.1 = (bf16[2,32,5120]{2,1,0:T(8,128)(2,1)}, bf16[2,32,5120]{2,1,0:T(8,128)(2,1)S(1)}, u32[]{:S(2)}, u32[]{:S(2)}) collective-permute-start(bf16[2,32,5120]{2,1,0:T(8,128)(2,1)} %param.4), channel_id=1, source_target_pairs={{16,0},{32,16},{48,32},{64,48},{80,64},{96,80},{112,96},{128,112},... | collective-permute-start | bytes 1966088 | tf_op jit(solution)/shard_map/ppermute | solution.py:106
  7.4 2.4 %reshape.61.own_ref = bf16[2,512,320]{2,1,0:T(8,128)(2,1)} reshape(bf16[2,32,5120]{2,1,0:T(8,128)(2,1)} %param.4) | data formatting | bytes 1310720 | tf_op jit(solution)/shard_map/reshape | solution.py:120
  9.8 0.0 copy-done
  9.8 1.2 %copy.6 = bf16[320,960]{0,1:T(8,128)(2,1)} copy(bf16[320,960]{1,0:T(8,128)(2,1)S(1)} %copy-done) | data formatting | bytes 1228800 | tf_op args[1]
  11.0 0.5 and_convert_fusion.valid_ref
  11.5 1.8 %collective-permute-done = bf16[2,32,5120]{2,1,0:T(8,128)(2,1)S(1)} collective-permute-done((bf16[2,32,5120]{2,1,0:T(8,128)(2,1)}, bf16[2,32,5120]{2,1,0:T(8,128)(2,1)S(1)}, u32[]{:S(2)}, u32[]{:S(2)}) %collective-permute-start) | collective-permute-done | bytes 655392 | tf_op jit(solution)/shard_map/ppermute | solution.py:106
  13.3 1.5 %reshape.60.prev_ref = bf16[2,512,320]{2,1,0:T(8,128)(2,1)} reshape(bf16[2,32,5120]{2,1,0:T(8,128)(2,1)S(1)} %collective-permute-done) | data formatting | bytes 1310720 | tf_op jit(solution)/shard_map/reshape | solution.py:120
  14.8 4.0 %collective-permute-done.1 = bf16[2,32,5120]{2,1,0:T(8,128)(2,1)S(1)} collective-permute-done((bf16[2,32,5120]{2,1,0:T(8,128)(2,1)}, bf16[2,32,5120]{2,1,0:T(8,128)(2,1)S(1)}, u32[]{:S(2)}, u32[]{:S(2)}) %collective-permute-start.1) | collective-permute-done | bytes 655392 | tf_op jit(solution)/shard_map/ppermute | solution.py:106
  18.8 1.5 %reshape.62.next_ref = bf16[2,512,320]{2,1,0:T(8,128)(2,1)} reshape(bf16[2,32,5120]{2,1,0:T(8,128)(2,1)S(1)} %collective-permute-done.1) | data formatting | bytes 1310720 | tf_op jit(solution)/shard_map/reshape | solution.py:120
  20.3 8.8 %shard_map.46 = bf16[2,512,320]{2,1,0:T(8,128)(2,1)} custom-call(s32[6]{0:T(128)} %and_convert_fusion.valid_ref, bf16[2,512,320]{2,1,0:T(8,128)(2,1)} %reshape.60.prev_ref, bf16[2,512,320]{2,1,0:T(8,128)(2,1)} %reshape.61.own_ref, bf16[2,512,320]{2,1,0:T(8,128)(2,1)} %reshape.62.next_ref, bf16[960,320]{1,0:T(8,128)(2,1)} %bitcast.1, bf16[320,320]{1,0:T(8,128)(2,1)} %wout_ref.1), custom_call_target="tpu_custom_call" | custom-call | tf_op jit(solution)/shard_map/pallas_call | solution.py:84
  29.1 0.0 copy-start.1
  29.1 1.8 %reshape.63 = bf16[2,32,5120]{2,1,0:T(8,128)(2,1)S(1)} reshape(bf16[2,512,320]{2,1,0:T(8,128)(2,1)} %shard_map.46) | data formatting | bytes 1310720 | tf_op jit(solution)/shard_map/reshape | solution.py:122
  30.9 0.1 fusion.9
  31.0 3.8 %collective-permute-start.2 = (bf16[2,1,5120]{2,1,0:T(2,128)(2,1)S(1)}, bf16[2,1,5120]{2,1,0:T(2,128)(2,1)S(1)}, u32[]{:S(2)}, u32[]{:S(2)}) collective-permute-start(bf16[2,1,5120]{2,1,0:T(2,128)(2,1)S(1)} %get-tuple-element.18), channel_id=1, source_target_pairs={{0,8},{1,9},{2,10},{3,11},{4,12},{5,13},{6,14},{7,15},{16,24},{17,... | collective-permute-start | bytes 61448 | tf_op jit(solution)/shard_map/ppermute | solution.py:106
  34.8 1.3 %collective-permute-start.3 = (bf16[2,1,5120]{2,1,0:T(2,128)(2,1)S(1)}, bf16[2,1,5120]{2,1,0:T(2,128)(2,1)S(1)}, u32[]{:S(2)}, u32[]{:S(2)}) collective-permute-start(bf16[2,1,5120]{2,1,0:T(2,128)(2,1)S(1)} %get-tuple-element.19), channel_id=1, source_target_pairs={{8,0},{9,1},{10,2},{11,3},{12,4},{13,5},{14,6},{15,7},{24,16},{25,... | collective-permute-start | bytes 61448 | tf_op jit(solution)/shard_map/ppermute | solution.py:106
  36.1 0.0 collective-permute-done.2
  36.1 4.9 %collective-permute-done.3 = bf16[2,1,5120]{2,1,0:T(2,128)(2,1)S(1)} collective-permute-done((bf16[2,1,5120]{2,1,0:T(2,128)(2,1)S(1)}, bf16[2,1,5120]{2,1,0:T(2,128)(2,1)S(1)}, u32[]{:S(2)}, u32[]{:S(2)}) %collective-permute-start.3) | collective-permute-done | bytes 20512 | tf_op jit(solution)/shard_map/ppermute | solution.py:106
  41.0 0.1 pad_maximum_fusion.5
  41.1 4.1 %collective-permute-start.4 = (bf16[2,34,320]{2,1,0:T(8,128)(2,1)S(1)}, bf16[2,34,320]{2,1,0:T(8,128)(2,1)S(1)}, u32[]{:S(2)}, u32[]{:S(2)}) collective-permute-start(bf16[2,34,320]{2,1,0:T(8,128)(2,1)S(1)} %get-tuple-element.16), channel_id=1, source_target_pairs={{0,1},{1,2},{2,3},{3,4},{4,5},{5,6},{6,7},{8,9},{9,10},{10,11},{11... | collective-permute-start | bytes 130568 | tf_op jit(solution)/shard_map/ppermute | solution.py:106
  45.2 1.9 %collective-permute-start.5 = (bf16[2,34,320]{2,1,0:T(8,128)(2,1)S(1)}, bf16[2,34,320]{2,1,0:T(8,128)(2,1)S(1)}, u32[]{:S(2)}, u32[]{:S(2)}) collective-permute-start(bf16[2,34,320]{2,1,0:T(8,128)(2,1)S(1)} %get-tuple-element.17), channel_id=1, source_target_pairs={{1,0},{2,1},{3,2},{4,3},{5,4},{6,5},{7,6},{9,8},{10,9},{11,10},{12... | collective-permute-start | bytes 130568 | tf_op jit(solution)/shard_map/ppermute | solution.py:106
  47.2 0.0 copy-done.1
  47.2 0.1 slice_reduce_fusion.8
  47.2 0.1 tile.42
  47.3 0.1 tile.44
  47.4 0.1 tile.46
  47.5 0.1 tile.48
  47.6 0.1 tile.50
  47.6 0.1 tile.52
  47.7 0.1 tile.54
  47.8 0.1 tile.56
  47.9 0.1 tile.58
  48.0 0.0 collective-permute-done.4
  48.0 3.1 %collective-permute-done.5 = bf16[2,34,320]{2,1,0:T(8,128)(2,1)S(1)} collective-permute-done((bf16[2,34,320]{2,1,0:T(8,128)(2,1)S(1)}, bf16[2,34,320]{2,1,0:T(8,128)(2,1)S(1)}, u32[]{:S(2)}, u32[]{:S(2)}) %collective-permute-start.5) | collective-permute-done | bytes 43552 | tf_op jit(solution)/shard_map/ppermute | solution.py:106
  51.1 0.8 %maximum_maximum_fusion = (bf16[2,34,5440]{2,1,0:T(8,128)(2,1)S(1)}, bf16[2,34,5440]{2,1,0:T(8,128)(2,1)S(1)}) fusion(bf16[2,1,5120]{2,1,0:T(2,128)(2,1)S(1)} %collective-permute-done.3, bf16[2,32,5120]{2,1,0:T(8,128)(2,1)S(1)} %reshape.63, bf16[2,1,5120]{2,1,0:T(2,128)(2,1)S(1)} %collective-permute-done.2, ...), kind=kLoop, calls=%fused_computation.11 | loop fusion | flops 5918720 | bytes 2263040 | tf_op jit(solution)/shard_map/concatenate | solution.py:129
  51.8 2.8 %fusion.8 = bf16[2,32,5120]{2,1,0:T(8,128)(2,1)} fusion(bf16[2,32,5120]{2,1,0:T(8,128)(2,1)S(1)} %reshape.63, bf16[2,34,5440]{2,1,0:T(8,128)(2,1)S(1)} %get-tuple-element.15, bf16[2,1,5120]{2,1,0:T(2,128)(2,1)S(1)} %collective-permute-done.3, bf16[2,34,5440]{2,1,0:T(8,128)(2,1)S(1)} %get-tuple-element.14, bf16[2,1,5120]{2,1,0:T(2,128)(2,1)S(1)} %collective-permute-done.2, ...), kind=kLoop, calls=%fused_computation.10 | loop fusion | flops 11141120 | bytes 5468160 | tf_op jit(solution)/shard_map/convert_element_type | solution.py:141
  (9 shorter events, 0.0 us)
Async XLA Ops:
  0.0 9.8 %copy-start = (bf16[320,960]{1,0:T(8,128)(2,1)S(1)}, bf16[320,960]{1,0:T(8,128)(2,1)}, u32[]{:S(2)}) copy-start(bf16[320,960]{1,0:T(8,128)(2,1)} %param.5) | copy-start | bytes 1843204
  0.0 13.3 %collective-permute-start = (bf16[2,32,5120]{2,1,0:T(8,128)(2,1)}, bf16[2,32,5120]{2,1,0:T(8,128)(2,1)S(1)}, u32[]{:S(2)}, u32[]{:S(2)}) collective-permute-start(bf16[2,32,5120]{2,1,0:T(8,128)(2,1)} %param.4), channel_id=1, source_target_pairs={{0,16},{16,32},{32,48},{48,64},{64,80},{80,96},{96,112},{112,128},... | collective-permute-start | bytes 1966088 | tf_op jit(solution)/shard_map/ppermute | solution.py:106
  5.4 13.3 %collective-permute-start.1 = (bf16[2,32,5120]{2,1,0:T(8,128)(2,1)}, bf16[2,32,5120]{2,1,0:T(8,128)(2,1)S(1)}, u32[]{:S(2)}, u32[]{:S(2)}) collective-permute-start(bf16[2,32,5120]{2,1,0:T(8,128)(2,1)} %param.4), channel_id=1, source_target_pairs={{16,0},{32,16},{48,32},{64,48},{80,64},{96,80},{112,96},{128,112},... | collective-permute-start | bytes 1966088 | tf_op jit(solution)/shard_map/ppermute | solution.py:106
  29.1 18.0 %copy-start.1 = (f32[9,320]{1,0:T(8,128)S(1)}, f32[9,320]{1,0:T(8,128)}, u32[]{:S(2)}) copy-start(f32[9,320]{1,0:T(8,128)} %param.7) | copy-start | bytes 34564
  31.0 5.1 %collective-permute-start.2 = (bf16[2,1,5120]{2,1,0:T(2,128)(2,1)S(1)}, bf16[2,1,5120]{2,1,0:T(2,128)(2,1)S(1)}, u32[]{:S(2)}, u32[]{:S(2)}) collective-permute-start(bf16[2,1,5120]{2,1,0:T(2,128)(2,1)S(1)} %get-tuple-element.18), channel_id=1, source_target_pairs={{0,8},{1,9},{2,10},{3,11},{4,12},{5,13},{6,14},{7,15},{16,24},{17,... | collective-permute-start | bytes 61448 | tf_op jit(solution)/shard_map/ppermute | solution.py:106
  34.8 6.3 %collective-permute-start.3 = (bf16[2,1,5120]{2,1,0:T(2,128)(2,1)S(1)}, bf16[2,1,5120]{2,1,0:T(2,128)(2,1)S(1)}, u32[]{:S(2)}, u32[]{:S(2)}) collective-permute-start(bf16[2,1,5120]{2,1,0:T(2,128)(2,1)S(1)} %get-tuple-element.19), channel_id=1, source_target_pairs={{8,0},{9,1},{10,2},{11,3},{12,4},{13,5},{14,6},{15,7},{24,16},{25,... | collective-permute-start | bytes 61448 | tf_op jit(solution)/shard_map/ppermute | solution.py:106
  41.1 6.8 %collective-permute-start.4 = (bf16[2,34,320]{2,1,0:T(8,128)(2,1)S(1)}, bf16[2,34,320]{2,1,0:T(8,128)(2,1)S(1)}, u32[]{:S(2)}, u32[]{:S(2)}) collective-permute-start(bf16[2,34,320]{2,1,0:T(8,128)(2,1)S(1)} %get-tuple-element.16), channel_id=1, source_target_pairs={{0,1},{1,2},{2,3},{3,4},{4,5},{5,6},{6,7},{8,9},{9,10},{10,11},{11... | collective-permute-start | bytes 130568 | tf_op jit(solution)/shard_map/ppermute | solution.py:106
  45.2 5.9 %collective-permute-start.5 = (bf16[2,34,320]{2,1,0:T(8,128)(2,1)S(1)}, bf16[2,34,320]{2,1,0:T(8,128)(2,1)S(1)}, u32[]{:S(2)}, u32[]{:S(2)}) collective-permute-start(bf16[2,34,320]{2,1,0:T(8,128)(2,1)S(1)} %get-tuple-element.17), channel_id=1, source_target_pairs={{1,0},{2,1},{3,2},{4,3},{5,4},{6,5},{7,6},{9,8},{10,9},{11,10},{12... | collective-permute-start | bytes 130568 | tf_op jit(solution)/shard_map/ppermute | solution.py:106

commit v3 on v2

--- a/solution.py
+++ b/solution.py
@@ -1,11 +1,10 @@
-import functools
-
 import jax
 import jax.numpy as jnp
 from jax import lax
 from jax.experimental import pallas as pl
 from jax.experimental.pallas import tpu as pltpu
 from jax.sharding import PartitionSpec as P
+
 
 HEAD_DIM = 64
 BLOCK = 128
@@ -75,11 +74,15 @@
     out_ref[1] = hidden[block:]
 
 
-def attend(valid, prev, own, nxt, w_qkv, w_out):
+def attend(valid, prev, own, nxt, w_qkv, w_out, start=0, count=None):
     frames, points, chans = own.shape
+    count = points if count is None else count
     w_qkv = w_qkv.T
-    grid = (points // BLOCK,)
-    cell_spec = pl.BlockSpec((frames, BLOCK, chans), lambda i: (0, i, 0))
+    grid = (count // BLOCK,)
+    assert count % BLOCK == 0 and start % BLOCK == 0
+    base = start // BLOCK
+    cell_spec = pl.BlockSpec((frames, BLOCK, chans), lambda i: (0, i + base, 0))
+    out_spec = pl.BlockSpec((frames, BLOCK, chans), lambda i: (0, i, 0))
     full = lambda shape: pl.BlockSpec(shape, lambda i: (0, 0))
     return pl.pallas_call(
         attend_kernel,
@@ -92,8 +95,8 @@
             full(w_qkv.shape),
             full(w_out.shape),
         ],
-        out_specs=cell_spec,
-        out_shape=jax.ShapeDtypeStruct(own.shape, jnp.bfloat16),
+        out_specs=out_spec,
+        out_shape=jax.ShapeDtypeStruct((frames, count, chans), jnp.bfloat16),
     )(valid, prev, own, nxt, w_qkv, w_out)
 
 
@@ -118,15 +121,43 @@
     where_t = first + jnp.arange(6, dtype=jnp.int32) - 2
     valid = ((where_t >= 0) & (where_t < total)).astype(jnp.int32)
     cells = lambda a: a.reshape(frames, points, chans)
-    hidden = attend(valid, cells(x_prev), cells(latents), cells(x_next), w_qkv, w_out)
-    hid = hidden.reshape(frames, rows, merged)
 
-    halo_top = shift(hid[:, rows - 1 :, :], "row", 1)
-    halo_bot = shift(hid[:, :1, :], "row", -1)
-    tall = jnp.concatenate([halo_top, hid, halo_bot], axis=1)
+    x_wide = jnp.concatenate([x_prev, latents, x_next], axis=0)
+    halo_top = shift(x_wide[:, rows - 1 :, :], "row", 1)
+    halo_bot = shift(x_wide[:, :1, :], "row", -1)
+    tall = jnp.concatenate([halo_top, x_wide, halo_bot], axis=1)
     halo_left = shift(tall[:, :, merged - chans :], "col", 1)
     halo_right = shift(tall[:, :, :chans], "col", -1)
-    padded = jnp.concatenate([halo_left, tall, halo_right], axis=2)
+
+    own_c = cells(latents)
+    prev_c, next_c = cells(x_prev), cells(x_next)
+    half = points // 2
+    hid_a = attend(valid, prev_c, own_c, next_c, w_qkv, w_out, 0, half)
+    hid_b = attend(valid, prev_c, own_c, next_c, w_qkv, w_out, half, half)
+    hid = jnp.concatenate([hid_a, hid_b], axis=1).reshape(frames, rows, merged)
+
+    span = 2 * (rows + 2) + 2 * cols
+    ring_pts = -(-span // BLOCK) * BLOCK
+    ring = jnp.concatenate(
+        [
+            halo_left,
+            halo_right,
+            halo_top.reshape(3 * frames, cols, chans),
+            halo_bot.reshape(3 * frames, cols, chans),
+            jnp.zeros((3 * frames, ring_pts - span, chans), jnp.bfloat16),
+        ],
+        axis=1,
+    )
+    ring_hid = attend(
+        valid, ring[:frames], ring[frames : 2 * frames], ring[2 * frames :], w_qkv, w_out
+    )
+    tall_n = rows + 2
+    h_left = ring_hid[:, :tall_n]
+    h_right = ring_hid[:, tall_n : 2 * tall_n]
+    h_top = ring_hid[:, 2 * tall_n : 2 * tall_n + cols].reshape(frames, 1, merged)
+    h_bot = ring_hid[:, 2 * tall_n + cols : span].reshape(frames, 1, merged)
+    h_tall = jnp.concatenate([h_top, hid, h_bot], axis=1)
+    padded = jnp.concatenate([h_left, h_tall, h_right], axis=2)
     taps = jnp.tile(conv_weight, (1, cols))
     acc = hid.astype(jnp.float32)
     for tap_a in range(3):

time: 55 us -> 67.1 us (1.22)
  the two profiles are of different devices: /device:TPU:99 before, /device:TPU:109 now
where the time goes in v3:
time: 67.1 us; the launch traced here: 66.6 us
  starting transfers between devices  20.5 us (31%)
  local copies, waits for them, and re-layouts  19.7 us (29%)
  Pallas kernels  14.7 us (22%)
  other arithmetic  5.86 us (9%)
  waiting for transfers between devices  5.54 us (8%)
    ppermute x6, starting transfers between devices, shift(): return lax.ppermute(x, axis, pairs)  20.5 us
    pallas_call x3, Pallas kernels, attend(): pl.pallas_call(attend_kernel, grid=grid, in_specs=[pl.BlockSpec(memory_sp...  14.7 us
    reshape x3, local copies, waits for them, and re-layouts, body(): cells = lambda a: a.reshape(frames, points, chans)  6.4 us
    another operation x18, local copies, waits for them, and re-layouts, body(): taps = jnp.tile(conv_weight, (1, cols))  5.55 us
    ppermute x6, waiting for transfers between devices, shift(): return lax.ppermute(x, axis, pairs)  5.54 us
    convert_element_type x1, other arithmetic, body(): return acc.astype(jnp.bfloat16)  2.84 us
  transfers between devices with their start and end apart: 6, of which 3 were waited for; matrix products, arithmetic and copies ran while one was open for 23% of the time, Pallas kernels for 16%

profile of v3, /device:TPU:109, one launch (start us, length us, event | category | flops | bytes accessed | tf_op | source)
XLA Modules:
  0.0 66.6 jit_solution(1491607714766384836)
XLA Ops:
  0.0 5.4 %collective-permute-start = (bf16[2,32,5120]{2,1,0:T(8,128)(2,1)}, bf16[2,32,5120]{2,1,0:T(8,128)(2,1)S(1)}, u32[]{:S(2)}, u32[]{:S(2)}) collective-permute-start(bf16[2,32,5120]{2,1,0:T(8,128)(2,1)} %param.4), channel_id=1, source_target_pairs={{0,16},{16,32},{32,48},{48,64},{64,80},{80,96},{96,112},{112,128},... | collective-permute-start | bytes 1966088 | tf_op jit(solution)/shard_map/ppermute | solution.py:109
  5.4 1.9 %collective-permute-start.1 = (bf16[2,32,5120]{2,1,0:T(8,128)(2,1)}, bf16[2,32,5120]{2,1,0:T(8,128)(2,1)}, u32[]{:S(2)}, u32[]{:S(2)}) collective-permute-start(bf16[2,32,5120]{2,1,0:T(8,128)(2,1)} %param.4), channel_id=1, source_target_pairs={{16,0},{32,16},{48,32},{64,48},{80,64},{96,80},{112,96},{128,112},... | collective-permute-start | bytes 1966088 | tf_op jit(solution)/shard_map/ppermute | solution.py:109
  7.4 2.4 %reshape.73.own_ref = bf16[2,512,320]{2,1,0:T(8,128)(2,1)} reshape(bf16[2,32,5120]{2,1,0:T(8,128)(2,1)} %param.4) | data formatting | bytes 1310720 | tf_op jit(solution)/shard_map/reshape | solution.py:123
  9.8 0.0 copy-done.3
  9.8 1.2 %copy.10 = bf16[320,960]{0,1:T(8,128)(2,1)} copy(bf16[320,960]{1,0:T(8,128)(2,1)S(1)} %copy-done.3) | data formatting | bytes 1228800 | tf_op args[1]
  11.0 0.1 slice_reduce_fusion.8
  11.1 0.1 tile.42
  11.1 0.7 %tile.44 = f32[5120]{0:T(1024)} reshape(f32[16,320]{1,0:T(8,128)S(1)} %tile.43) | data formatting | bytes 40960 | tf_op jit(solution)/shard_map/tile | solution.py:161
  11.8 0.7 %tile.46 = f32[5120]{0:T(1024)} reshape(f32[16,320]{1,0:T(8,128)S(1)} %tile.45) | data formatting | bytes 40960 | tf_op jit(solution)/shard_map/tile | solution.py:161
  12.5 0.7 %tile.48 = f32[5120]{0:T(1024)} reshape(f32[16,320]{1,0:T(8,128)S(1)} %tile.47) | data formatting | bytes 40960 | tf_op jit(solution)/shard_map/tile | solution.py:161
  13.2 0.7 %tile.50 = f32[5120]{0:T(1024)} reshape(f32[16,320]{1,0:T(8,128)S(1)} %tile.49) | data formatting | bytes 40960 | tf_op jit(solution)/shard_map/tile | solution.py:161
  13.9 0.7 %tile.52 = f32[5120]{0:T(1024)} reshape(f32[16,320]{1,0:T(8,128)S(1)} %tile.51) | data formatting | bytes 40960 | tf_op jit(solution)/shard_map/tile | solution.py:161
  14.6 0.7 %tile.54 = f32[5120]{0:T(1024)} reshape(f32[16,320]{1,0:T(8,128)S(1)} %tile.53) | data formatting | bytes 40960 | tf_op jit(solution)/shard_map/tile | solution.py:161
  15.2 0.7 %tile.56 = f32[5120]{0:T(1024)} reshape(f32[16,320]{1,0:T(8,128)S(1)} %tile.55) | data formatting | bytes 40960 | tf_op jit(solution)/shard_map/tile | solution.py:161
  15.9 0.7 %tile.58 = f32[5120]{0:T(1024)} reshape(f32[16,320]{1,0:T(8,128)S(1)} %tile.57) | data formatting | bytes 40960 | tf_op jit(solution)/shard_map/tile | solution.py:161
  16.6 0.0 collective-permute-done
  16.7 2.2 %collective-permute-done.1 = bf16[2,32,5120]{2,1,0:T(8,128)(2,1)} collective-permute-done((bf16[2,32,5120]{2,1,0:T(8,128)(2,1)}, bf16[2,32,5120]{2,1,0:T(8,128)(2,1)}, u32[]{:S(2)}, u32[]{:S(2)}) %collective-permute-start.1) | collective-permute-done | bytes 655392 | tf_op jit(solution)/shard_map/ppermute | solution.py:109
  18.9 1.1 %constant_dynamic-update-slice_fusion = bf16[6,32,5120]{2,1,0:T(8,128)(2,1)S(1)} fusion(bf16[6,32,5120]{2,1,0:T(8,128)(2,1)S(1)} %constant_dynamic-update-slice_fusion.1, bf16[2,32,5120]{2,1,0:T(8,128)(2,1)} %collective-permute-done.1), kind=kLoop, calls=%fused_computation.19 | loop fusion | bytes 1310720 | tf_op jit(solution)/shard_map/concatenate | solution.py:125
  20.0 0.2 fusion.9
  20.2 1.3 %collective-permute-start.2 = (bf16[6,1,5120]{2,1,0:T(2,128)(2,1)S(1)}, bf16[6,1,5120]{2,1,0:T(2,128)(2,1)S(1)}, u32[]{:S(2)}, u32[]{:S(2)}) collective-permute-start(bf16[6,1,5120]{2,1,0:T(2,128)(2,1)S(1)} %get-tuple-element.16), channel_id=1, source_target_pairs={{0,8},{1,9},{2,10},{3,11},{4,12},{5,13},{6,14},{7,15},{16,24},{17,... | collective-permute-start | bytes 184328 | tf_op jit(solution)/shard_map/ppermute | solution.py:109
  21.5 5.5 %collective-permute-start.3 = (bf16[6,1,5120]{2,1,0:T(2,128)(2,1)S(1)}, bf16[6,1,5120]{2,1,0:T(2,128)(2,1)S(1)}, u32[]{:S(2)}, u32[]{:S(2)}) collective-permute-start(bf16[6,1,5120]{2,1,0:T(2,128)(2,1)S(1)} %get-tuple-element.17), channel_id=1, source_target_pairs={{8,0},{9,1},{10,2},{11,3},{12,4},{13,5},{14,6},{15,7},{24,16},{25,... | collective-permute-start | bytes 184328 | tf_op jit(solution)/shard_map/ppermute | solution.py:109
  27.0 0.6 and_convert_fusion.valid_ref
  27.6 1.5 %reshape.72.prev_ref = bf16[2,512,320]{2,1,0:T(8,128)(2,1)} reshape(bf16[2,32,5120]{2,1,0:T(8,128)(2,1)S(1)} %collective-permute-done) | data formatting | bytes 1310720 | tf_op jit(solution)/shard_map/reshape | solution.py:123
  29.1 2.4 %reshape.74.next_ref = bf16[2,512,320]{2,1,0:T(8,128)(2,1)} reshape(bf16[2,32,5120]{2,1,0:T(8,128)(2,1)} %collective-permute-done.1) | data formatting | bytes 1310720 | tf_op jit(solution)/shard_map/reshape | solution.py:123
  31.6 5.5 %shard_map.47 = bf16[2,256,320]{2,1,0:T(8,128)(2,1)} custom-call(s32[6]{0:T(128)} %and_convert_fusion.valid_ref, bf16[2,512,320]{2,1,0:T(8,128)(2,1)} %reshape.72.prev_ref, bf16[2,512,320]{2,1,0:T(8,128)(2,1)} %reshape.73.own_ref, bf16[2,512,320]{2,1,0:T(8,128)(2,1)} %reshape.74.next_ref, bf16[960,320]{1,0:T(8,128)(2,1)} %bitcast.1, bf16[320,320]{1,0:T(8,128)(2,1)} %wout_ref.5), custom_call_target="tpu_custom_call" | custom-call | tf_op jit(solution)/shard_map/pallas_call | solution.py:87
  37.1 5.5 %shard_map.46 = bf16[2,256,320]{2,1,0:T(8,128)(2,1)} custom-call(s32[6]{0:T(128)} %and_convert_fusion.valid_ref, bf16[2,512,320]{2,1,0:T(8,128)(2,1)} %reshape.72.prev_ref, bf16[2,512,320]{2,1,0:T(8,128)(2,1)} %reshape.73.own_ref, bf16[2,512,320]{2,1,0:T(8,128)(2,1)} %reshape.74.next_ref, bf16[960,320]{1,0:T(8,128)(2,1)} %bitcast.2, bf16[320,320]{1,0:T(8,128)(2,1)} %wout_ref.5), custom_call_target="tpu_custom_call" | custom-call | tf_op jit(solution)/shard_map/pallas_call | solution.py:87
  42.6 0.0 collective-permute-done.2
  42.6 0.0 collective-permute-done.3
  42.6 0.9 %pad_maximum_fusion.4 = (bf16[6,34,320]{2,1,0:T(8,128)(2,1)}, bf16[6,34,320]{2,1,0:T(8,128)(2,1)}) fusion(bf16[6,1,5120]{2,1,0:T(2,128)(2,1)S(1)} %collective-permute-done.3, bf16[6,32,5120]{2,1,0:T(8,128)(2,1)S(1)} %constant_dynamic-update-slice_fusion, bf16[6,1,5120]{2,1,0:T(2,128)(2,1)S(1)} %collective-permute-done.2), kind=kLoop, calls=%fused_computation.16 | loop fusion | flops 783360 | bytes 2350080 | tf_op jit(solution)/shard_map/concatenate | solution.py:128
  43.5 2.8 %collective-permute-start.4 = (bf16[6,34,320]{2,1,0:T(8,128)(2,1)}, bf16[6,34,320]{2,1,0:T(8,128)(2,1)S(1)}, u32[]{:S(2)}, u32[]{:S(2)}) collective-permute-start(bf16[6,34,320]{2,1,0:T(8,128)(2,1)} %get-tuple-element.15), channel_id=1, source_target_pairs={{0,1},{1,2},{2,3},{3,4},{4,5},{5,6},{6,7},{8,9},{9,10},{10,11},{11... | collective-permute-start | bytes 391688 | tf_op jit(solution)/shard_map/ppermute | solution.py:109
  46.3 3.5 %collective-permute-start.5 = (bf16[6,34,320]{2,1,0:T(8,128)(2,1)}, bf16[6,34,320]{2,1,0:T(8,128)(2,1)S(1)}, u32[]{:S(2)}, u32[]{:S(2)}) collective-permute-start(bf16[6,34,320]{2,1,0:T(8,128)(2,1)} %get-tuple-element.14), channel_id=1, source_target_pairs={{1,0},{2,1},{3,2},{4,3},{5,4},{6,5},{7,6},{9,8},{10,9},{11,10},{12... | collective-permute-start | bytes 391688 | tf_op jit(solution)/shard_map/ppermute | solution.py:109
  49.9 0.1 pad_maximum_fusion.1
  50.0 0.6 reshape.75
  50.6 0.3 reduce
  51.0 0.1 reshape.76
  51.1 0.4 reduce.1
  51.4 0.1 reshape.77
  51.6 1.3 %collective-permute-done.4 = bf16[6,34,320]{2,1,0:T(8,128)(2,1)S(1)} collective-permute-done((bf16[6,34,320]{2,1,0:T(8,128)(2,1)}, bf16[6,34,320]{2,1,0:T(8,128)(2,1)S(1)}, u32[]{:S(2)}, u32[]{:S(2)}) %collective-permute-start.4) | collective-permute-done | bytes 130592 | tf_op jit(solution)/shard_map/ppermute | solution.py:109
  52.8 2.1 %collective-permute-done.5 = bf16[6,34,320]{2,1,0:T(8,128)(2,1)S(1)} collective-permute-done((bf16[6,34,320]{2,1,0:T(8,128)(2,1)}, bf16[6,34,320]{2,1,0:T(8,128)(2,1)S(1)}, u32[]{:S(2)}, u32[]{:S(2)}) %collective-permute-start.5) | collective-permute-done | bytes 130592 | tf_op jit(solution)/shard_map/ppermute | solution.py:109
  55.0 1.3 %concatenate.35 = bf16[6,128,320]{2,1,0:T(8,128)(2,1)S(1)} concatenate(bf16[6,34,320]{2,1,0:T(8,128)(2,1)S(1)} %collective-permute-done.4, bf16[6,34,320]{2,1,0:T(8,128)(2,1)S(1)} %collective-permute-done.5, bf16[6,16,320]{2,1,0:T(8,128)(2,1)S(1)} %reshape.76, bf16[6,16,320]{2,1,0:T(8,128)(2,1)S(1)} %reshape.77, bf16[6,28,320]{2,1,0:T(8,128)(2,1)S(1)} %broadcast_in_dim.3), dimensions={1} | concatenate | bytes 983040 | tf_op jit(solution)/shard_map/concatenate | solution.py:141
  56.3 0.8 %fusion.10 = (bf16[2,128,320]{2,1,0:T(8,128)(2,1)}, bf16[2,128,320]{2,1,0:T(8,128)(2,1)}, bf16[2,128,320]{2,1,0:T(8,128)(2,1)}) fusion(bf16[6,128,320]{2,1,0:T(8,128)(2,1)S(1)} %concatenate.35), kind=kLoop, calls=%fused_computation.33 | loop fusion | bytes 983040 | tf_op jit(solution)/shard_map/slice | solution.py:152
  57.1 3.7 %shard_map.48 = bf16[2,128,320]{2,1,0:T(8,128)(2,1)} custom-call(s32[6]{0:T(128)} %and_convert_fusion.valid_ref, bf16[2,128,320]{2,1,0:T(8,128)(2,1)} %get-tuple-element.22.prev_ref, bf16[2,128,320]{2,1,0:T(8,128)(2,1)} %get-tuple-element.21.own_ref, bf16[2,128,320]{2,1,0:T(8,128)(2,1)} %get-tuple-element.20.next_ref, bf16[960,320]{1,0:T(8,128)(2,1)} %bitcast.3, ...), custom_call_target="tpu_custom_call" | custom-call | tf_op jit(solution)/shard_map/pallas_call | solution.py:87
  60.8 1.0 %fusion.11 = (bf16[2,34,320]{2,1,0:T(8,128)(2,1)S(1)}, bf16[2,34,320]{2,1,0:T(8,128)(2,1)S(1)}) fusion(bf16[2,128,320]{2,1,0:T(8,128)(2,1)} %shard_map.48), kind=kLoop, calls=%fused_computation.34 | loop fusion | bytes 174080 | tf_op jit(solution)/shard_map/slice | solution.py:155
  61.8 0.9 %fusion.12 = (bf16[2,16,320]{2,1,0:T(8,128)(2,1)S(1)}, bf16[2,16,320]{2,1,0:T(8,128)(2,1)S(1)}) fusion(bf16[2,128,320]{2,1,0:T(8,128)(2,1)} %shard_map.48), kind=kLoop, calls=%fused_computation.35 | loop fusion | bytes 81920 | tf_op jit(solution)/shard_map/slice | solution.py:157
  62.6 0.1 reshape.80
  62.8 0.1 reshape.81
  62.9 0.8 %maximum_maximum_fusion = (bf16[2,34,5440]{2,1,0:T(8,128)(2,1)S(1)}, bf16[2,34,5440]{2,1,0:T(8,128)(2,1)S(1)}) fusion(bf16[2,1,5120]{2,1,0:T(2,128)(2,1)S(1)} %reshape.81, bf16[2,32,5120]{2,1,0:T(8,128)(2,1)S(1)} %reshape.75, bf16[2,1,5120]{2,1,0:T(2,128)(2,1)S(1)} %reshape.80, bf16[2,34,320]{2,1,0:T(8,128)(2,1)S(1)} %get-tuple-element.23, ...), kind=kLoop, calls=%fused_computation.11 | loop fusion | flops 5918720 | bytes 2263040 | tf_op jit(solution)/shard_map/concatenate | solution.py:160
  63.8 2.8 %fusion.8 = bf16[2,32,5120]{2,1,0:T(8,128)(2,1)} fusion(bf16[2,32,5120]{2,1,0:T(8,128)(2,1)S(1)} %reshape.75, bf16[2,34,5440]{2,1,0:T(8,128)(2,1)S(1)} %get-tuple-element.19, bf16[2,1,5120]{2,1,0:T(2,128)(2,1)S(1)} %reshape.81, bf16[2,34,5440]{2,1,0:T(8,128)(2,1)S(1)} %get-tuple-element.18, bf16[2,1,5120]{2,1,0:T(2,128)(2,1)S(1)} %reshape.80, ...), kind=kLoop, calls=%fused_computation.10 | loop fusion | flops 11141120 | bytes 5468160 | tf_op jit(solution)/shard_map/convert_element_type | solution.py:172
  (37 shorter events, 0.2 us)
Async XLA Ops:
  0.0 9.8 %copy-start.3 = (bf16[320,960]{1,0:T(8,128)(2,1)S(1)}, bf16[320,960]{1,0:T(8,128)(2,1)}, u32[]{:S(2)}) copy-start(bf16[320,960]{1,0:T(8,128)(2,1)} %param.5) | copy-start | bytes 1843204
  0.0 16.6 %collective-permute-start = (bf16[2,32,5120]{2,1,0:T(8,128)(2,1)}, bf16[2,32,5120]{2,1,0:T(8,128)(2,1)S(1)}, u32[]{:S(2)}, u32[]{:S(2)}) collective-permute-start(bf16[2,32,5120]{2,1,0:T(8,128)(2,1)} %param.4), channel_id=1, source_target_pairs={{0,16},{16,32},{32,48},{48,64},{64,80},{80,96},{96,112},{112,128},... | collective-permute-start | bytes 1966088 | tf_op jit(solution)/shard_map/ppermute | solution.py:109
  5.4 13.4 %collective-permute-start.1 = (bf16[2,32,5120]{2,1,0:T(8,128)(2,1)}, bf16[2,32,5120]{2,1,0:T(8,128)(2,1)}, u32[]{:S(2)}, u32[]{:S(2)}) collective-permute-start(bf16[2,32,5120]{2,1,0:T(8,128)(2,1)} %param.4), channel_id=1, source_target_pairs={{16,0},{32,16},{48,32},{64,48},{80,64},{96,80},{112,96},{128,112},... | collective-permute-start | bytes 1966088 | tf_op jit(solution)/shard_map/ppermute | solution.py:109
  7.4 3.6 %copy-start.12 = (f32[9,320]{1,0:T(8,128)S(1)}, f32[9,320]{1,0:T(8,128)}, u32[]{:S(2)}) copy-start(f32[9,320]{1,0:T(8,128)} %param.7) | copy-start | bytes 34564
  11.0 5.7 %copy-start = (bf16[2,32,5120]{2,1,0:T(8,128)(2,1)S(1)}, bf16[2,32,5120]{2,1,0:T(8,128)(2,1)}, u32[]{:S(2)}) copy-start(bf16[2,32,5120]{2,1,0:T(8,128)(2,1)} %param.4) | copy-start | bytes 1966084
  20.2 22.3 %collective-permute-start.2 = (bf16[6,1,5120]{2,1,0:T(2,128)(2,1)S(1)}, bf16[6,1,5120]{2,1,0:T(2,128)(2,1)S(1)}, u32[]{:S(2)}, u32[]{:S(2)}) collective-permute-start(bf16[6,1,5120]{2,1,0:T(2,128)(2,1)S(1)} %get-tuple-element.16), channel_id=1, source_target_pairs={{0,8},{1,9},{2,10},{3,11},{4,12},{5,13},{6,14},{7,15},{16,24},{17,... | collective-permute-start | bytes 184328 | tf_op jit(solution)/shard_map/ppermute | solution.py:109
  21.5 21.1 %collective-permute-start.3 = (bf16[6,1,5120]{2,1,0:T(2,128)(2,1)S(1)}, bf16[6,1,5120]{2,1,0:T(2,128)(2,1)S(1)}, u32[]{:S(2)}, u32[]{:S(2)}) collective-permute-start(bf16[6,1,5120]{2,1,0:T(2,128)(2,1)S(1)} %get-tuple-element.17), channel_id=1, source_target_pairs={{8,0},{9,1},{10,2},{11,3},{12,4},{13,5},{14,6},{15,7},{24,16},{25,... | collective-permute-start | bytes 184328 | tf_op jit(solution)/shard_map/ppermute | solution.py:109
  42.6 7.3 %copy-start.1 = (bf16[2,256,320]{2,1,0:T(8,128)(2,1)S(1)}, bf16[2,256,320]{2,1,0:T(8,128)(2,1)}, u32[]{:S(2)}) copy-start(bf16[2,256,320]{2,1,0:T(8,128)(2,1)} %shard_map.47) | copy-start | bytes 983044
  42.6 7.3 %copy-start.2 = (bf16[2,256,320]{2,1,0:T(8,128)(2,1)S(1)}, bf16[2,256,320]{2,1,0:T(8,128)(2,1)}, u32[]{:S(2)}) copy-start(bf16[2,256,320]{2,1,0:T(8,128)(2,1)} %shard_map.46) | copy-start | bytes 983044
  43.5 9.3 %collective-permute-start.4 = (bf16[6,34,320]{2,1,0:T(8,128)(2,1)}, bf16[6,34,320]{2,1,0:T(8,128)(2,1)S(1)}, u32[]{:S(2)}, u32[]{:S(2)}) collective-permute-start(bf16[6,34,320]{2,1,0:T(8,128)(2,1)} %get-tuple-element.15), channel_id=1, source_target_pairs={{0,1},{1,2},{2,3},{3,4},{4,5},{5,6},{6,7},{8,9},{9,10},{10,11},{11... | collective-permute-start | bytes 391688 | tf_op jit(solution)/shard_map/ppermute | solution.py:109
  46.3 8.6 %collective-permute-start.5 = (bf16[6,34,320]{2,1,0:T(8,128)(2,1)}, bf16[6,34,320]{2,1,0:T(8,128)(2,1)S(1)}, u32[]{:S(2)}, u32[]{:S(2)}) collective-permute-start(bf16[6,34,320]{2,1,0:T(8,128)(2,1)} %get-tuple-element.14), channel_id=1, source_target_pairs={{1,0},{2,1},{3,2},{4,3},{5,4},{6,5},{7,6},{9,8},{10,9},{11,10},{12... | collective-permute-start | bytes 391688 | tf_op jit(solution)/shard_map/ppermute | solution.py:109
  62.9 0.8 %copy-start.4 = (f32[5120]{0:T(1024)S(1)}, f32[5120]{0:T(1024)}, u32[]{:S(2)}) copy-start(f32[5120]{0:T(1024)} %tile.44) | copy-start | bytes 61444
  62.9 0.8 %copy-start.5 = (f32[5120]{0:T(1024)S(1)}, f32[5120]{0:T(1024)}, u32[]{:S(2)}) copy-start(f32[5120]{0:T(1024)} %tile.46) | copy-start | bytes 61444
  62.9 0.8 %copy-start.6 = (f32[5120]{0:T(1024)S(1)}, f32[5120]{0:T(1024)}, u32[]{:S(2)}) copy-start(f32[5120]{0:T(1024)} %tile.48) | copy-start | bytes 61444
  62.9 0.8 %copy-start.7 = (f32[5120]{0:T(1024)S(1)}, f32[5120]{0:T(1024)}, u32[]{:S(2)}) copy-start(f32[5120]{0:T(1024)} %tile.50) | copy-start | bytes 61444
  62.9 0.8 %copy-start.8 = (f32[5120]{0:T(1024)S(1)}, f32[5120]{0:T(1024)}, u32[]{:S(2)}) copy-start(f32[5120]{0:T(1024)} %tile.52) | copy-start | bytes 61444
  62.9 0.8 %copy-start.9 = (f32[5120]{0:T(1024)S(1)}, f32[5120]{0:T(1024)}, u32[]{:S(2)}) copy-start(f32[5120]{0:T(1024)} %tile.54) | copy-start | bytes 61444
  62.9 0.8 %copy-start.10 = (f32[5120]{0:T(1024)S(1)}, f32[5120]{0:T(1024)}, u32[]{:S(2)}) copy-start(f32[5120]{0:T(1024)} %tile.56) | copy-start | bytes 61444
  62.9 0.8 %copy-start.11 = (f32[5120]{0:T(1024)S(1)}, f32[5120]{0:T(1024)}, u32[]{:S(2)}) copy-start(f32[5120]{0:T(1024)} %tile.58) | copy-start | bytes 61444

commit v4 on v2

--- a/solution.py
+++ b/solution.py
@@ -11,27 +11,24 @@
 BLOCK = 128
 
 
-def layer_norm(flat):
-    mean = jnp.mean(flat, axis=-1, keepdims=True)
-    cent = flat - mean
-    var = jnp.mean(cent * cent, axis=-1, keepdims=True)
+def layer_norm_t(cols):
+    mean = jnp.mean(cols, axis=0, keepdims=True)
+    cent = cols - mean
+    var = jnp.mean(cent * cent, axis=0, keepdims=True)
     return (cent * lax.rsqrt(var + 1e-05)).astype(jnp.bfloat16)
 
 
 def attend_kernel(valid_ref, prev_ref, own_ref, next_ref, wqkv_ref, wout_ref, out_ref):
     chans = wout_ref.shape[0]
     heads = chans // HEAD_DIM
-    block = own_ref.shape[1]
+    block = own_ref.shape[2]
     frames = [prev_ref[0], prev_ref[1], own_ref[0], own_ref[1], next_ref[0], next_ref[1]]
-    normed = [layer_norm(f.astype(jnp.float32)) for f in frames]
-    nt = (((1,), (1,)), ((), ()))
-    own_n = jnp.concatenate([normed[2], normed[3]], axis=0)
-    qkv = lax.dot_general(
-        wqkv_ref[...], own_n, nt, preferred_element_type=jnp.float32
-    ).astype(jnp.bfloat16)
-    nb_n = jnp.concatenate([normed[0], normed[1], normed[4], normed[5]], axis=0)
-    kv_nb = lax.dot_general(
-        wqkv_ref[chans:, :], nb_n, nt, preferred_element_type=jnp.float32
+    normed = [layer_norm_t(f.astype(jnp.float32)) for f in frames]
+    own_n = jnp.concatenate([normed[2], normed[3]], axis=1)
+    qkv = jnp.dot(wqkv_ref[...], own_n, preferred_element_type=jnp.float32).astype(jnp.bfloat16)
+    nb_n = jnp.concatenate([normed[0], normed[1], normed[4], normed[5]], axis=1)
+    kv_nb = jnp.dot(
+        wqkv_ref[chans:, :], nb_n, preferred_element_type=jnp.float32
     ).astype(jnp.bfloat16)
     keys = [None] * 6
     vals = [None] * 6
@@ -67,20 +64,21 @@
             mixed = term if mixed is None else mixed + term
         outs.append(mixed.astype(jnp.bfloat16))
     attended = jnp.concatenate(outs, axis=1)
-    tn = (((0,), (0,)), ((), ()))
-    proj = lax.dot_general(attended, wout_ref[...], tn, preferred_element_type=jnp.float32)
-    xown = jnp.concatenate([own_ref[0], own_ref[1]], axis=0).astype(jnp.float32)
+    proj = jnp.dot(wout_ref[...], attended, preferred_element_type=jnp.float32)
+    xown = jnp.concatenate([own_ref[0], own_ref[1]], axis=1).astype(jnp.float32)
     hidden = (xown + proj).astype(jnp.bfloat16)
-    out_ref[0] = hidden[:block]
-    out_ref[1] = hidden[block:]
+    out_ref[0] = hidden[:, :block]
+    out_ref[1] = hidden[:, block:]
 
 
 def attend(valid, prev, own, nxt, w_qkv, w_out):
-    frames, points, chans = own.shape
+    frames, chans, points = own.shape
+    grid = (points // BLOCK,)
+    assert points % BLOCK == 0
+    cell_spec = pl.BlockSpec((frames, chans, BLOCK), lambda i: (0, 0, i))
+    full = lambda shape: pl.BlockSpec(shape, lambda i: (0, 0))
     w_qkv = w_qkv.T
-    grid = (points // BLOCK,)
-    cell_spec = pl.BlockSpec((frames, BLOCK, chans), lambda i: (0, i, 0))
-    full = lambda shape: pl.BlockSpec(shape, lambda i: (0, 0))
+    w_out = w_out.T
     return pl.pallas_call(
         attend_kernel,
         grid=grid,
@@ -117,9 +115,13 @@
     total = lax.axis_size("tm") * frames
     where_t = first + jnp.arange(6, dtype=jnp.int32) - 2
     valid = ((where_t >= 0) & (where_t < total)).astype(jnp.int32)
-    cells = lambda a: a.reshape(frames, points, chans)
+    cells = lambda a: a.reshape(frames, rows, cols, chans).transpose(0, 3, 1, 2).reshape(
+        frames, chans, points
+    )
     hidden = attend(valid, cells(x_prev), cells(latents), cells(x_next), w_qkv, w_out)
-    hid = hidden.reshape(frames, rows, merged)
+    hid = (
+        hidden.reshape(frames, chans, rows, cols).transpose(0, 2, 3, 1).reshape(frames, rows, merged)
+    )
 
     halo_top = shift(hid[:, rows - 1 :, :], "row", 1)
     halo_bot = shift(hid[:, :1, :], "row", -1)

time: 55 us -> 54.6 us (level)
  local copies, waits for them, and re-layouts: 9.3 us -> 11.3 us
  waiting for transfers between devices: 13.8 us -> 12.3 us
  Pallas kernels: 8.85 us -> 7.98 us
    ppermute x6, waiting for transfers between devices: 13.8 us -> 12.3 us  [shift(): return lax.ppermute(x, axis, pairs)]
    pallas_call x0 -> x1, local copies, waits for them, and re-layouts: none -> 1.44 us  [attend(): pl.pallas_call(attend_kernel, grid=grid, in_specs=[pl.BlockSpec(memory_sp...]
    pallas_call x1, Pallas kernels: 8.85 us -> 7.98 us  [attend(): pl.pallas_call(attend_kernel, grid=grid, in_specs=[pl.BlockSpec(memory_sp...]
    unnamed x5 -> x8, local copies, waits for them, and re-layouts: 1.18 us -> 2.04 us
    reshape x4 -> x7, local copies, waits for them, and re-layouts: 7.26 us -> 7 us  [the longest x6 6.38 us: body(): a.reshape(frames, rows, cols, chans).transpose(0, 3, 1, 2)]
  transfers between devices with their start and end apart: 6 -> 6, of which waited for: 4 -> 4; matrix products, arithmetic and copies ran while one was open for 12% -> 15% of each run, Pallas kernels for 0% -> 0%
where the time goes in v4:
time: 54.6 us; the launch traced here: 54.2 us
  starting transfers between devices  18.3 us (34%)
  waiting for transfers between devices  12.3 us (23%)
  local copies, waits for them, and re-layouts  11.3 us (21%)
  Pallas kernels  7.98 us (15%)
  other arithmetic  4.22 us (8%)
    ppermute x6, starting transfers between devices, shift(): return lax.ppermute(x, axis, pairs)  18.3 us
    ppermute x6, waiting for transfers between devices, shift(): return lax.ppermute(x, axis, pairs)  12.3 us
    pallas_call x1, Pallas kernels, attend(): pl.pallas_call(attend_kernel, grid=grid, in_specs=[pl.BlockSpec(memory_sp...  7.98 us
    reshape x6, local copies, waits for them, and re-layouts, body(): a.reshape(frames, rows, cols, chans).transpose(0, 3, 1, 2)  6.38 us
    convert_element_type x1, other arithmetic, body(): return acc.astype(jnp.bfloat16)  2.85 us
    unnamed x8, local copies, waits for them, and re-layouts  2.04 us
    pallas_call x1, local copies, waits for them, and re-layouts, attend(): pl.pallas_call(attend_kernel, grid=grid, in_specs=[pl.BlockSpec(memory_sp...  1.44 us
  transfers between devices with their start and end apart: 6, of which 4 were waited for; matrix products, arithmetic and copies ran while one was open for 15% of the time, Pallas kernels for 0%

profile of v4, /device:TPU:99, one launch (start us, length us, event | category | flops | bytes accessed | tf_op | source)
XLA Modules:
  0.0 54.2 jit_solution(3162238651839345805)
XLA Ops:
  0.0 5.3 %collective-permute-start = (bf16[2,32,5120]{2,1,0:T(8,128)(2,1)}, bf16[2,32,5120]{2,1,0:T(8,128)(2,1)S(1)}, u32[]{:S(2)}, u32[]{:S(2)}) collective-permute-start(bf16[2,32,5120]{2,1,0:T(8,128)(2,1)} %param.4), channel_id=1, source_target_pairs={{0,16},{16,32},{32,48},{48,64},{64,80},{80,96},{96,112},{112,128},... | collective-permute-start | bytes 1966088 | tf_op jit(solution)/shard_map/ppermute | solution.py:104
  5.3 1.9 %collective-permute-start.1 = (bf16[2,32,5120]{2,1,0:T(8,128)(2,1)}, bf16[2,32,5120]{2,1,0:T(8,128)(2,1)S(1)}, u32[]{:S(2)}, u32[]{:S(2)}) collective-permute-start(bf16[2,32,5120]{2,1,0:T(8,128)(2,1)} %param.4), channel_id=1, source_target_pairs={{16,0},{32,16},{48,32},{64,48},{80,64},{96,80},{112,96},{128,112},... | collective-permute-start | bytes 1966088 | tf_op jit(solution)/shard_map/ppermute | solution.py:104
  7.2 1.8 %reshape.74 = bf16[2,32,16,320]{3,2,1,0:T(8,128)(2,1)S(1)} reshape(bf16[2,32,5120]{2,1,0:T(8,128)(2,1)} %param.4) | data formatting | bytes 1310720 | tf_op jit(solution)/shard_map/reshape | solution.py:118
  9.0 0.0 copy-start
  9.0 1.1 %copy.14.own_ref = bf16[2,320,512]{2,1,0:T(8,128)(2,1)} copy(bf16[2,320,512]{1,2,0:T(8,128)(2,1)S(1)} %bitcast.16) | data formatting | bytes 1310720 | tf_op jit(solution)/shard_map/reshape | solution.py:118
  10.1 0.0 copy-done
  10.1 0.0 copy-start.1
  10.1 1.2 %copy.11 = bf16[320,960]{0,1:T(8,128)(2,1)} copy(bf16[320,960]{1,0:T(8,128)(2,1)S(1)} %copy-done) | data formatting | bytes 1228800 | tf_op args[1]
  11.3 0.0 copy-done.1
  11.3 0.9 %copy.12 = bf16[320,320]{0,1:T(8,128)(2,1)} copy(bf16[320,320]{1,0:T(8,128)(2,1)S(1)} %copy-done.1) | data formatting | bytes 409600 | tf_op args[2]
  12.2 0.5 and_convert_fusion.valid_ref
  12.7 0.5 collective-permute-done
  13.1 0.6 %reshape.72 = bf16[2,32,16,320]{3,2,1,0:T(8,128)(2,1)S(1)} reshape(bf16[2,32,5120]{2,1,0:T(8,128)(2,1)S(1)} %collective-permute-done) | data formatting | bytes 1310720 | tf_op jit(solution)/shard_map/reshape | solution.py:118
  13.8 1.1 %copy.13.prev_ref = bf16[2,320,512]{2,1,0:T(8,128)(2,1)} copy(bf16[2,320,512]{1,2,0:T(8,128)(2,1)S(1)} %bitcast.17) | data formatting | bytes 1310720 | tf_op jit(solution)/shard_map/reshape | solution.py:118
  14.9 3.8 %collective-permute-done.1 = bf16[2,32,5120]{2,1,0:T(8,128)(2,1)S(1)} collective-permute-done((bf16[2,32,5120]{2,1,0:T(8,128)(2,1)}, bf16[2,32,5120]{2,1,0:T(8,128)(2,1)S(1)}, u32[]{:S(2)}, u32[]{:S(2)}) %collective-permute-start.1) | collective-permute-done | bytes 655392 | tf_op jit(solution)/shard_map/ppermute | solution.py:104
  18.6 0.6 %reshape.76 = bf16[2,32,16,320]{3,2,1,0:T(8,128)(2,1)S(1)} reshape(bf16[2,32,5120]{2,1,0:T(8,128)(2,1)S(1)} %collective-permute-done.1) | data formatting | bytes 1310720 | tf_op jit(solution)/shard_map/reshape | solution.py:118
  19.3 1.1 %copy.15.next_ref = bf16[2,320,512]{2,1,0:T(8,128)(2,1)} copy(bf16[2,320,512]{1,2,0:T(8,128)(2,1)S(1)} %bitcast.18) | data formatting | bytes 1310720 | tf_op jit(solution)/shard_map/reshape | solution.py:118
  20.4 8.0 %shard_map.46 = bf16[2,320,512]{2,1,0:T(8,128)(2,1)} custom-call(s32[6]{0:T(128)} %and_convert_fusion.valid_ref, bf16[2,320,512]{2,1,0:T(8,128)(2,1)} %copy.13.prev_ref, bf16[2,320,512]{2,1,0:T(8,128)(2,1)} %copy.14.own_ref, bf16[2,320,512]{2,1,0:T(8,128)(2,1)} %copy.15.next_ref, bf16[960,320]{1,0:T(8,128)(2,1)} %bitcast.20, bf16[320,320]{1,0:T(8,128)(2,1)} %bitcast.21), custom_call_target="tpu_custom_call" | custom-call | tf_op jit(solution)/shard_map/pallas_call | solution.py:82
  28.4 1.4 %copy.16 = bf16[2,320,512]{1,2,0:T(8,128)(2,1)S(1)} copy(bf16[2,320,512]{2,1,0:T(8,128)(2,1)} %shard_map.46) | data formatting | bytes 1310720 | tf_op jit(solution)/shard_map/pallas_call | solution.py:82
  29.8 0.0 copy-start.2
  29.9 0.6 %reshape.79 = bf16[2,32,5120]{2,1,0:T(8,128)(2,1)S(1)} reshape(bf16[2,32,16,320]{3,2,1,0:T(8,128)(2,1)S(1)} %bitcast.19) | data formatting | bytes 1310720 | tf_op jit(solution)/shard_map/reshape | solution.py:123
  30.5 0.1 fusion.9
  30.6 3.7 %collective-permute-start.2 = (bf16[2,1,5120]{2,1,0:T(2,128)(2,1)S(1)}, bf16[2,1,5120]{2,1,0:T(2,128)(2,1)S(1)}, u32[]{:S(2)}, u32[]{:S(2)}) collective-permute-start(bf16[2,1,5120]{2,1,0:T(2,128)(2,1)S(1)} %get-tuple-element.18), channel_id=1, source_target_pairs={{0,8},{1,9},{2,10},{3,11},{4,12},{5,13},{6,14},{7,15},{16,24},{17,... | collective-permute-start | bytes 61448 | tf_op jit(solution)/shard_map/ppermute | solution.py:104
  34.3 1.3 %collective-permute-start.3 = (bf16[2,1,5120]{2,1,0:T(2,128)(2,1)S(1)}, bf16[2,1,5120]{2,1,0:T(2,128)(2,1)S(1)}, u32[]{:S(2)}, u32[]{:S(2)}) collective-permute-start(bf16[2,1,5120]{2,1,0:T(2,128)(2,1)S(1)} %get-tuple-element.19), channel_id=1, source_target_pairs={{8,0},{9,1},{10,2},{11,3},{12,4},{13,5},{14,6},{15,7},{24,16},{25,... | collective-permute-start | bytes 61448 | tf_op jit(solution)/shard_map/ppermute | solution.py:104
  35.6 0.0 collective-permute-done.2
  35.6 4.9 %collective-permute-done.3 = bf16[2,1,5120]{2,1,0:T(2,128)(2,1)S(1)} collective-permute-done((bf16[2,1,5120]{2,1,0:T(2,128)(2,1)S(1)}, bf16[2,1,5120]{2,1,0:T(2,128)(2,1)S(1)}, u32[]{:S(2)}, u32[]{:S(2)}) %collective-permute-start.3) | collective-permute-done | bytes 20512 | tf_op jit(solution)/shard_map/ppermute | solution.py:104
  40.6 0.1 pad_maximum_fusion.5
  40.7 4.1 %collective-permute-start.4 = (bf16[2,34,320]{2,1,0:T(8,128)(2,1)S(1)}, bf16[2,34,320]{2,1,0:T(8,128)(2,1)S(1)}, u32[]{:S(2)}, u32[]{:S(2)}) collective-permute-start(bf16[2,34,320]{2,1,0:T(8,128)(2,1)S(1)} %get-tuple-element.16), channel_id=1, source_target_pairs={{0,1},{1,2},{2,3},{3,4},{4,5},{5,6},{6,7},{8,9},{9,10},{10,11},{11... | collective-permute-start | bytes 130568 | tf_op jit(solution)/shard_map/ppermute | solution.py:104
  44.8 1.9 %collective-permute-start.5 = (bf16[2,34,320]{2,1,0:T(8,128)(2,1)S(1)}, bf16[2,34,320]{2,1,0:T(8,128)(2,1)S(1)}, u32[]{:S(2)}, u32[]{:S(2)}) collective-permute-start(bf16[2,34,320]{2,1,0:T(8,128)(2,1)S(1)} %get-tuple-element.17), channel_id=1, source_target_pairs={{1,0},{2,1},{3,2},{4,3},{5,4},{6,5},{7,6},{9,8},{10,9},{11,10},{12... | collective-permute-start | bytes 130568 | tf_op jit(solution)/shard_map/ppermute | solution.py:104
  46.7 0.0 copy-done.2
  46.7 0.1 slice_reduce_fusion.8
  46.8 0.1 tile.42
  46.9 0.1 tile.44
  46.9 0.1 tile.46
  47.0 0.1 tile.48
  47.1 0.1 tile.50
  47.2 0.1 tile.52
  47.3 0.1 tile.54
  47.4 0.1 tile.56
  47.4 0.1 tile.58
  47.5 0.0 collective-permute-done.4
  47.5 3.1 %collective-permute-done.5 = bf16[2,34,320]{2,1,0:T(8,128)(2,1)S(1)} collective-permute-done((bf16[2,34,320]{2,1,0:T(8,128)(2,1)S(1)}, bf16[2,34,320]{2,1,0:T(8,128)(2,1)S(1)}, u32[]{:S(2)}, u32[]{:S(2)}) %collective-permute-start.5) | collective-permute-done | bytes 43552 | tf_op jit(solution)/shard_map/ppermute | solution.py:104
  50.6 0.8 %maximum_maximum_fusion = (bf16[2,34,5440]{2,1,0:T(8,128)(2,1)S(1)}, bf16[2,34,5440]{2,1,0:T(8,128)(2,1)S(1)}) fusion(bf16[2,1,5120]{2,1,0:T(2,128)(2,1)S(1)} %collective-permute-done.3, bf16[2,32,5120]{2,1,0:T(8,128)(2,1)S(1)} %reshape.79, bf16[2,1,5120]{2,1,0:T(2,128)(2,1)S(1)} %collective-permute-done.2, ...), kind=kLoop, calls=%fused_computation.11 | loop fusion | flops 5918720 | bytes 2263040 | tf_op jit(solution)/shard_map/concatenate | solution.py:131
  51.4 2.8 %fusion.8 = bf16[2,32,5120]{2,1,0:T(8,128)(2,1)} fusion(bf16[2,32,5120]{2,1,0:T(8,128)(2,1)S(1)} %reshape.79, bf16[2,34,5440]{2,1,0:T(8,128)(2,1)S(1)} %get-tuple-element.15, bf16[2,1,5120]{2,1,0:T(2,128)(2,1)S(1)} %collective-permute-done.3, bf16[2,34,5440]{2,1,0:T(8,128)(2,1)S(1)} %get-tuple-element.14, bf16[2,1,5120]{2,1,0:T(2,128)(2,1)S(1)} %collective-permute-done.2, ...), kind=kLoop, calls=%fused_computation.10 | loop fusion | flops 11141120 | bytes 5468160 | tf_op jit(solution)/shard_map/convert_element_type | solution.py:143
  (9 shorter events, 0.0 us)
Async XLA Ops:
  0.0 13.1 %collective-permute-start = (bf16[2,32,5120]{2,1,0:T(8,128)(2,1)}, bf16[2,32,5120]{2,1,0:T(8,128)(2,1)S(1)}, u32[]{:S(2)}, u32[]{:S(2)}) collective-permute-start(bf16[2,32,5120]{2,1,0:T(8,128)(2,1)} %param.4), channel_id=1, source_target_pairs={{0,16},{16,32},{32,48},{48,64},{64,80},{80,96},{96,112},{112,128},... | collective-permute-start | bytes 1966088 | tf_op jit(solution)/shard_map/ppermute | solution.py:104
  5.3 13.3 %collective-permute-start.1 = (bf16[2,32,5120]{2,1,0:T(8,128)(2,1)}, bf16[2,32,5120]{2,1,0:T(8,128)(2,1)S(1)}, u32[]{:S(2)}, u32[]{:S(2)}) collective-permute-start(bf16[2,32,5120]{2,1,0:T(8,128)(2,1)} %param.4), channel_id=1, source_target_pairs={{16,0},{32,16},{48,32},{64,48},{80,64},{96,80},{112,96},{128,112},... | collective-permute-start | bytes 1966088 | tf_op jit(solution)/shard_map/ppermute | solution.py:104
  9.0 1.1 %copy-start = (bf16[320,960]{1,0:T(8,128)(2,1)S(1)}, bf16[320,960]{1,0:T(8,128)(2,1)}, u32[]{:S(2)}) copy-start(bf16[320,960]{1,0:T(8,128)(2,1)} %param.5) | copy-start | bytes 1843204
  10.1 1.2 %copy-start.1 = (bf16[320,320]{1,0:T(8,128)(2,1)S(1)}, bf16[320,320]{1,0:T(8,128)(2,1)}, u32[]{:S(2)}) copy-start(bf16[320,320]{1,0:T(8,128)(2,1)} %param.6) | copy-start | bytes 614404
  29.8 16.9 %copy-start.2 = (f32[9,320]{1,0:T(8,128)S(1)}, f32[9,320]{1,0:T(8,128)}, u32[]{:S(2)}) copy-start(f32[9,320]{1,0:T(8,128)} %param.7) | copy-start | bytes 34564
  30.6 5.1 %collective-permute-start.2 = (bf16[2,1,5120]{2,1,0:T(2,128)(2,1)S(1)}, bf16[2,1,5120]{2,1,0:T(2,128)(2,1)S(1)}, u32[]{:S(2)}, u32[]{:S(2)}) collective-permute-start(bf16[2,1,5120]{2,1,0:T(2,128)(2,1)S(1)} %get-tuple-element.18), channel_id=1, source_target_pairs={{0,8},{1,9},{2,10},{3,11},{4,12},{5,13},{6,14},{7,15},{16,24},{17,... | collective-permute-start | bytes 61448 | tf_op jit(solution)/shard_map/ppermute | solution.py:104
  34.3 6.3 %collective-permute-start.3 = (bf16[2,1,5120]{2,1,0:T(2,128)(2,1)S(1)}, bf16[2,1,5120]{2,1,0:T(2,128)(2,1)S(1)}, u32[]{:S(2)}, u32[]{:S(2)}) collective-permute-start(bf16[2,1,5120]{2,1,0:T(2,128)(2,1)S(1)} %get-tuple-element.19), channel_id=1, source_target_pairs={{8,0},{9,1},{10,2},{11,3},{12,4},{13,5},{14,6},{15,7},{24,16},{25,... | collective-permute-start | bytes 61448 | tf_op jit(solution)/shard_map/ppermute | solution.py:104
  40.7 6.8 %collective-permute-start.4 = (bf16[2,34,320]{2,1,0:T(8,128)(2,1)S(1)}, bf16[2,34,320]{2,1,0:T(8,128)(2,1)S(1)}, u32[]{:S(2)}, u32[]{:S(2)}) collective-permute-start(bf16[2,34,320]{2,1,0:T(8,128)(2,1)S(1)} %get-tuple-element.16), channel_id=1, source_target_pairs={{0,1},{1,2},{2,3},{3,4},{4,5},{5,6},{6,7},{8,9},{9,10},{10,11},{11... | collective-permute-start | bytes 130568 | tf_op jit(solution)/shard_map/ppermute | solution.py:104
  44.8 5.9 %collective-permute-start.5 = (bf16[2,34,320]{2,1,0:T(8,128)(2,1)S(1)}, bf16[2,34,320]{2,1,0:T(8,128)(2,1)S(1)}, u32[]{:S(2)}, u32[]{:S(2)}) collective-permute-start(bf16[2,34,320]{2,1,0:T(8,128)(2,1)S(1)} %get-tuple-element.17), channel_id=1, source_target_pairs={{1,0},{2,1},{3,2},{4,3},{5,4},{6,5},{7,6},{9,8},{10,9},{11,10},{12... | collective-permute-start | bytes 130568 | tf_op jit(solution)/shard_map/ppermute | solution.py:104

commit v5 on v4

--- a/solution.py
+++ b/solution.py
@@ -104,13 +104,37 @@
     return lax.ppermute(x, axis, pairs)
 
 
+def swap(send_even, send_odd, axis, offset):
+    count = lax.axis_size(axis)
+    pairs = []
+    for i in range(offset, count - 1, 2):
+        pairs += [(i, i + 1), (i + 1, i)]
+    even = lax.axis_index(axis) % 2 == 0
+    if offset:
+        payload = jnp.where(even, send_odd, send_even)
+    else:
+        payload = jnp.where(even, send_even, send_odd)
+    return lax.ppermute(payload, axis, pairs)
+
+
+def exchange(to_next, to_prev, axis):
+    even = lax.axis_index(axis) % 2 == 0
+    got_a = swap(to_next, to_prev, axis, 0)
+    if lax.axis_size(axis) <= 2:
+        zero = jnp.zeros_like(got_a)
+        return jnp.where(even, zero, got_a), jnp.where(even, got_a, zero)
+    got_b = swap(to_next, to_prev, axis, 1)
+    from_prev = jnp.where(even, got_b, got_a)
+    from_next = jnp.where(even, got_a, got_b)
+    return from_prev, from_next
+
+
 def body(latents, w_qkv, w_out, conv_weight):
     frames, rows, merged = latents.shape
     chans = w_out.shape[0]
     cols = merged // chans
     points = rows * cols
-    x_prev = shift(latents, "tm", 1)
-    x_next = shift(latents, "tm", -1)
+    x_prev, x_next = exchange(latents, latents, "tm")
     first = lax.axis_index("tm") * frames
     total = lax.axis_size("tm") * frames
     where_t = first + jnp.arange(6, dtype=jnp.int32) - 2
@@ -123,11 +147,9 @@
         hidden.reshape(frames, chans, rows, cols).transpose(0, 2, 3, 1).reshape(frames, rows, merged)
     )
 
-    halo_top = shift(hid[:, rows - 1 :, :], "row", 1)
-    halo_bot = shift(hid[:, :1, :], "row", -1)
+    halo_top, halo_bot = exchange(hid[:, rows - 1 :, :], hid[:, :1, :], "row")
     tall = jnp.concatenate([halo_top, hid, halo_bot], axis=1)
-    halo_left = shift(tall[:, :, merged - chans :], "col", 1)
-    halo_right = shift(tall[:, :, :chans], "col", -1)
+    halo_left, halo_right = exchange(tall[:, :, merged - chans :], tall[:, :, :chans], "col")
     padded = jnp.concatenate([halo_left, tall, halo_right], axis=2)
     taps = jnp.tile(conv_weight, (1, cols))
     acc = hid.astype(jnp.float32)

time: 54.6 us -> 45.3 us (0.83)
  the two profiles are of different devices: /device:TPU:99 before, /device:TPU:152 now
where the time goes in v5:
time: 45.3 us; the launch traced here: 45.1 us
  local copies, waits for them, and re-layouts  11.3 us (25%)
  waiting for transfers between devices  10.8 us (24%)
  starting transfers between devices  10.4 us (23%)
  Pallas kernels  7.98 us (18%)
  other arithmetic  4.48 us (10%)
    ppermute x5, waiting for transfers between devices, swap(): return lax.ppermute(payload, axis, pairs)  10.8 us
    ppermute x5, starting transfers between devices, swap(): return lax.ppermute(payload, axis, pairs)  10.4 us
    pallas_call x1, Pallas kernels, attend(): pl.pallas_call(attend_kernel, grid=grid, in_specs=[pl.BlockSpec(memory_sp...  7.98 us
    reshape x6, local copies, waits for them, and re-layouts, body(): a.reshape(frames, rows, cols, chans).transpose(0, 3, 1, 2)  6.37 us
    convert_element_type x1, other arithmetic, body(): return acc.astype(jnp.bfloat16)  2.85 us
    unnamed x8, local copies, waits for them, and re-layouts  2.04 us
    pallas_call x1, local copies, waits for them, and re-layouts, attend(): pl.pallas_call(attend_kernel, grid=grid, in_specs=[pl.BlockSpec(memory_sp...  1.44 us
  transfers between devices with their start and end apart: 5, of which 3 were waited for; matrix products, arithmetic and copies ran while one was open for 14% of the time, Pallas kernels for 0%

profile of v5, /device:TPU:152, one launch (start us, length us, event | category | flops | bytes accessed | tf_op | source)
XLA Modules:
  0.0 45.1 jit_solution(5546561333116548232)
XLA Ops:
  0.0 1.9 %collective-permute-start = (bf16[2,32,5120]{2,1,0:T(8,128)(2,1)}, bf16[2,32,5120]{2,1,0:T(8,128)(2,1)S(1)}, u32[]{:S(2)}, u32[]{:S(2)}) collective-permute-start(bf16[2,32,5120]{2,1,0:T(8,128)(2,1)} %param.4), channel_id=1, source_target_pairs={{16,32},{32,16},{48,64},{64,48},{80,96},{96,80},{112,128},{128,112... | collective-permute-start | bytes 1966088 | tf_op jit(solution)/shard_map/ppermute | solution.py:117
  1.9 1.2 %collective-permute-start.1 = (bf16[2,32,5120]{2,1,0:T(8,128)(2,1)}, bf16[2,32,5120]{2,1,0:T(8,128)(2,1)S(1)}, u32[]{:S(2)}, u32[]{:S(2)}) collective-permute-start(bf16[2,32,5120]{2,1,0:T(8,128)(2,1)} %param.4), channel_id=1, source_target_pairs={{0,16},{16,0},{32,48},{48,32},{64,80},{80,64},{96,112},{112,96},{1... | collective-permute-start | bytes 1966088 | tf_op jit(solution)/shard_map/ppermute | solution.py:117
  3.1 1.8 %reshape.74 = bf16[2,32,16,320]{3,2,1,0:T(8,128)(2,1)S(1)} reshape(bf16[2,32,5120]{2,1,0:T(8,128)(2,1)} %param.4) | data formatting | bytes 1310720 | tf_op jit(solution)/shard_map/reshape | solution.py:142
  4.9 0.0 copy-start
  4.9 1.1 %copy.14.own_ref = bf16[2,320,512]{2,1,0:T(8,128)(2,1)} copy(bf16[2,320,512]{1,2,0:T(8,128)(2,1)S(1)} %bitcast.16) | data formatting | bytes 1310720 | tf_op jit(solution)/shard_map/reshape | solution.py:142
  6.0 0.0 copy-done
  6.0 0.0 copy-start.1
  6.0 1.2 %copy.11 = bf16[320,960]{0,1:T(8,128)(2,1)} copy(bf16[320,960]{1,0:T(8,128)(2,1)S(1)} %copy-done) | data formatting | bytes 1228800 | tf_op args[1]
  7.2 0.0 copy-done.1
  7.2 0.9 %copy.12 = bf16[320,320]{0,1:T(8,128)(2,1)} copy(bf16[320,320]{1,0:T(8,128)(2,1)S(1)} %copy-done.1) | data formatting | bytes 409600 | tf_op args[2]
  8.1 0.5 %and_convert_fusion.valid_ref = s32[6]{0:T(128)} fusion(s32[]{:T(128)S(6)} %mul.75), kind=kLoop, calls=%fused_computation.27 | loop fusion | flops 36 | bytes 28 | tf_op jit(solution)/shard_map/convert_element_type | solution.py:141
  8.6 4.7 %collective-permute-done = bf16[2,32,5120]{2,1,0:T(8,128)(2,1)S(1)} collective-permute-done((bf16[2,32,5120]{2,1,0:T(8,128)(2,1)}, bf16[2,32,5120]{2,1,0:T(8,128)(2,1)S(1)}, u32[]{:S(2)}, u32[]{:S(2)}) %collective-permute-start) | collective-permute-done | bytes 655392 | tf_op jit(solution)/shard_map/ppermute | solution.py:117
  13.3 0.0 collective-permute-done.1
  13.3 0.1 broadcast_select_fusion
  13.4 0.6 %reshape.72 = bf16[2,32,16,320]{3,2,1,0:T(8,128)(2,1)S(1)} reshape(bf16[2,32,5120]{2,1,0:T(8,128)(2,1)S(1)} %get-tuple-element.18) | data formatting | bytes 1310720 | tf_op jit(solution)/shard_map/reshape | solution.py:142
  14.0 1.1 %copy.13.prev_ref = bf16[2,320,512]{2,1,0:T(8,128)(2,1)} copy(bf16[2,320,512]{1,2,0:T(8,128)(2,1)S(1)} %bitcast.17) | data formatting | bytes 1310720 | tf_op jit(solution)/shard_map/reshape | solution.py:142
  15.2 0.6 %reshape.76 = bf16[2,32,16,320]{3,2,1,0:T(8,128)(2,1)S(1)} reshape(bf16[2,32,5120]{2,1,0:T(8,128)(2,1)S(1)} %get-tuple-element.17) | data formatting | bytes 1310720 | tf_op jit(solution)/shard_map/reshape | solution.py:142
  15.8 1.1 %copy.15.next_ref = bf16[2,320,512]{2,1,0:T(8,128)(2,1)} copy(bf16[2,320,512]{1,2,0:T(8,128)(2,1)S(1)} %bitcast.18) | data formatting | bytes 1310720 | tf_op jit(solution)/shard_map/reshape | solution.py:142
  16.9 8.0 %shard_map.46 = bf16[2,320,512]{2,1,0:T(8,128)(2,1)} custom-call(s32[6]{0:T(128)} %and_convert_fusion.valid_ref, bf16[2,320,512]{2,1,0:T(8,128)(2,1)} %copy.13.prev_ref, bf16[2,320,512]{2,1,0:T(8,128)(2,1)} %copy.14.own_ref, bf16[2,320,512]{2,1,0:T(8,128)(2,1)} %copy.15.next_ref, bf16[960,320]{1,0:T(8,128)(2,1)} %bitcast.20, bf16[320,320]{1,0:T(8,128)(2,1)} %bitcast.21), custom_call_target="tpu_custom_call" | custom-call | tf_op jit(solution)/shard_map/pallas_call | solution.py:82
  24.9 1.4 %copy.16 = bf16[2,320,512]{1,2,0:T(8,128)(2,1)S(1)} copy(bf16[2,320,512]{2,1,0:T(8,128)(2,1)} %shard_map.46) | data formatting | bytes 1310720 | tf_op jit(solution)/shard_map/pallas_call | solution.py:82
  26.4 0.6 %reshape.79 = bf16[2,32,5120]{2,1,0:T(8,128)(2,1)S(1)} reshape(bf16[2,32,16,320]{3,2,1,0:T(8,128)(2,1)S(1)} %bitcast.19) | data formatting | bytes 1310720 | tf_op jit(solution)/shard_map/reshape | solution.py:147
  27.0 0.0 copy-start.2
  27.0 0.1 broadcast_select_fusion.4
  27.1 3.1 %collective-permute-start.2 = (bf16[2,1,5120]{2,1,0:T(2,128)(2,1)S(1)}, bf16[2,1,5120]{2,1,0:T(2,128)(2,1)S(1)}, u32[]{:S(2)}, u32[]{:S(2)}) collective-permute-start(bf16[2,1,5120]{2,1,0:T(2,128)(2,1)S(1)} %broadcast_select_fusion.4), channel_id=1, source_target_pairs={{0,8},{8,0},{1,9},{9,1},{2,10},{10,2},{3,11},{11,3},{4,12},{12,4},... | collective-permute-start | bytes 61448 | tf_op jit(solution)/shard_map/ppermute | solution.py:117
  30.2 2.5 %collective-permute-done.2 = bf16[2,1,5120]{2,1,0:T(2,128)(2,1)S(1)} collective-permute-done((bf16[2,1,5120]{2,1,0:T(2,128)(2,1)S(1)}, bf16[2,1,5120]{2,1,0:T(2,128)(2,1)S(1)}, u32[]{:S(2)}, u32[]{:S(2)}) %collective-permute-start.2) | collective-permute-done | bytes 20512 | tf_op jit(solution)/shard_map/ppermute | solution.py:117
  32.7 0.1 broadcast_select_fusion.3
  32.8 0.1 broadcast_select_fusion.8
  32.9 1.6 %collective-permute-start.4 = (bf16[2,34,320]{2,1,0:T(8,128)(2,1)S(1)}, bf16[2,34,320]{2,1,0:T(8,128)(2,1)S(1)}, u32[]{:S(2)}, u32[]{:S(2)}) collective-permute-start(bf16[2,34,320]{2,1,0:T(8,128)(2,1)S(1)} %broadcast_select_fusion.7), channel_id=1, source_target_pairs={{0,1},{1,0},{2,3},{3,2},{4,5},{5,4},{6,7},{7,6},{8,9},{9,8},{10,11... | collective-permute-start | bytes 130568 | tf_op jit(solution)/shard_map/ppermute | solution.py:117
  34.5 2.6 %collective-permute-start.3 = (bf16[2,34,320]{2,1,0:T(8,128)(2,1)S(1)}, bf16[2,34,320]{2,1,0:T(8,128)(2,1)S(1)}, u32[]{:S(2)}, u32[]{:S(2)}) collective-permute-start(bf16[2,34,320]{2,1,0:T(8,128)(2,1)S(1)} %get-tuple-element.14), channel_id=1, source_target_pairs={{1,2},{2,1},{3,4},{4,3},{5,6},{6,5},{9,10},{10,9},{11,12},{12,11},... | collective-permute-start | bytes 130568 | tf_op jit(solution)/shard_map/ppermute | solution.py:117
  37.1 0.0 copy-done.2
  37.1 0.1 slice_reduce_fusion.8
  37.2 0.1 tile.42
  37.2 0.1 tile.44
  37.3 0.1 tile.46
  37.4 0.1 tile.48
  37.5 0.1 tile.50
  37.6 0.1 tile.52
  37.7 0.1 tile.54
  37.7 0.1 tile.56
  37.8 0.1 tile.58
  37.9 0.0 collective-permute-done.4
  37.9 3.6 %collective-permute-done.3 = bf16[2,34,320]{2,1,0:T(8,128)(2,1)S(1)} collective-permute-done((bf16[2,34,320]{2,1,0:T(8,128)(2,1)S(1)}, bf16[2,34,320]{2,1,0:T(8,128)(2,1)S(1)}, u32[]{:S(2)}, u32[]{:S(2)}) %collective-permute-start.3) | collective-permute-done | bytes 43552 | tf_op jit(solution)/shard_map/ppermute | solution.py:117
  41.5 0.8 %maximum_maximum_fusion = (bf16[2,34,5440]{2,1,0:T(8,128)(2,1)S(1)}, bf16[2,34,5440]{2,1,0:T(8,128)(2,1)S(1)}) fusion(bf16[2,1,5120]{2,1,0:T(2,128)(2,1)S(1)} %get-tuple-element.24, bf16[2,32,5120]{2,1,0:T(8,128)(2,1)S(1)} %reshape.79, bf16[2,1,5120]{2,1,0:T(2,128)(2,1)S(1)} %get-tuple-element.23, bf16[2,34,320]{2,1,0:T(8,128)(2,1)S(1)} %get-tuple-element.21, ...), kind=kLoop, calls=%fused_computation.11 | loop fusion | flops 5918720 | bytes 2263040 | tf_op jit(solution)/shard_map/concatenate | solution.py:153
  42.2 2.8 %fusion.8 = bf16[2,32,5120]{2,1,0:T(8,128)(2,1)} fusion(bf16[2,32,5120]{2,1,0:T(8,128)(2,1)S(1)} %reshape.79, bf16[2,34,5440]{2,1,0:T(8,128)(2,1)S(1)} %get-tuple-element.20, bf16[2,1,5120]{2,1,0:T(2,128)(2,1)S(1)} %get-tuple-element.24, bf16[2,34,5440]{2,1,0:T(8,128)(2,1)S(1)} %get-tuple-element.19, bf16[2,1,5120]{2,1,0:T(2,128)(2,1)S(1)} %get-tuple-element.23, ...), kind=kLoop, calls=%fused_computation.10 | loop fusion | flops 11141120 | bytes 5468160 | tf_op jit(solution)/shard_map/convert_element_type | solution.py:165
  (11 shorter events, 0.1 us)
Async XLA Ops:
  0.0 13.3 %collective-permute-start = (bf16[2,32,5120]{2,1,0:T(8,128)(2,1)}, bf16[2,32,5120]{2,1,0:T(8,128)(2,1)S(1)}, u32[]{:S(2)}, u32[]{:S(2)}) collective-permute-start(bf16[2,32,5120]{2,1,0:T(8,128)(2,1)} %param.4), channel_id=1, source_target_pairs={{16,32},{32,16},{48,64},{64,48},{80,96},{96,80},{112,128},{128,112... | collective-permute-start | bytes 1966088 | tf_op jit(solution)/shard_map/ppermute | solution.py:117
  1.9 11.4 %collective-permute-start.1 = (bf16[2,32,5120]{2,1,0:T(8,128)(2,1)}, bf16[2,32,5120]{2,1,0:T(8,128)(2,1)S(1)}, u32[]{:S(2)}, u32[]{:S(2)}) collective-permute-start(bf16[2,32,5120]{2,1,0:T(8,128)(2,1)} %param.4), channel_id=1, source_target_pairs={{0,16},{16,0},{32,48},{48,32},{64,80},{80,64},{96,112},{112,96},{1... | collective-permute-start | bytes 1966088 | tf_op jit(solution)/shard_map/ppermute | solution.py:117
  4.9 1.1 %copy-start = (bf16[320,960]{1,0:T(8,128)(2,1)S(1)}, bf16[320,960]{1,0:T(8,128)(2,1)}, u32[]{:S(2)}) copy-start(bf16[320,960]{1,0:T(8,128)(2,1)} %param.5) | copy-start | bytes 1843204
  6.0 1.2 %copy-start.1 = (bf16[320,320]{1,0:T(8,128)(2,1)S(1)}, bf16[320,320]{1,0:T(8,128)(2,1)}, u32[]{:S(2)}) copy-start(bf16[320,320]{1,0:T(8,128)(2,1)} %param.6) | copy-start | bytes 614404
  27.0 10.1 %copy-start.2 = (f32[9,320]{1,0:T(8,128)S(1)}, f32[9,320]{1,0:T(8,128)}, u32[]{:S(2)}) copy-start(f32[9,320]{1,0:T(8,128)} %param.7) | copy-start | bytes 34564
  27.1 5.6 %collective-permute-start.2 = (bf16[2,1,5120]{2,1,0:T(2,128)(2,1)S(1)}, bf16[2,1,5120]{2,1,0:T(2,128)(2,1)S(1)}, u32[]{:S(2)}, u32[]{:S(2)}) collective-permute-start(bf16[2,1,5120]{2,1,0:T(2,128)(2,1)S(1)} %broadcast_select_fusion.4), channel_id=1, source_target_pairs={{0,8},{8,0},{1,9},{9,1},{2,10},{10,2},{3,11},{11,3},{4,12},{12,4},... | collective-permute-start | bytes 61448 | tf_op jit(solution)/shard_map/ppermute | solution.py:117
  32.9 5.0 %collective-permute-start.4 = (bf16[2,34,320]{2,1,0:T(8,128)(2,1)S(1)}, bf16[2,34,320]{2,1,0:T(8,128)(2,1)S(1)}, u32[]{:S(2)}, u32[]{:S(2)}) collective-permute-start(bf16[2,34,320]{2,1,0:T(8,128)(2,1)S(1)} %broadcast_select_fusion.7), channel_id=1, source_target_pairs={{0,1},{1,0},{2,3},{3,2},{4,5},{5,4},{6,7},{7,6},{8,9},{9,8},{10,11... | collective-permute-start | bytes 130568 | tf_op jit(solution)/shard_map/ppermute | solution.py:117
  34.5 7.0 %collective-permute-start.3 = (bf16[2,34,320]{2,1,0:T(8,128)(2,1)S(1)}, bf16[2,34,320]{2,1,0:T(8,128)(2,1)S(1)}, u32[]{:S(2)}, u32[]{:S(2)}) collective-permute-start(bf16[2,34,320]{2,1,0:T(8,128)(2,1)S(1)} %get-tuple-element.14), channel_id=1, source_target_pairs={{1,2},{2,1},{3,4},{4,3},{5,6},{6,5},{9,10},{10,9},{11,12},{12,11},... | collective-permute-start | bytes 130568 | tf_op jit(solution)/shard_map/ppermute | solution.py:117

commit v6 on v5

--- a/solution.py
+++ b/solution.py
@@ -8,7 +8,7 @@
 from jax.sharding import PartitionSpec as P
 
 HEAD_DIM = 64
-BLOCK = 128
+BLOCK = 512
 
 
 def layer_norm_t(cols):
@@ -117,6 +117,19 @@
     return lax.ppermute(payload, axis, pairs)
 
 
+def diag_swap(to_right, to_left, offset):
+    rows = lax.axis_size("row")
+    cols = lax.axis_size("col")
+    pairs = []
+    for c in range(offset, cols - 1, 2):
+        for r in range(rows):
+            pairs += [(r * cols + c, (rows - 1 - r) * cols + c + 1)]
+            pairs += [((rows - 1 - r) * cols + c + 1, r * cols + c)]
+    left_member = lax.axis_index("col") % 2 == offset
+    payload = jnp.where(left_member, to_right, to_left)
+    return lax.ppermute(payload, ("row", "col"), pairs)
+
+
 def exchange(to_next, to_prev, axis):
     even = lax.axis_index(axis) % 2 == 0
     got_a = swap(to_next, to_prev, axis, 0)
@@ -147,10 +160,31 @@
         hidden.reshape(frames, chans, rows, cols).transpose(0, 2, 3, 1).reshape(frames, rows, merged)
     )
 
-    halo_top, halo_bot = exchange(hid[:, rows - 1 :, :], hid[:, :1, :], "row")
-    tall = jnp.concatenate([halo_top, hid, halo_bot], axis=1)
-    halo_left, halo_right = exchange(tall[:, :, merged - chans :], tall[:, :, :chans], "col")
-    padded = jnp.concatenate([halo_left, tall, halo_right], axis=2)
+    bot_row = hid[:, rows - 1 :, :]
+    top_row = hid[:, :1, :]
+    halo_top, halo_bot = exchange(bot_row, top_row, "row")
+    halo_left, halo_right = exchange(hid[:, :, merged - chans :], hid[:, :, :chans], "col")
+    upper = lax.axis_index("row") == 0
+    to_right = jnp.where(upper, bot_row[:, :, merged - chans :], top_row[:, :, merged - chans :])
+    to_left = jnp.where(upper, bot_row[:, :, :chans], top_row[:, :, :chans])
+    got_a = diag_swap(to_right, to_left, 0)
+    got_b = diag_swap(to_right, to_left, 1)
+    even = lax.axis_index("col") % 2 == 0
+    from_right = jnp.where(even, got_a, got_b)
+    from_left = jnp.where(even, got_b, got_a)
+    zero = jnp.zeros_like(from_left)
+    c_tl = jnp.where(upper, zero, from_left)
+    c_bl = jnp.where(upper, from_left, zero)
+    c_tr = jnp.where(upper, zero, from_right)
+    c_br = jnp.where(upper, from_right, zero)
+    padded = jnp.concatenate(
+        [
+            jnp.concatenate([c_tl, halo_top, c_tr], axis=2),
+            jnp.concatenate([halo_left, hid, halo_right], axis=2),
+            jnp.concatenate([c_bl, halo_bot, c_br], axis=2),
+        ],
+        axis=1,
+    )
     taps = jnp.tile(conv_weight, (1, cols))
     acc = hid.astype(jnp.float32)
     for tap_a in range(3):

time: 45.3 us -> 47.8 us (1.055); the launches traced: 45.1 us -> 46.8 us
  waiting for transfers between devices: 10.8 us -> 6.13 us
  starting transfers between devices: 10.4 us -> 14.3 us
  local copies, waits for them, and re-layouts: 11.3 us -> 13.7 us
  Pallas kernels: 7.98 us -> 6.78 us
  other arithmetic: 4.48 us -> 5.68 us
    ppermute x0 -> x2, starting transfers between devices: none -> 4.95 us  [diag_swap(): return lax.ppermute(payload, ('row', 'col'), pairs)]
    ppermute x5, waiting for transfers between devices: 10.8 us -> 6.12 us  [swap(): return lax.ppermute(payload, axis, pairs)]
    convert_element_type x1, other arithmetic: 2.85 us -> 4.66 us  [body(): return acc.astype(jnp.bfloat16)]
    concatenate x0 -> x3, local copies, waits for them, and re-layouts: none -> 1.25 us  [the longest x1 0.78 us: body(): jnp.concatenate([halo_left, hid, halo_right], axis=2)]
    pallas_call x1, Pallas kernels: 7.98 us -> 6.78 us  [attend(): pl.pallas_call(attend_kernel, grid=grid, in_specs=[pl.BlockSpec(memory_sp...]
    another operation x18, local copies, waits for them, and re-layouts: 0.74 us -> 1.93 us  [body(): taps = jnp.tile(conv_weight, (1, cols))]
    ppermute x5, starting transfers between devices: 10.4 us -> 9.33 us  [swap(): return lax.ppermute(payload, axis, pairs)]
    concatenate x1 -> x0, other arithmetic: 0.75 us -> none  [body(): padded = jnp.concatenate([halo_left, tall, halo_right], axis=2)]
  transfers between devices with their start and end apart: 5 -> 7, of which waited for: 3 -> 3; matrix products, arithmetic and copies ran while one was open for 14% -> 17% of each run, Pallas kernels for 0% -> 0%
where the time goes in v6:
time: 47.8 us; the launch traced here: 46.8 us
  starting transfers between devices  14.3 us (30%)
  local copies, waits for them, and re-layouts  13.7 us (29%)
  Pallas kernels  6.78 us (14%)
  waiting for transfers between devices  6.13 us (13%)
  other arithmetic  5.68 us (12%)
    ppermute x5, starting transfers between devices, swap(): return lax.ppermute(payload, axis, pairs)  9.33 us
    pallas_call x1, Pallas kernels, attend(): pl.pallas_call(attend_kernel, grid=grid, in_specs=[pl.BlockSpec(memory_sp...  6.78 us
    reshape x6, local copies, waits for them, and re-layouts, body(): a.reshape(frames, rows, cols, chans).transpose(0, 3, 1, 2)  6.37 us
    ppermute x5, waiting for transfers between devices, swap(): return lax.ppermute(payload, axis, pairs)  6.12 us
    ppermute x2, starting transfers between devices, diag_swap(): return lax.ppermute(payload, ('row', 'col'), pairs)  4.95 us
    convert_element_type x1, other arithmetic, body(): return acc.astype(jnp.bfloat16)  4.66 us
    unnamed x12, local copies, waits for them, and re-layouts  2.04 us
    another operation x18, local copies, waits for them, and re-layouts, body(): taps = jnp.tile(conv_weight, (1, cols))  1.93 us
  transfers between devices with their start and end apart: 7, of which 3 were waited for; matrix products, arithmetic and copies ran while one was open for 17% of the time, Pallas kernels for 0%

profile of v6, /device:TPU:152, one launch (start us, length us, event | category | flops | bytes accessed | tf_op | source)
XLA Modules:
  0.0 46.8 jit_solution(11546454437628931203)
XLA Ops:
  0.0 1.9 %collective-permute-start = (bf16[2,32,5120]{2,1,0:T(8,128)(2,1)}, bf16[2,32,5120]{2,1,0:T(8,128)(2,1)S(1)}, u32[]{:S(2)}, u32[]{:S(2)}) collective-permute-start(bf16[2,32,5120]{2,1,0:T(8,128)(2,1)} %param.4), channel_id=1, source_target_pairs={{16,32},{32,16},{48,64},{64,48},{80,96},{96,80},{112,128},{128,112... | collective-permute-start | bytes 1966088 | tf_op jit(solution)/shard_map/ppermute | solution.py:117
  1.9 1.2 %collective-permute-start.1 = (bf16[2,32,5120]{2,1,0:T(8,128)(2,1)}, bf16[2,32,5120]{2,1,0:T(8,128)(2,1)S(1)}, u32[]{:S(2)}, u32[]{:S(2)}) collective-permute-start(bf16[2,32,5120]{2,1,0:T(8,128)(2,1)} %param.4), channel_id=1, source_target_pairs={{0,16},{16,0},{32,48},{48,32},{64,80},{80,64},{96,112},{112,96},{1... | collective-permute-start | bytes 1966088 | tf_op jit(solution)/shard_map/ppermute | solution.py:117
  3.1 1.8 %reshape.74 = bf16[2,32,16,320]{3,2,1,0:T(8,128)(2,1)S(1)} reshape(bf16[2,32,5120]{2,1,0:T(8,128)(2,1)} %param.4) | data formatting | bytes 1310720 | tf_op jit(solution)/shard_map/reshape | solution.py:155
  4.9 0.0 copy-start
  4.9 1.1 %copy.14.own_ref = bf16[2,320,512]{2,1,0:T(8,128)(2,1)} copy(bf16[2,320,512]{1,2,0:T(8,128)(2,1)S(1)} %bitcast.16) | data formatting | bytes 1310720 | tf_op jit(solution)/shard_map/reshape | solution.py:155
  6.1 1.2 %copy.11 = bf16[320,960]{0,1:T(8,128)(2,1)} copy(bf16[320,960]{1,0:T(8,128)(2,1)S(1)} %copy-done) | data formatting | bytes 1228800 | tf_op args[1]
  7.2 0.9 %copy.12 = bf16[320,320]{0,1:T(8,128)(2,1)} copy(bf16[320,320]{1,0:T(8,128)(2,1)S(1)} %copy-done.1) | data formatting | bytes 409600 | tf_op args[2]
  8.1 0.0 copy-done.4
  8.1 0.1 slice_reduce_fusion.8
  8.1 0.1 tile.42
  8.2 0.1 tile.44
  8.3 0.1 tile.46
  8.4 0.1 tile.48
  8.5 0.1 tile.50
  8.6 0.1 tile.52
  8.6 0.1 tile.54
  8.7 0.7 %tile.56 = f32[5120]{0:T(1024)} reshape(f32[16,320]{1,0:T(8,128)S(1)} %tile.55) | data formatting | bytes 40960 | tf_op jit(solution)/shard_map/tile | solution.py:188
  9.4 0.7 %tile.58 = f32[5120]{0:T(1024)} reshape(f32[16,320]{1,0:T(8,128)S(1)} %tile.57) | data formatting | bytes 40960 | tf_op jit(solution)/shard_map/tile | solution.py:188
  10.1 0.6 %and_convert_fusion.valid_ref = s32[6]{0:T(128)} fusion(s32[]{:T(128)S(6)} %mul.75), kind=kLoop, calls=%fused_computation.46 | loop fusion | flops 36 | bytes 28 | tf_op jit(solution)/shard_map/convert_element_type | solution.py:154
  10.7 2.7 %collective-permute-done = bf16[2,32,5120]{2,1,0:T(8,128)(2,1)S(1)} collective-permute-done((bf16[2,32,5120]{2,1,0:T(8,128)(2,1)}, bf16[2,32,5120]{2,1,0:T(8,128)(2,1)S(1)}, u32[]{:S(2)}, u32[]{:S(2)}) %collective-permute-start) | collective-permute-done | bytes 655392 | tf_op jit(solution)/shard_map/ppermute | solution.py:117
  13.3 0.0 collective-permute-done.1
  13.3 0.1 broadcast_select_fusion
  13.4 0.6 %reshape.72 = bf16[2,32,16,320]{3,2,1,0:T(8,128)(2,1)S(1)} reshape(bf16[2,32,5120]{2,1,0:T(8,128)(2,1)S(1)} %get-tuple-element.15) | data formatting | bytes 1310720 | tf_op jit(solution)/shard_map/reshape | solution.py:155
  14.0 1.1 %copy.13.prev_ref = bf16[2,320,512]{2,1,0:T(8,128)(2,1)} copy(bf16[2,320,512]{1,2,0:T(8,128)(2,1)S(1)} %bitcast.17) | data formatting | bytes 1310720 | tf_op jit(solution)/shard_map/reshape | solution.py:155
  15.2 0.6 %reshape.76 = bf16[2,32,16,320]{3,2,1,0:T(8,128)(2,1)S(1)} reshape(bf16[2,32,5120]{2,1,0:T(8,128)(2,1)S(1)} %get-tuple-element.14) | data formatting | bytes 1310720 | tf_op jit(solution)/shard_map/reshape | solution.py:155
  15.8 1.1 %copy.15.next_ref = bf16[2,320,512]{2,1,0:T(8,128)(2,1)} copy(bf16[2,320,512]{1,2,0:T(8,128)(2,1)S(1)} %bitcast.18) | data formatting | bytes 1310720 | tf_op jit(solution)/shard_map/reshape | solution.py:155
  16.9 6.8 %shard_map.46 = bf16[2,320,512]{2,1,0:T(8,128)(2,1)} custom-call(s32[6]{0:T(128)} %and_convert_fusion.valid_ref, bf16[2,320,512]{2,1,0:T(8,128)(2,1)} %copy.13.prev_ref, bf16[2,320,512]{2,1,0:T(8,128)(2,1)} %copy.14.own_ref, bf16[2,320,512]{2,1,0:T(8,128)(2,1)} %copy.15.next_ref, bf16[960,320]{1,0:T(8,128)(2,1)} %bitcast.20, bf16[320,320]{1,0:T(8,128)(2,1)} %bitcast.21), custom_call_target="tpu_custom_call" | custom-call | tf_op jit(solution)/shard_map/pallas_call | solution.py:82
  23.7 1.4 %copy.16 = bf16[2,320,512]{1,2,0:T(8,128)(2,1)S(1)} copy(bf16[2,320,512]{2,1,0:T(8,128)(2,1)} %shard_map.46) | data formatting | bytes 1310720 | tf_op jit(solution)/shard_map/pallas_call | solution.py:82
  25.2 0.6 %reshape.79 = bf16[2,32,5120]{2,1,0:T(8,128)(2,1)S(1)} reshape(bf16[2,32,16,320]{3,2,1,0:T(8,128)(2,1)S(1)} %bitcast.19) | data formatting | bytes 1310720 | tf_op jit(solution)/shard_map/reshape | solution.py:160
  25.8 0.1 broadcast_select_fusion.12
  25.9 4.9 %collective-permute-start.2 = (bf16[2,1,320]{2,1,0:T(2,128)(2,1)S(1)}, bf16[2,1,320]{2,1,0:T(2,128)(2,1)S(1)}, u32[]{:S(2)}, u32[]{:S(2)}) collective-permute-start(bf16[2,1,320]{2,1,0:T(2,128)(2,1)S(1)} %get-tuple-element.17), channel_id=1, source_target_pairs={{1,10},{10,1},{9,2},{2,9},{3,12},{12,3},{11,4},{4,11},{5,14},{14,5... | collective-permute-start | bytes 3848 | tf_op jit(solution)/shard_map/ppermute | solution.py:130
  30.8 0.1 collective-permute-start.3
  30.9 0.1 broadcast_select_fusion.4
  30.9 0.1 broadcast_select_fusion.7
  31.0 0.9 %collective-permute-start.4 = (bf16[2,1,5120]{2,1,0:T(2,128)(2,1)S(1)}, bf16[2,1,5120]{2,1,0:T(2,128)(2,1)S(1)}, u32[]{:S(2)}, u32[]{:S(2)}) collective-permute-start(bf16[2,1,5120]{2,1,0:T(2,128)(2,1)S(1)} %broadcast_select_fusion.4), channel_id=1, source_target_pairs={{0,8},{8,0},{1,9},{9,1},{2,10},{10,2},{3,11},{11,3},{4,12},{12,4},... | collective-permute-start | bytes 61448 | tf_op jit(solution)/shard_map/ppermute | solution.py:117
  31.9 5.0 %collective-permute-start.5 = (bf16[2,32,320]{2,1,0:T(8,128)(2,1)S(1)}, bf16[2,32,320]{2,1,0:T(8,128)(2,1)S(1)}, u32[]{:S(2)}, u32[]{:S(2)}) collective-permute-start(bf16[2,32,320]{2,1,0:T(8,128)(2,1)S(1)} %get-tuple-element.19), channel_id=1, source_target_pairs={{1,2},{2,1},{3,4},{4,3},{5,6},{6,5},{9,10},{10,9},{11,12},{12,11},... | collective-permute-start | bytes 122888 | tf_op jit(solution)/shard_map/ppermute | solution.py:117
  37.0 0.3 collective-permute-start.6
  37.2 0.0 collective-permute-done.2
  37.3 0.0 collective-permute-done.3
  37.3 0.0 collective-permute-done.4
  37.3 0.1 broadcast_select_fusion.3
  37.4 0.2 concatenate.26
  37.6 0.2 concatenate.31
  37.9 1.2 %collective-permute-done.5 = bf16[2,32,320]{2,1,0:T(8,128)(2,1)S(1)} collective-permute-done((bf16[2,32,320]{2,1,0:T(8,128)(2,1)S(1)}, bf16[2,32,320]{2,1,0:T(8,128)(2,1)S(1)}, u32[]{:S(2)}, u32[]{:S(2)}) %collective-permute-start.5) | collective-permute-done | bytes 40992 | tf_op jit(solution)/shard_map/ppermute | solution.py:117
  39.0 2.3 %collective-permute-done.6 = bf16[2,32,320]{2,1,0:T(8,128)(2,1)S(1)} collective-permute-done((bf16[2,32,320]{2,1,0:T(8,128)(2,1)S(1)}, bf16[2,32,320]{2,1,0:T(8,128)(2,1)S(1)}, u32[]{:S(2)}, u32[]{:S(2)}) %collective-permute-start.6) | collective-permute-done | bytes 40992 | tf_op jit(solution)/shard_map/ppermute | solution.py:117
  41.4 0.8 %concatenate.27 = bf16[2,32,5760]{2,1,0:T(8,128)(2,1)S(1)} concatenate(bf16[2,32,320]{2,1,0:T(8,128)(2,1)S(1)} %get-tuple-element.21, bf16[2,32,5120]{2,1,0:T(8,128)(2,1)S(1)} %reshape.79, bf16[2,32,320]{2,1,0:T(8,128)(2,1)S(1)} %get-tuple-element.20), dimensions={2} | concatenate | bytes 1474560 | tf_op jit(solution)/shard_map/concatenate | solution.py:183
  42.1 0.0 copy-done.2
  42.2 4.7 %fusion.8 = bf16[2,32,5120]{2,1,0:T(8,128)(2,1)} fusion(bf16[2,32,5120]{2,1,0:T(8,128)(2,1)S(1)} %reshape.79, bf16[2,32,5760]{2,1,0:T(8,128)(2,1)S(1)} %concatenate.27, bf16[2,1,5760]{2,1,0:T(2,128)(2,1)S(1)} %concatenate.31, bf16[2,1,5760]{2,1,0:T(2,128)(2,1)S(1)} %concatenate.26, bf16[2,32,320]{2,1,0:T(8,128)(2,1)S(1)} %get-tuple-element.20, ...), kind=kLoop, calls=%fused_computation.10 | loop fusion | flops 17039360 | bytes 2360320 | tf_op jit(solution)/shard_map/convert_element_type | solution.py:199
  (18 shorter events, 0.1 us)
Async XLA Ops:
  0.0 13.3 %collective-permute-start = (bf16[2,32,5120]{2,1,0:T(8,128)(2,1)}, bf16[2,32,5120]{2,1,0:T(8,128)(2,1)S(1)}, u32[]{:S(2)}, u32[]{:S(2)}) collective-permute-start(bf16[2,32,5120]{2,1,0:T(8,128)(2,1)} %param.4), channel_id=1, source_target_pairs={{16,32},{32,16},{48,64},{64,48},{80,96},{96,80},{112,128},{128,112... | collective-permute-start | bytes 1966088 | tf_op jit(solution)/shard_map/ppermute | solution.py:117
  1.9 11.4 %collective-permute-start.1 = (bf16[2,32,5120]{2,1,0:T(8,128)(2,1)}, bf16[2,32,5120]{2,1,0:T(8,128)(2,1)S(1)}, u32[]{:S(2)}, u32[]{:S(2)}) collective-permute-start(bf16[2,32,5120]{2,1,0:T(8,128)(2,1)} %param.4), channel_id=1, source_target_pairs={{0,16},{16,0},{32,48},{48,32},{64,80},{80,64},{96,112},{112,96},{1... | collective-permute-start | bytes 1966088 | tf_op jit(solution)/shard_map/ppermute | solution.py:117
  4.9 1.2 %copy-start = (bf16[320,960]{1,0:T(8,128)(2,1)S(1)}, bf16[320,960]{1,0:T(8,128)(2,1)}, u32[]{:S(2)}) copy-start(bf16[320,960]{1,0:T(8,128)(2,1)} %param.5) | copy-start | bytes 1843204
  6.1 1.2 %copy-start.1 = (bf16[320,320]{1,0:T(8,128)(2,1)S(1)}, bf16[320,320]{1,0:T(8,128)(2,1)}, u32[]{:S(2)}) copy-start(bf16[320,320]{1,0:T(8,128)(2,1)} %param.6) | copy-start | bytes 614404
  6.1 2.0 %copy-start.4 = (f32[9,320]{1,0:T(8,128)S(1)}, f32[9,320]{1,0:T(8,128)}, u32[]{:S(2)}) copy-start(f32[9,320]{1,0:T(8,128)} %param.7) | copy-start | bytes 34564
  25.9 11.4 %collective-permute-start.2 = (bf16[2,1,320]{2,1,0:T(2,128)(2,1)S(1)}, bf16[2,1,320]{2,1,0:T(2,128)(2,1)S(1)}, u32[]{:S(2)}, u32[]{:S(2)}) collective-permute-start(bf16[2,1,320]{2,1,0:T(2,128)(2,1)S(1)} %get-tuple-element.17), channel_id=1, source_target_pairs={{1,10},{10,1},{9,2},{2,9},{3,12},{12,3},{11,4},{4,11},{5,14},{14,5... | collective-permute-start | bytes 3848 | tf_op jit(solution)/shard_map/ppermute | solution.py:130
  30.8 6.5 %collective-permute-start.3 = (bf16[2,1,320]{2,1,0:T(2,128)(2,1)S(1)}, bf16[2,1,320]{2,1,0:T(2,128)(2,1)S(1)}, u32[]{:S(2)}, u32[]{:S(2)}) collective-permute-start(bf16[2,1,320]{2,1,0:T(2,128)(2,1)S(1)} %get-tuple-element.16), channel_id=1, source_target_pairs={{0,9},{9,0},{8,1},{1,8},{2,11},{11,2},{10,3},{3,10},{4,13},{13,4},... | collective-permute-start | bytes 3848 | tf_op jit(solution)/shard_map/ppermute | solution.py:130
  31.0 6.3 %collective-permute-start.4 = (bf16[2,1,5120]{2,1,0:T(2,128)(2,1)S(1)}, bf16[2,1,5120]{2,1,0:T(2,128)(2,1)S(1)}, u32[]{:S(2)}, u32[]{:S(2)}) collective-permute-start(bf16[2,1,5120]{2,1,0:T(2,128)(2,1)S(1)} %broadcast_select_fusion.4), channel_id=1, source_target_pairs={{0,8},{8,0},{1,9},{9,1},{2,10},{10,2},{3,11},{11,3},{4,12},{12,4},... | collective-permute-start | bytes 61448 | tf_op jit(solution)/shard_map/ppermute | solution.py:117
  31.9 7.1 %collective-permute-start.5 = (bf16[2,32,320]{2,1,0:T(8,128)(2,1)S(1)}, bf16[2,32,320]{2,1,0:T(8,128)(2,1)S(1)}, u32[]{:S(2)}, u32[]{:S(2)}) collective-permute-start(bf16[2,32,320]{2,1,0:T(8,128)(2,1)S(1)} %get-tuple-element.19), channel_id=1, source_target_pairs={{1,2},{2,1},{3,4},{4,3},{5,6},{6,5},{9,10},{10,9},{11,12},{12,11},... | collective-permute-start | bytes 122888 | tf_op jit(solution)/shard_map/ppermute | solution.py:117
  37.0 4.4 %collective-permute-start.6 = (bf16[2,32,320]{2,1,0:T(8,128)(2,1)S(1)}, bf16[2,32,320]{2,1,0:T(8,128)(2,1)S(1)}, u32[]{:S(2)}, u32[]{:S(2)}) collective-permute-start(bf16[2,32,320]{2,1,0:T(8,128)(2,1)S(1)} %get-tuple-element.18), channel_id=1, source_target_pairs={{0,1},{1,0},{2,3},{3,2},{4,5},{5,4},{6,7},{7,6},{8,9},{9,8},{10,11... | collective-permute-start | bytes 122888 | tf_op jit(solution)/shard_map/ppermute | solution.py:117
  41.3 0.8 %copy-start.2 = (f32[5120]{0:T(1024)S(1)}, f32[5120]{0:T(1024)}, u32[]{:S(2)}) copy-start(f32[5120]{0:T(1024)} %tile.56) | copy-start | bytes 61444
  41.4 0.8 %copy-start.3 = (f32[5120]{0:T(1024)S(1)}, f32[5120]{0:T(1024)}, u32[]{:S(2)}) copy-start(f32[5120]{0:T(1024)} %tile.58) | copy-start | bytes 61444

commit v7 on v5

--- a/solution.py
+++ b/solution.py
@@ -8,7 +8,7 @@
 from jax.sharding import PartitionSpec as P
 
 HEAD_DIM = 64
-BLOCK = 128
+BLOCK = 512
 
 
 def layer_norm_t(cols):

time: 45.3 us -> 44.1 us (0.974)
  Pallas kernels: 7.98 us -> 6.78 us
    pallas_call x1, Pallas kernels: 7.98 us -> 6.78 us  [attend(): pl.pallas_call(attend_kernel, grid=grid, in_specs=[pl.BlockSpec(memory_sp...]
where the time goes in v7:
time: 44.1 us; the launch traced here: 43.9 us
  local copies, waits for them, and re-layouts  11.3 us (26%)
  starting transfers between devices  10.6 us (24%)
  waiting for transfers between devices  10.6 us (24%)
  Pallas kernels  6.78 us (15%)
  other arithmetic  4.48 us (10%)
    ppermute x5, waiting for transfers between devices, swap(): return lax.ppermute(payload, axis, pairs)  10.6 us
    ppermute x5, starting transfers between devices, swap(): return lax.ppermute(payload, axis, pairs)  10.6 us
    pallas_call x1, Pallas kernels, attend(): pl.pallas_call(attend_kernel, grid=grid, in_specs=[pl.BlockSpec(memory_sp...  6.78 us
    reshape x6, local copies, waits for them, and re-layouts, body(): a.reshape(frames, rows, cols, chans).transpose(0, 3, 1, 2)  6.37 us
    convert_element_type x1, other arithmetic, body(): return acc.astype(jnp.bfloat16)  2.85 us
    unnamed x8, local copies, waits for them, and re-layouts  2.04 us
    pallas_call x1, local copies, waits for them, and re-layouts, attend(): pl.pallas_call(attend_kernel, grid=grid, in_specs=[pl.BlockSpec(memory_sp...  1.44 us
  transfers between devices with their start and end apart: 5, of which 3 were waited for; matrix products, arithmetic and copies ran while one was open for 14% of the time, Pallas kernels for 0%

profile of v7, /device:TPU:152, one launch (start us, length us, event | category | flops | bytes accessed | tf_op | source)
XLA Modules:
  0.0 43.9 jit_solution(5579320679082771948)
XLA Ops:
  0.0 1.9 %collective-permute-start = (bf16[2,32,5120]{2,1,0:T(8,128)(2,1)}, bf16[2,32,5120]{2,1,0:T(8,128)(2,1)S(1)}, u32[]{:S(2)}, u32[]{:S(2)}) collective-permute-start(bf16[2,32,5120]{2,1,0:T(8,128)(2,1)} %param.4), channel_id=1, source_target_pairs={{16,32},{32,16},{48,64},{64,48},{80,96},{96,80},{112,128},{128,112... | collective-permute-start | bytes 1966088 | tf_op jit(solution)/shard_map/ppermute | solution.py:117
  1.9 1.2 %collective-permute-start.1 = (bf16[2,32,5120]{2,1,0:T(8,128)(2,1)}, bf16[2,32,5120]{2,1,0:T(8,128)(2,1)S(1)}, u32[]{:S(2)}, u32[]{:S(2)}) collective-permute-start(bf16[2,32,5120]{2,1,0:T(8,128)(2,1)} %param.4), channel_id=1, source_target_pairs={{0,16},{16,0},{32,48},{48,32},{64,80},{80,64},{96,112},{112,96},{1... | collective-permute-start | bytes 1966088 | tf_op jit(solution)/shard_map/ppermute | solution.py:117
  3.1 1.8 %reshape.74 = bf16[2,32,16,320]{3,2,1,0:T(8,128)(2,1)S(1)} reshape(bf16[2,32,5120]{2,1,0:T(8,128)(2,1)} %param.4) | data formatting | bytes 1310720 | tf_op jit(solution)/shard_map/reshape | solution.py:142
  4.9 0.0 copy-start
  4.9 1.1 %copy.14.own_ref = bf16[2,320,512]{2,1,0:T(8,128)(2,1)} copy(bf16[2,320,512]{1,2,0:T(8,128)(2,1)S(1)} %bitcast.16) | data formatting | bytes 1310720 | tf_op jit(solution)/shard_map/reshape | solution.py:142
  6.0 0.0 copy-done
  6.0 0.0 copy-start.1
  6.0 1.2 %copy.11 = bf16[320,960]{0,1:T(8,128)(2,1)} copy(bf16[320,960]{1,0:T(8,128)(2,1)S(1)} %copy-done) | data formatting | bytes 1228800 | tf_op args[1]
  7.2 0.0 copy-done.1
  7.2 0.9 %copy.12 = bf16[320,320]{0,1:T(8,128)(2,1)} copy(bf16[320,320]{1,0:T(8,128)(2,1)S(1)} %copy-done.1) | data formatting | bytes 409600 | tf_op args[2]
  8.1 0.5 %and_convert_fusion.valid_ref = s32[6]{0:T(128)} fusion(s32[]{:T(128)S(6)} %mul.75), kind=kLoop, calls=%fused_computation.27 | loop fusion | flops 36 | bytes 28 | tf_op jit(solution)/shard_map/convert_element_type | solution.py:141
  8.6 4.7 %collective-permute-done = bf16[2,32,5120]{2,1,0:T(8,128)(2,1)S(1)} collective-permute-done((bf16[2,32,5120]{2,1,0:T(8,128)(2,1)}, bf16[2,32,5120]{2,1,0:T(8,128)(2,1)S(1)}, u32[]{:S(2)}, u32[]{:S(2)}) %collective-permute-start) | collective-permute-done | bytes 655392 | tf_op jit(solution)/shard_map/ppermute | solution.py:117
  13.3 0.0 collective-permute-done.1
  13.3 0.1 broadcast_select_fusion
  13.4 0.6 %reshape.72 = bf16[2,32,16,320]{3,2,1,0:T(8,128)(2,1)S(1)} reshape(bf16[2,32,5120]{2,1,0:T(8,128)(2,1)S(1)} %get-tuple-element.18) | data formatting | bytes 1310720 | tf_op jit(solution)/shard_map/reshape | solution.py:142
  14.0 1.1 %copy.13.prev_ref = bf16[2,320,512]{2,1,0:T(8,128)(2,1)} copy(bf16[2,320,512]{1,2,0:T(8,128)(2,1)S(1)} %bitcast.17) | data formatting | bytes 1310720 | tf_op jit(solution)/shard_map/reshape | solution.py:142
  15.2 0.6 %reshape.76 = bf16[2,32,16,320]{3,2,1,0:T(8,128)(2,1)S(1)} reshape(bf16[2,32,5120]{2,1,0:T(8,128)(2,1)S(1)} %get-tuple-element.17) | data formatting | bytes 1310720 | tf_op jit(solution)/shard_map/reshape | solution.py:142
  15.8 1.1 %copy.15.next_ref = bf16[2,320,512]{2,1,0:T(8,128)(2,1)} copy(bf16[2,320,512]{1,2,0:T(8,128)(2,1)S(1)} %bitcast.18) | data formatting | bytes 1310720 | tf_op jit(solution)/shard_map/reshape | solution.py:142
  16.9 6.8 %shard_map.46 = bf16[2,320,512]{2,1,0:T(8,128)(2,1)} custom-call(s32[6]{0:T(128)} %and_convert_fusion.valid_ref, bf16[2,320,512]{2,1,0:T(8,128)(2,1)} %copy.13.prev_ref, bf16[2,320,512]{2,1,0:T(8,128)(2,1)} %copy.14.own_ref, bf16[2,320,512]{2,1,0:T(8,128)(2,1)} %copy.15.next_ref, bf16[960,320]{1,0:T(8,128)(2,1)} %bitcast.20, bf16[320,320]{1,0:T(8,128)(2,1)} %bitcast.21), custom_call_target="tpu_custom_call" | custom-call | tf_op jit(solution)/shard_map/pallas_call | solution.py:82
  23.7 1.4 %copy.16 = bf16[2,320,512]{1,2,0:T(8,128)(2,1)S(1)} copy(bf16[2,320,512]{2,1,0:T(8,128)(2,1)} %shard_map.46) | data formatting | bytes 1310720 | tf_op jit(solution)/shard_map/pallas_call | solution.py:82
  25.2 0.6 %reshape.79 = bf16[2,32,5120]{2,1,0:T(8,128)(2,1)S(1)} reshape(bf16[2,32,16,320]{3,2,1,0:T(8,128)(2,1)S(1)} %bitcast.19) | data formatting | bytes 1310720 | tf_op jit(solution)/shard_map/reshape | solution.py:147
  25.8 0.0 copy-start.2
  25.8 0.1 broadcast_select_fusion.4
  25.9 3.1 %collective-permute-start.2 = (bf16[2,1,5120]{2,1,0:T(2,128)(2,1)S(1)}, bf16[2,1,5120]{2,1,0:T(2,128)(2,1)S(1)}, u32[]{:S(2)}, u32[]{:S(2)}) collective-permute-start(bf16[2,1,5120]{2,1,0:T(2,128)(2,1)S(1)} %broadcast_select_fusion.4), channel_id=1, source_target_pairs={{0,8},{8,0},{1,9},{9,1},{2,10},{10,2},{3,11},{11,3},{4,12},{12,4},... | collective-permute-start | bytes 61448 | tf_op jit(solution)/shard_map/ppermute | solution.py:117
  29.0 2.5 %collective-permute-done.2 = bf16[2,1,5120]{2,1,0:T(2,128)(2,1)S(1)} collective-permute-done((bf16[2,1,5120]{2,1,0:T(2,128)(2,1)S(1)}, bf16[2,1,5120]{2,1,0:T(2,128)(2,1)S(1)}, u32[]{:S(2)}, u32[]{:S(2)}) %collective-permute-start.2) | collective-permute-done | bytes 20512 | tf_op jit(solution)/shard_map/ppermute | solution.py:117
  31.5 0.1 broadcast_select_fusion.3
  31.6 0.1 broadcast_select_fusion.8
  31.7 1.6 %collective-permute-start.4 = (bf16[2,34,320]{2,1,0:T(8,128)(2,1)S(1)}, bf16[2,34,320]{2,1,0:T(8,128)(2,1)S(1)}, u32[]{:S(2)}, u32[]{:S(2)}) collective-permute-start(bf16[2,34,320]{2,1,0:T(8,128)(2,1)S(1)} %broadcast_select_fusion.7), channel_id=1, source_target_pairs={{0,1},{1,0},{2,3},{3,2},{4,5},{5,4},{6,7},{7,6},{8,9},{9,8},{10,11... | collective-permute-start | bytes 130568 | tf_op jit(solution)/shard_map/ppermute | solution.py:117
  33.3 2.8 %collective-permute-start.3 = (bf16[2,34,320]{2,1,0:T(8,128)(2,1)S(1)}, bf16[2,34,320]{2,1,0:T(8,128)(2,1)S(1)}, u32[]{:S(2)}, u32[]{:S(2)}) collective-permute-start(bf16[2,34,320]{2,1,0:T(8,128)(2,1)S(1)} %get-tuple-element.14), channel_id=1, source_target_pairs={{1,2},{2,1},{3,4},{4,3},{5,6},{6,5},{9,10},{10,9},{11,12},{12,11},... | collective-permute-start | bytes 130568 | tf_op jit(solution)/shard_map/ppermute | solution.py:117
  36.1 0.0 copy-done.2
  36.1 0.1 slice_reduce_fusion.8
  36.1 0.1 tile.42
  36.2 0.1 tile.44
  36.3 0.1 tile.46
  36.4 0.1 tile.48
  36.5 0.1 tile.50
  36.6 0.1 tile.52
  36.6 0.1 tile.54
  36.7 0.1 tile.56
  36.8 0.1 tile.58
  36.9 0.0 collective-permute-done.4
  36.9 3.4 %collective-permute-done.3 = bf16[2,34,320]{2,1,0:T(8,128)(2,1)S(1)} collective-permute-done((bf16[2,34,320]{2,1,0:T(8,128)(2,1)S(1)}, bf16[2,34,320]{2,1,0:T(8,128)(2,1)S(1)}, u32[]{:S(2)}, u32[]{:S(2)}) %collective-permute-start.3) | collective-permute-done | bytes 43552 | tf_op jit(solution)/shard_map/ppermute | solution.py:117
  40.3 0.8 %maximum_maximum_fusion = (bf16[2,34,5440]{2,1,0:T(8,128)(2,1)S(1)}, bf16[2,34,5440]{2,1,0:T(8,128)(2,1)S(1)}) fusion(bf16[2,1,5120]{2,1,0:T(2,128)(2,1)S(1)} %get-tuple-element.24, bf16[2,32,5120]{2,1,0:T(8,128)(2,1)S(1)} %reshape.79, bf16[2,1,5120]{2,1,0:T(2,128)(2,1)S(1)} %get-tuple-element.23, bf16[2,34,320]{2,1,0:T(8,128)(2,1)S(1)} %get-tuple-element.21, ...), kind=kLoop, calls=%fused_computation.11 | loop fusion | flops 5918720 | bytes 2263040 | tf_op jit(solution)/shard_map/concatenate | solution.py:153
  41.1 2.8 %fusion.8 = bf16[2,32,5120]{2,1,0:T(8,128)(2,1)} fusion(bf16[2,32,5120]{2,1,0:T(8,128)(2,1)S(1)} %reshape.79, bf16[2,34,5440]{2,1,0:T(8,128)(2,1)S(1)} %get-tuple-element.20, bf16[2,1,5120]{2,1,0:T(2,128)(2,1)S(1)} %get-tuple-element.24, bf16[2,34,5440]{2,1,0:T(8,128)(2,1)S(1)} %get-tuple-element.19, bf16[2,1,5120]{2,1,0:T(2,128)(2,1)S(1)} %get-tuple-element.23, ...), kind=kLoop, calls=%fused_computation.10 | loop fusion | flops 11141120 | bytes 5468160 | tf_op jit(solution)/shard_map/convert_element_type | solution.py:165
  (11 shorter events, 0.1 us)
Async XLA Ops:
  0.0 13.3 %collective-permute-start = (bf16[2,32,5120]{2,1,0:T(8,128)(2,1)}, bf16[2,32,5120]{2,1,0:T(8,128)(2,1)S(1)}, u32[]{:S(2)}, u32[]{:S(2)}) collective-permute-start(bf16[2,32,5120]{2,1,0:T(8,128)(2,1)} %param.4), channel_id=1, source_target_pairs={{16,32},{32,16},{48,64},{64,48},{80,96},{96,80},{112,128},{128,112... | collective-permute-start | bytes 1966088 | tf_op jit(solution)/shard_map/ppermute | solution.py:117
  1.9 11.4 %collective-permute-start.1 = (bf16[2,32,5120]{2,1,0:T(8,128)(2,1)}, bf16[2,32,5120]{2,1,0:T(8,128)(2,1)S(1)}, u32[]{:S(2)}, u32[]{:S(2)}) collective-permute-start(bf16[2,32,5120]{2,1,0:T(8,128)(2,1)} %param.4), channel_id=1, source_target_pairs={{0,16},{16,0},{32,48},{48,32},{64,80},{80,64},{96,112},{112,96},{1... | collective-permute-start | bytes 1966088 | tf_op jit(solution)/shard_map/ppermute | solution.py:117
  4.9 1.1 %copy-start = (bf16[320,960]{1,0:T(8,128)(2,1)S(1)}, bf16[320,960]{1,0:T(8,128)(2,1)}, u32[]{:S(2)}) copy-start(bf16[320,960]{1,0:T(8,128)(2,1)} %param.5) | copy-start | bytes 1843204
  6.0 1.2 %copy-start.1 = (bf16[320,320]{1,0:T(8,128)(2,1)S(1)}, bf16[320,320]{1,0:T(8,128)(2,1)}, u32[]{:S(2)}) copy-start(bf16[320,320]{1,0:T(8,128)(2,1)} %param.6) | copy-start | bytes 614404
  25.8 10.3 %copy-start.2 = (f32[9,320]{1,0:T(8,128)S(1)}, f32[9,320]{1,0:T(8,128)}, u32[]{:S(2)}) copy-start(f32[9,320]{1,0:T(8,128)} %param.7) | copy-start | bytes 34564
  25.9 5.6 %collective-permute-start.2 = (bf16[2,1,5120]{2,1,0:T(2,128)(2,1)S(1)}, bf16[2,1,5120]{2,1,0:T(2,128)(2,1)S(1)}, u32[]{:S(2)}, u32[]{:S(2)}) collective-permute-start(bf16[2,1,5120]{2,1,0:T(2,128)(2,1)S(1)} %broadcast_select_fusion.4), channel_id=1, source_target_pairs={{0,8},{8,0},{1,9},{9,1},{2,10},{10,2},{3,11},{11,3},{4,12},{12,4},... | collective-permute-start | bytes 61448 | tf_op jit(solution)/shard_map/ppermute | solution.py:117
  31.7 5.2 %collective-permute-start.4 = (bf16[2,34,320]{2,1,0:T(8,128)(2,1)S(1)}, bf16[2,34,320]{2,1,0:T(8,128)(2,1)S(1)}, u32[]{:S(2)}, u32[]{:S(2)}) collective-permute-start(bf16[2,34,320]{2,1,0:T(8,128)(2,1)S(1)} %broadcast_select_fusion.7), channel_id=1, source_target_pairs={{0,1},{1,0},{2,3},{3,2},{4,5},{5,4},{6,7},{7,6},{8,9},{9,8},{10,11... | collective-permute-start | bytes 130568 | tf_op jit(solution)/shard_map/ppermute | solution.py:117
  33.3 7.0 %collective-permute-start.3 = (bf16[2,34,320]{2,1,0:T(8,128)(2,1)S(1)}, bf16[2,34,320]{2,1,0:T(8,128)(2,1)S(1)}, u32[]{:S(2)}, u32[]{:S(2)}) collective-permute-start(bf16[2,34,320]{2,1,0:T(8,128)(2,1)S(1)} %get-tuple-element.14), channel_id=1, source_target_pairs={{1,2},{2,1},{3,4},{4,3},{5,6},{6,5},{9,10},{10,9},{11,12},{12,11},... | collective-permute-start | bytes 130568 | tf_op jit(solution)/shard_map/ppermute | solution.py:117

commit v8 on v7

--- a/solution.py
+++ b/solution.py
@@ -134,15 +134,16 @@
     chans = w_out.shape[0]
     cols = merged // chans
     points = rows * cols
-    x_prev, x_next = exchange(latents, latents, "tm")
+    cells = lambda a: a.reshape(frames, rows, cols, chans).transpose(0, 3, 1, 2).reshape(
+        frames, chans, points
+    )
+    own_c = cells(latents)
+    x_prev, x_next = exchange(own_c, own_c, "tm")
     first = lax.axis_index("tm") * frames
     total = lax.axis_size("tm") * frames
     where_t = first + jnp.arange(6, dtype=jnp.int32) - 2
     valid = ((where_t >= 0) & (where_t < total)).astype(jnp.int32)
-    cells = lambda a: a.reshape(frames, rows, cols, chans).transpose(0, 3, 1, 2).reshape(
-        frames, chans, points
-    )
-    hidden = attend(valid, cells(x_prev), cells(latents), cells(x_next), w_qkv, w_out)
+    hidden = attend(valid, x_prev, own_c, x_next, w_qkv, w_out)
     hid = (
         hidden.reshape(frames, chans, rows, cols).transpose(0, 2, 3, 1).reshape(frames, rows, merged)
     )

time: 44.1 us -> 43.7 us (level)
  local copies, waits for them, and re-layouts: 11.3 us -> 6.94 us
  waiting for transfers between devices: 10.6 us -> 13.5 us
  other arithmetic: 4.48 us -> 5.53 us
    reshape x6 -> x2, local copies, waits for them, and re-layouts: 6.37 us -> 2.03 us  [body(): a.reshape(frames, rows, cols, chans).transpose(0, 3, 1, 2)]
    ppermute x5, waiting for transfers between devices: 10.6 us -> 13.5 us  [swap(): return lax.ppermute(payload, axis, pairs)]
    select_n x1, other arithmetic: 0.09 us -> 1.14 us  [exchange(): from_next = jnp.where(even, got_a, got_b)]
    unnamed x8 -> x10, local copies, waits for them, and re-layouts: 2.04 us -> 2.04 us
  transfers between devices with their start and end apart: 5 -> 5, of which waited for: 3 -> 3; matrix products, arithmetic and copies ran while one was open for 14% -> 8% of each run, Pallas kernels for 0% -> 0%
where the time goes in v8:
time: 43.7 us; the launch traced here: 43.5 us
  waiting for transfers between devices  13.5 us (31%)
  starting transfers between devices  10.5 us (24%)
  local copies, waits for them, and re-layouts  6.94 us (16%)
  Pallas kernels  6.79 us (16%)
  other arithmetic  5.53 us (13%)
    ppermute x5, waiting for transfers between devices, swap(): return lax.ppermute(payload, axis, pairs)  13.5 us
    ppermute x5, starting transfers between devices, swap(): return lax.ppermute(payload, axis, pairs)  10.5 us
    pallas_call x1, Pallas kernels, attend(): pl.pallas_call(attend_kernel, grid=grid, in_specs=[pl.BlockSpec(memory_sp...  6.79 us
    convert_element_type x1, other arithmetic, body(): return acc.astype(jnp.bfloat16)  2.85 us
    unnamed x10, local copies, waits for them, and re-layouts  2.04 us
    reshape x2, local copies, waits for them, and re-layouts, body(): a.reshape(frames, rows, cols, chans).transpose(0, 3, 1, 2)  2.03 us
    pallas_call x1, local copies, waits for them, and re-layouts, attend(): pl.pallas_call(attend_kernel, grid=grid, in_specs=[pl.BlockSpec(memory_sp...  1.44 us
    select_n x1, other arithmetic, exchange(): from_next = jnp.where(even, got_a, got_b)  1.14 us
  transfers between devices with their start and end apart: 5, of which 3 were waited for; matrix products, arithmetic and copies ran while one was open for 8% of the time, Pallas kernels for 0%

profile of v8, /device:TPU:152, one launch (start us, length us, event | category | flops | bytes accessed | tf_op | source)
XLA Modules:
  0.0 43.5 jit_solution(12872540337322652188)
XLA Ops:
  0.0 1.8 %reshape.60 = bf16[2,32,16,320]{3,2,1,0:T(8,128)(2,1)S(1)} reshape(bf16[2,32,5120]{2,1,0:T(8,128)(2,1)} %param.4) | data formatting | bytes 1310720 | tf_op jit(solution)/shard_map/reshape | solution.py:137
  1.8 0.0 copy-start.1
  1.8 0.3 copy.9.own_ref
  2.1 0.0 copy-start
  2.1 0.0 copy-start.2
  2.1 2.1 %collective-permute-start = (bf16[2,320,512]{2,1,0:T(8,128)(2,1)S(1)}, bf16[2,320,512]{2,1,0:T(8,128)(2,1)S(1)}, u32[]{:S(2)}, u32[]{:S(2)}) collective-permute-start(bf16[2,320,512]{2,1,0:T(8,128)(2,1)S(1)} %copy.9.own_ref), channel_id=1, source_target_pairs={{16,32},{32,16},{48,64},{64,48},{80,96},{96,80},{112,128},{128,112... | collective-permute-start | bytes 1966088 | tf_op jit(solution)/shard_map/ppermute | solution.py:117
  4.1 1.2 %collective-permute-start.1 = (bf16[2,320,512]{2,1,0:T(8,128)(2,1)S(1)}, bf16[2,320,512]{2,1,0:T(8,128)(2,1)S(1)}, u32[]{:S(2)}, u32[]{:S(2)}) collective-permute-start(bf16[2,320,512]{2,1,0:T(8,128)(2,1)S(1)} %copy.9.own_ref), channel_id=1, source_target_pairs={{0,16},{16,0},{32,48},{48,32},{64,80},{80,64},{96,112},{112,96},{1... | collective-permute-start | bytes 1966088 | tf_op jit(solution)/shard_map/ppermute | solution.py:117
  5.4 0.0 copy-done.1
  5.4 1.2 %copy.11 = bf16[320,960]{0,1:T(8,128)(2,1)} copy(bf16[320,960]{1,0:T(8,128)(2,1)S(1)} %copy-done.1) | data formatting | bytes 1228800 | tf_op args[1]
  6.5 0.0 copy-done.2
  6.5 0.9 %copy.12 = bf16[320,320]{0,1:T(8,128)(2,1)} copy(bf16[320,320]{1,0:T(8,128)(2,1)S(1)} %copy-done.2) | data formatting | bytes 409600 | tf_op args[2]
  7.4 0.0 copy-done
  7.4 0.5 %and_convert_fusion.valid_ref = s32[6]{0:T(128)} fusion(s32[]{:T(128)S(6)} %mul.75), kind=kLoop, calls=%fused_computation.27 | loop fusion | flops 36 | bytes 28 | tf_op jit(solution)/shard_map/convert_element_type | solution.py:145
  7.9 7.4 %collective-permute-done = bf16[2,320,512]{2,1,0:T(8,128)(2,1)S(1)} collective-permute-done((bf16[2,320,512]{2,1,0:T(8,128)(2,1)S(1)}, bf16[2,320,512]{2,1,0:T(8,128)(2,1)S(1)}, u32[]{:S(2)}, u32[]{:S(2)}) %collective-permute-start) | collective-permute-done | bytes 655392 | tf_op jit(solution)/shard_map/ppermute | solution.py:117
  15.3 0.0 collective-permute-done.1
  15.3 1.1 %broadcast_select_fusion = (bf16[2,320,512]{2,1,0:T(8,128)(2,1)}, bf16[2,320,512]{2,1,0:T(8,128)(2,1)}) fusion(bf16[2,320,512]{2,1,0:T(8,128)(2,1)S(1)} %collective-permute-done.1, bf16[2,320,512]{2,1,0:T(8,128)(2,1)S(1)} %collective-permute-done, pred[]{:T(512)S(6)} %eq.23), kind=kLoop, calls=%fused_computation.15 | loop fusion | flops 655360 | bytes 2621441 | tf_op jit(solution)/shard_map/jit(_where)/select_n | solution.py:128
  16.5 6.8 %shard_map.46 = bf16[2,320,512]{2,1,0:T(8,128)(2,1)} custom-call(s32[6]{0:T(128)} %and_convert_fusion.valid_ref, bf16[2,320,512]{2,1,0:T(8,128)(2,1)} %get-tuple-element.18.prev_ref, bf16[2,320,512]{2,1,0:T(8,128)(2,1)} %copy-done, bf16[2,320,512]{2,1,0:T(8,128)(2,1)} %get-tuple-element.17.next_ref, bf16[960,320]{1,0:T(8,128)(2,1)} %bitcast.12, ...), custom_call_target="tpu_custom_call" | custom-call | tf_op jit(solution)/shard_map/pallas_call | solution.py:82
  23.3 1.4 %copy.14 = bf16[2,320,512]{1,2,0:T(8,128)(2,1)S(1)} copy(bf16[2,320,512]{2,1,0:T(8,128)(2,1)} %shard_map.46) | data formatting | bytes 1310720 | tf_op jit(solution)/shard_map/pallas_call | solution.py:82
  24.7 0.6 %reshape.63 = bf16[2,32,5120]{2,1,0:T(8,128)(2,1)S(1)} reshape(bf16[2,32,16,320]{3,2,1,0:T(8,128)(2,1)S(1)} %bitcast.10) | data formatting | bytes 1310720 | tf_op jit(solution)/shard_map/reshape | solution.py:148
  25.4 0.0 copy-start.3
  25.4 0.1 broadcast_select_fusion.4
  25.4 3.1 %collective-permute-start.2 = (bf16[2,1,5120]{2,1,0:T(2,128)(2,1)S(1)}, bf16[2,1,5120]{2,1,0:T(2,128)(2,1)S(1)}, u32[]{:S(2)}, u32[]{:S(2)}) collective-permute-start(bf16[2,1,5120]{2,1,0:T(2,128)(2,1)S(1)} %broadcast_select_fusion.4), channel_id=1, source_target_pairs={{0,8},{8,0},{1,9},{9,1},{2,10},{10,2},{3,11},{11,3},{4,12},{12,4},... | collective-permute-start | bytes 61448 | tf_op jit(solution)/shard_map/ppermute | solution.py:117
  28.5 2.5 %collective-permute-done.2 = bf16[2,1,5120]{2,1,0:T(2,128)(2,1)S(1)} collective-permute-done((bf16[2,1,5120]{2,1,0:T(2,128)(2,1)S(1)}, bf16[2,1,5120]{2,1,0:T(2,128)(2,1)S(1)}, u32[]{:S(2)}, u32[]{:S(2)}) %collective-permute-start.2) | collective-permute-done | bytes 20512 | tf_op jit(solution)/shard_map/ppermute | solution.py:117
  31.0 0.1 broadcast_select_fusion.3
  31.1 0.1 broadcast_select_fusion.8
  31.2 1.6 %collective-permute-start.4 = (bf16[2,34,320]{2,1,0:T(8,128)(2,1)S(1)}, bf16[2,34,320]{2,1,0:T(8,128)(2,1)S(1)}, u32[]{:S(2)}, u32[]{:S(2)}) collective-permute-start(bf16[2,34,320]{2,1,0:T(8,128)(2,1)S(1)} %broadcast_select_fusion.7), channel_id=1, source_target_pairs={{0,1},{1,0},{2,3},{3,2},{4,5},{5,4},{6,7},{7,6},{8,9},{9,8},{10,11... | collective-permute-start | bytes 130568 | tf_op jit(solution)/shard_map/ppermute | solution.py:117
  32.8 2.6 %collective-permute-start.3 = (bf16[2,34,320]{2,1,0:T(8,128)(2,1)S(1)}, bf16[2,34,320]{2,1,0:T(8,128)(2,1)S(1)}, u32[]{:S(2)}, u32[]{:S(2)}) collective-permute-start(bf16[2,34,320]{2,1,0:T(8,128)(2,1)S(1)} %get-tuple-element.14), channel_id=1, source_target_pairs={{1,2},{2,1},{3,4},{4,3},{5,6},{6,5},{9,10},{10,9},{11,12},{12,11},... | collective-permute-start | bytes 130568 | tf_op jit(solution)/shard_map/ppermute | solution.py:117
  35.4 0.0 copy-done.3
  35.5 0.1 slice_reduce_fusion.8
  35.5 0.1 tile.42
  35.6 0.1 tile.44
  35.7 0.1 tile.46
  35.8 0.1 tile.48
  35.8 0.1 tile.50
  35.9 0.1 tile.52
  36.0 0.1 tile.54
  36.1 0.1 tile.56
  36.2 0.1 tile.58
  36.3 0.0 collective-permute-done.4
  36.3 3.6 %collective-permute-done.3 = bf16[2,34,320]{2,1,0:T(8,128)(2,1)S(1)} collective-permute-done((bf16[2,34,320]{2,1,0:T(8,128)(2,1)S(1)}, bf16[2,34,320]{2,1,0:T(8,128)(2,1)S(1)}, u32[]{:S(2)}, u32[]{:S(2)}) %collective-permute-start.3) | collective-permute-done | bytes 43552 | tf_op jit(solution)/shard_map/ppermute | solution.py:117
  39.8 0.8 %maximum_maximum_fusion = (bf16[2,34,5440]{2,1,0:T(8,128)(2,1)S(1)}, bf16[2,34,5440]{2,1,0:T(8,128)(2,1)S(1)}) fusion(bf16[2,1,5120]{2,1,0:T(2,128)(2,1)S(1)} %get-tuple-element.24, bf16[2,32,5120]{2,1,0:T(8,128)(2,1)S(1)} %reshape.63, bf16[2,1,5120]{2,1,0:T(2,128)(2,1)S(1)} %get-tuple-element.23, bf16[2,34,320]{2,1,0:T(8,128)(2,1)S(1)} %get-tuple-element.21, ...), kind=kLoop, calls=%fused_computation.11 | loop fusion | flops 5918720 | bytes 2263040 | tf_op jit(solution)/shard_map/concatenate | solution.py:154
  40.6 2.8 %fusion.8 = bf16[2,32,5120]{2,1,0:T(8,128)(2,1)} fusion(bf16[2,32,5120]{2,1,0:T(8,128)(2,1)S(1)} %reshape.63, bf16[2,34,5440]{2,1,0:T(8,128)(2,1)S(1)} %get-tuple-element.20, bf16[2,1,5120]{2,1,0:T(2,128)(2,1)S(1)} %get-tuple-element.24, bf16[2,34,5440]{2,1,0:T(8,128)(2,1)S(1)} %get-tuple-element.19, bf16[2,1,5120]{2,1,0:T(2,128)(2,1)S(1)} %get-tuple-element.23, ...), kind=kLoop, calls=%fused_computation.10 | loop fusion | flops 11141120 | bytes 5468160 | tf_op jit(solution)/shard_map/convert_element_type | solution.py:166
  (11 shorter events, 0.1 us)
Async XLA Ops:
  1.8 3.6 %copy-start.1 = (bf16[320,960]{1,0:T(8,128)(2,1)S(1)}, bf16[320,960]{1,0:T(8,128)(2,1)}, u32[]{:S(2)}) copy-start(bf16[320,960]{1,0:T(8,128)(2,1)} %param.5) | copy-start | bytes 1843204
  2.1 5.3 %copy-start = (bf16[2,320,512]{2,1,0:T(8,128)(2,1)}, bf16[2,320,512]{2,1,0:T(8,128)(2,1)S(1)}, u32[]{:S(2)}) copy-start(bf16[2,320,512]{2,1,0:T(8,128)(2,1)S(1)} %copy.9.own_ref) | copy-start | bytes 1966084
  2.1 4.4 %copy-start.2 = (bf16[320,320]{1,0:T(8,128)(2,1)S(1)}, bf16[320,320]{1,0:T(8,128)(2,1)}, u32[]{:S(2)}) copy-start(bf16[320,320]{1,0:T(8,128)(2,1)} %param.6) | copy-start | bytes 614404
  2.1 13.2 %collective-permute-start = (bf16[2,320,512]{2,1,0:T(8,128)(2,1)S(1)}, bf16[2,320,512]{2,1,0:T(8,128)(2,1)S(1)}, u32[]{:S(2)}, u32[]{:S(2)}) collective-permute-start(bf16[2,320,512]{2,1,0:T(8,128)(2,1)S(1)} %copy.9.own_ref), channel_id=1, source_target_pairs={{16,32},{32,16},{48,64},{64,48},{80,96},{96,80},{112,128},{128,112... | collective-permute-start | bytes 1966088 | tf_op jit(solution)/shard_map/ppermute | solution.py:117
  4.1 11.2 %collective-permute-start.1 = (bf16[2,320,512]{2,1,0:T(8,128)(2,1)S(1)}, bf16[2,320,512]{2,1,0:T(8,128)(2,1)S(1)}, u32[]{:S(2)}, u32[]{:S(2)}) collective-permute-start(bf16[2,320,512]{2,1,0:T(8,128)(2,1)S(1)} %copy.9.own_ref), channel_id=1, source_target_pairs={{0,16},{16,0},{32,48},{48,32},{64,80},{80,64},{96,112},{112,96},{1... | collective-permute-start | bytes 1966088 | tf_op jit(solution)/shard_map/ppermute | solution.py:117
  25.4 10.1 %copy-start.3 = (f32[9,320]{1,0:T(8,128)S(1)}, f32[9,320]{1,0:T(8,128)}, u32[]{:S(2)}) copy-start(f32[9,320]{1,0:T(8,128)} %param.7) | copy-start | bytes 34564
  25.4 5.6 %collective-permute-start.2 = (bf16[2,1,5120]{2,1,0:T(2,128)(2,1)S(1)}, bf16[2,1,5120]{2,1,0:T(2,128)(2,1)S(1)}, u32[]{:S(2)}, u32[]{:S(2)}) collective-permute-start(bf16[2,1,5120]{2,1,0:T(2,128)(2,1)S(1)} %broadcast_select_fusion.4), channel_id=1, source_target_pairs={{0,8},{8,0},{1,9},{9,1},{2,10},{10,2},{3,11},{11,3},{4,12},{12,4},... | collective-permute-start | bytes 61448 | tf_op jit(solution)/shard_map/ppermute | solution.py:117
  31.2 5.0 %collective-permute-start.4 = (bf16[2,34,320]{2,1,0:T(8,128)(2,1)S(1)}, bf16[2,34,320]{2,1,0:T(8,128)(2,1)S(1)}, u32[]{:S(2)}, u32[]{:S(2)}) collective-permute-start(bf16[2,34,320]{2,1,0:T(8,128)(2,1)S(1)} %broadcast_select_fusion.7), channel_id=1, source_target_pairs={{0,1},{1,0},{2,3},{3,2},{4,5},{5,4},{6,7},{7,6},{8,9},{9,8},{10,11... | collective-permute-start | bytes 130568 | tf_op jit(solution)/shard_map/ppermute | solution.py:117
  32.8 7.0 %collective-permute-start.3 = (bf16[2,34,320]{2,1,0:T(8,128)(2,1)S(1)}, bf16[2,34,320]{2,1,0:T(8,128)(2,1)S(1)}, u32[]{:S(2)}, u32[]{:S(2)}) collective-permute-start(bf16[2,34,320]{2,1,0:T(8,128)(2,1)S(1)} %get-tuple-element.14), channel_id=1, source_target_pairs={{1,2},{2,1},{3,4},{4,3},{5,6},{6,5},{9,10},{10,9},{11,12},{12,11},... | collective-permute-start | bytes 130568 | tf_op jit(solution)/shard_map/ppermute | solution.py:117

commit v9 on v8

--- a/solution.py
+++ b/solution.py
@@ -147,12 +147,25 @@
     hid = (
         hidden.reshape(frames, chans, rows, cols).transpose(0, 2, 3, 1).reshape(frames, rows, merged)
     )
-
-    halo_top, halo_bot = exchange(hid[:, rows - 1 :, :], hid[:, :1, :], "row")
-    tall = jnp.concatenate([halo_top, hid, halo_bot], axis=1)
-    halo_left, halo_right = exchange(tall[:, :, merged - chans :], tall[:, :, :chans], "col")
-    padded = jnp.concatenate([halo_left, tall, halo_right], axis=2)
+    as_row = lambda a: a.transpose(0, 2, 1).reshape(frames, 1, merged)
+    as_col = lambda a: a.transpose(0, 2, 1)
+    bot_row = as_row(hidden[:, :, (rows - 1) * cols :])
+    top_row = as_row(hidden[:, :, :cols])
+    halo_top, halo_bot = exchange(bot_row, top_row, "row")
+    left_col = as_col(hidden[:, :, 0::cols])
+    right_col = as_col(hidden[:, :, cols - 1 :: cols])
+    tall_l = jnp.concatenate([halo_top[:, :, :chans], left_col, halo_bot[:, :, :chans]], axis=1)
+    tall_r = jnp.concatenate(
+        [halo_top[:, :, merged - chans :], right_col, halo_bot[:, :, merged - chans :]], axis=1
+    )
+    halo_left, halo_right = exchange(tall_r, tall_l, "col")
+
     taps = jnp.tile(conv_weight, (1, cols))
+    zero_col = jnp.zeros((frames, rows + 2, chans), jnp.bfloat16)
+    zero_row = jnp.zeros((frames, 1, merged), jnp.bfloat16)
+    padded = jnp.concatenate(
+        [zero_col, jnp.concatenate([zero_row, hid, zero_row], axis=1), zero_col], axis=2
+    )
     acc = hid.astype(jnp.float32)
     for tap_a in range(3):
         for tap_b in range(3):
@@ -163,6 +176,27 @@
                 )
                 * taps[3 * tap_a + tap_b]
             )
+    acc = lax.optimization_barrier(acc)
+    top_full = jnp.concatenate([halo_left[:, :1], halo_top, halo_right[:, :1]], axis=2)
+    bot_full = jnp.concatenate([halo_left[:, rows + 1 :], halo_bot, halo_right[:, rows + 1 :]], axis=2)
+    row_term = lambda full, a: sum(
+        full[:, :, b * chans : b * chans + merged].astype(jnp.float32) * taps[3 * a + b]
+        for b in range(3)
+    )
+    side = lambda halo: jnp.concatenate(
+        [jnp.zeros((frames, 1, chans), jnp.bfloat16), halo[:, 1 : rows + 1], jnp.zeros((frames, 1, chans), jnp.bfloat16)],
+        axis=1,
+    )
+    col_term = lambda halo, b: sum(
+        side(halo)[:, a : a + rows].astype(jnp.float32) * conv_weight[3 * a + b] for a in range(3)
+    )
+    border = (
+        jnp.pad(row_term(top_full, 0), ((0, 0), (0, rows - 1), (0, 0)))
+        + jnp.pad(row_term(bot_full, 2), ((0, 0), (rows - 1, 0), (0, 0)))
+        + jnp.pad(col_term(halo_left, 0), ((0, 0), (0, 0), (0, merged - chans)))
+        + jnp.pad(col_term(halo_right, 2), ((0, 0), (0, 0), (merged - chans, 0)))
+    )
+    acc = acc + border
     return acc.astype(jnp.bfloat16)
 
 

time: 43.7 us -> 76 us (1.74)
  the two profiles are of different devices: /device:TPU:152 before, /device:TPU:104 now
where the time goes in v9:
time: 76 us; the launch traced here: 75.6 us
  other arithmetic  30.3 us (40%)
  local copies, waits for them, and re-layouts  24.8 us (33%)
  starting transfers between devices  13.3 us (18%)
  Pallas kernels  6.8 us (9%)
    ppermute x5, starting transfers between devices, swap(): return lax.ppermute(payload, axis, pairs)  13.3 us
    add x1, other arithmetic, body(): acc + padded[:, tap_a:tap_a + rows, tap_b * chans:tap_b * chans + merged]...  11.6 us
    add x1, other arithmetic, body(): sum((full[:, :, b * chans:b * chans + merged].astype(jnp.float32) * taps[...  7.35 us
    pallas_call x1, Pallas kernels, attend(): pl.pallas_call(attend_kernel, grid=grid, in_specs=[pl.BlockSpec(memory_sp...  6.8 us
    unnamed x30, local copies, waits for them, and re-layouts  4.56 us
    concatenate x1, other arithmetic, body(): jnp.concatenate([zero_row, hid, zero_row], axis=1)  3.88 us
    another operation x18, local copies, waits for them, and re-layouts, body(): taps = jnp.tile(conv_weight, (1, cols))  3.13 us
    ppermute x1, local copies, waits for them, and re-layouts, swap(): return lax.ppermute(payload, axis, pairs)  2.76 us
  transfers between devices with their start and end apart: 5, of which 0 were waited for; matrix products, arithmetic and copies ran while one was open for 40% of the time, Pallas kernels for 0%

profile of v9, /device:TPU:104, one launch (start us, length us, event | category | flops | bytes accessed | tf_op | source)
XLA Modules:
  0.0 75.6 jit_solution(1997893626842725669)
XLA Ops:
  0.0 1.8 %reshape.133 = bf16[2,32,16,320]{3,2,1,0:T(8,128)(2,1)S(1)} reshape(bf16[2,32,5120]{2,1,0:T(8,128)(2,1)} %param.4) | data formatting | bytes 1310720 | tf_op jit(solution)/shard_map/reshape | solution.py:137
  1.8 0.3 copy.71.own_ref
  2.1 1.9 %collective-permute-start = (bf16[2,320,512]{2,1,0:T(8,128)(2,1)S(1)}, bf16[2,320,512]{2,1,0:T(8,128)(2,1)S(1)}, u32[]{:S(2)}, u32[]{:S(2)}) collective-permute-start(bf16[2,320,512]{2,1,0:T(8,128)(2,1)S(1)} %copy.71.own_ref), channel_id=1, source_target_pairs={{16,32},{32,16},{48,64},{64,48},{80,96},{96,80},{112,128},{128,112... | collective-permute-start | bytes 1966088 | tf_op jit(solution)/shard_map/ppermute | solution.py:117
  4.0 3.3 %collective-permute-start.1 = (bf16[2,320,512]{2,1,0:T(8,128)(2,1)S(1)}, bf16[2,320,512]{2,1,0:T(8,128)(2,1)S(1)}, u32[]{:S(2)}, u32[]{:S(2)}) collective-permute-start(bf16[2,320,512]{2,1,0:T(8,128)(2,1)S(1)} %copy.71.own_ref), channel_id=1, source_target_pairs={{0,16},{16,0},{32,48},{48,32},{64,80},{80,64},{96,112},{112,96},{1... | collective-permute-start | bytes 1966088 | tf_op jit(solution)/shard_map/ppermute | solution.py:117
  7.3 2.2 %copy.73 = bf16[320,960]{0,1:T(8,128)(2,1)} copy(bf16[320,960]{1,0:T(8,128)(2,1)} %param.5) | data formatting | bytes 1228800 | tf_op args[1]
  9.6 1.8 %copy.74 = bf16[320,320]{0,1:T(8,128)(2,1)} copy(bf16[320,320]{1,0:T(8,128)(2,1)} %param.6) | data formatting | bytes 409600 | tf_op args[2]
  11.4 1.0 %slice_reduce_fusion.8 = (f32[320]{0:T(512)S(1)}, f32[320]{0:T(512)S(1)}, f32[320]{0:T(512)S(1)}, f32[320]{0:T(512)S(1)}, f32[320]{0:T(512)S(1)}, /*index=5*/f32...) fusion(f32[9,320]{1,0:T(8,128)} %param.7), kind=kLoop, calls=%fused_computation.41 | loop fusion | bytes 23040 | tf_op jit(solution)/shard_map/slice | solution.py:177
  12.5 0.1 tile.42
  12.5 0.4 copy-done.10
  13.0 0.1 tile.46
  13.1 0.1 tile.54
  13.2 0.1 tile.58
  13.2 0.1 tile.44
  13.3 0.7 tile.56
  14.0 0.7 tile.48
  14.7 0.7 tile.52
  15.4 0.7 tile.50
  16.0 0.6 and_convert_fusion.valid_ref
  16.6 0.0 collective-permute-done.1
  16.6 1.2 %broadcast_select_fusion.2 = (bf16[2,320,512]{2,1,0:T(8,128)(2,1)}, bf16[2,320,512]{2,1,0:T(8,128)(2,1)}) fusion(bf16[2,320,512]{2,1,0:T(8,128)(2,1)S(1)} %collective-permute-done.1, bf16[2,320,512]{2,1,0:T(8,128)(2,1)S(1)} %collective-permute-done, pred[]{:T(512)S(6)} %eq.23), kind=kLoop, calls=%fused_computation.20 | loop fusion | flops 655360 | bytes 2621441 | tf_op jit(solution)/shard_map/jit(_where)/select_n | solution.py:128
  17.8 6.8 %shard_map.46 = bf16[2,320,512]{2,1,0:T(8,128)(2,1)} custom-call(s32[6]{0:T(128)} %and_convert_fusion.valid_ref, bf16[2,320,512]{2,1,0:T(8,128)(2,1)} %get-tuple-element.21.prev_ref, bf16[2,320,512]{2,1,0:T(8,128)(2,1)} %copy-done.2, bf16[2,320,512]{2,1,0:T(8,128)(2,1)} %get-tuple-element.20.next_ref, bf16[960,320]{1,0:T(8,128)(2,1)} %bitcast.17, ...), custom_call_target="tpu_custom_call" | custom-call | tf_op jit(solution)/shard_map/pallas_call | solution.py:82
  24.6 1.4 %copy.76 = bf16[2,320,512]{1,2,0:T(8,128)(2,1)S(1)} copy(bf16[2,320,512]{2,1,0:T(8,128)(2,1)} %shard_map.46) | data formatting | bytes 1310720 | tf_op jit(solution)/shard_map/pallas_call | solution.py:82
  26.1 1.1 %fusion.8 = bf16[2,16,320]{1,2,0:T(8,128)(2,1)S(1)} fusion(bf16[2,320,512]{2,1,0:T(8,128)(2,1)} %shard_map.46, pred[]{:T(512)S(6)} %eq.25), kind=kLoop, calls=%fused_computation.25 | loop fusion | flops 10240 | bytes 61441 | tf_op jit(solution)/shard_map/jit(_where)/select_n | solution.py:116
  27.2 0.1 copy.78
  27.3 0.7 select_n.104
  28.0 3.0 %collective-permute-start.2 = (bf16[2,1,5120]{2,0,1:T(2,128)(2,1)}, bf16[2,1,5120]{2,0,1:T(2,128)(2,1)}, u32[]{:S(2)}, u32[]{:S(2)}) collective-permute-start(bf16[2,1,5120]{2,0,1:T(2,128)(2,1)} %select_n.104), channel_id=1, source_target_pairs={{0,8},{8,0},{1,9},{9,1},{2,10},{10,2},{3,11},{11,3},{4,12},{12,4},... | collective-permute-start | bytes 61448 | tf_op jit(solution)/shard_map/ppermute | solution.py:117
  31.0 1.8 %copy.77 = bf16[2,32,16,320]{1,3,2,0:T(8,128)(2,1)S(1)} copy(bf16[2,32,16,320]{3,2,1,0:T(8,128)(2,1)S(1)} %bitcast.16) | data formatting | bytes 1310720 | tf_op jit(solution)/shard_map/transpose | solution.py:148
  32.9 0.3 broadcast.121
  33.2 3.9 %pad_maximum_fusion.4 = bf16[2,34,5120]{1,2,0:T(8,128)(2,1)} fusion(bf16[2,1,5120]{1,2,0:T(8,128)(2,1)S(1)} %broadcast.121, bf16[2,32,5120]{1,2,0:T(8,128)(2,1)S(1)} %bitcast.13), kind=kLoop, calls=%fused_computation.17 | loop fusion | flops 2088960 | bytes 1372160 | tf_op jit(solution)/shard_map/concatenate | solution.py:167
  37.1 1.7 %slice.211 = bf16[2,320,32]{2,1,0:T(8,128)(2,1)S(1)} slice(bf16[2,320,512]{2,1,0:T(8,128)(2,1)S(1)} %copy-done.1), slice={[0:2:1], [0:320:1], [0:512:16]} | slice | bytes 81920 | tf_op jit(solution)/shard_map/slice | solution.py:155
  38.8 2.3 %slice.214 = bf16[2,320,32]{2,1,0:T(8,128)(2,1)} slice(bf16[2,320,512]{2,1,0:T(8,128)(2,1)S(1)} %copy-done.1), slice={[0:2:1], [0:320:1], [15:512:16]} | slice | bytes 81920 | tf_op jit(solution)/shard_map/slice | solution.py:156
  41.1 0.0 collective-permute-done.2
  41.1 2.8 %copy.79 = bf16[2,1,5120]{1,2,0:T(8,128)(2,1)} copy(bf16[2,1,5120]{2,0,1:T(2,128)(2,1)} %collective-permute-done.2) | data formatting | bytes 40960 | tf_op jit(solution)/shard_map/ppermute | solution.py:117
  43.9 2.2 %broadcast_select_fusion.1 = (bf16[2,1,5120]{1,2,0:T(8,128)(2,1)S(1)}, bf16[2,1,5120]{1,2,0:T(8,128)(2,1)S(1)}) fusion(bf16[2,1,5120]{1,2,0:T(8,128)(2,1)} %copy.79, pred[]{:T(512)S(6)} %eq.25), kind=kLoop, calls=%fused_computation.19 | loop fusion | flops 20480 | bytes 61441 | tf_op jit(solution)/shard_map/jit(_where)/select_n | solution.py:125
  46.2 0.3 broadcast_select_fusion.7
  46.5 2.4 %collective-permute-start.3 = (bf16[2,34,320]{1,2,0:T(8,128)(2,1)S(1)}, bf16[2,34,320]{1,2,0:T(8,128)(2,1)S(1)}, u32[]{:S(2)}, u32[]{:S(2)}) collective-permute-start(bf16[2,34,320]{1,2,0:T(8,128)(2,1)S(1)} %get-tuple-element.22), channel_id=1, source_target_pairs={{1,2},{2,1},{3,4},{4,3},{5,6},{6,5},{9,10},{10,9},{11,12},{12,11},... | collective-permute-start | bytes 130568 | tf_op jit(solution)/shard_map/ppermute | solution.py:117
  49.0 2.7 %collective-permute-start.4 = (bf16[2,34,320]{1,2,0:T(8,128)(2,1)S(1)}, bf16[2,34,320]{1,2,0:T(8,128)(2,1)S(1)}, u32[]{:S(2)}, u32[]{:S(2)}) collective-permute-start(bf16[2,34,320]{1,2,0:T(8,128)(2,1)S(1)} %get-tuple-element.23), channel_id=1, source_target_pairs={{0,1},{1,0},{2,3},{3,2},{4,5},{5,4},{6,7},{7,6},{8,9},{9,8},{10,11... | collective-permute-start | bytes 130568 | tf_op jit(solution)/shard_map/ppermute | solution.py:117
  51.6 11.6 %fusion.7 = f32[2,32,5120]{1,2,0:T(8,128)S(1)} fusion(bf16[2,32,5120]{1,2,0:T(8,128)(2,1)S(1)} %bitcast.14, f32[5120]{0:T(1024)S(1)} %tile.58, f32[5120]{0:T(1024)S(1)} %copy-done.4, f32[5120]{0:T(1024)S(1)} %tile.54, f32[5120]{0:T(1024)S(1)} %copy-done.6, f32[5120]{0:T(1024)S(1)} %copy-done.7, f32[5120]{0:T(1024)S(1)} %copy-done.5, f32[5120]{0:T(1024)S(1)} %tile.46, ...), kind=kLoop, calls=%fused_computation.9 | loop fusion | flops 8847360 | bytes 2846720 | tf_op jit(solution)/shard_map/add | solution.py:173
  63.2 0.0 collective-permute-done.3
  63.2 0.0 collective-permute-done.4
  63.3 0.1 fusion.11
  63.4 0.1 slice.240
  63.5 0.1 fusion.12
  63.6 0.1 slice.241
  63.8 0.5 multiply_add_fusion.2
  64.3 7.3 %multiply_add_fusion = (f32[2,1,5120]{1,2,0:T(8,128)S(1)}, f32[2,1,5120]{1,2,0:T(8,128)S(1)}) fusion(bf16[2,1,5120]{1,2,0:T(8,128)(2,1)S(1)} %get-tuple-element.19, bf16[2,1,320]{1,2,0:T(8,128)(2,1)S(1)} %get-tuple-element.29, bf16[2,1,320]{1,2,0:T(8,128)(2,1)S(1)} %get-tuple-element.27, f32[5120]{0:T(1024)S(1)} %tile.58, f32[5120]{0:T(1024)S(1)} %copy-done.4, ...), kind=kLoop, calls=%fused_computation.11 | loop fusion | flops 286720 | bytes 250880 | tf_op jit(solution)/shard_map/add | solution.py:182
  71.6 1.5 %add_convert_fusion = bf16[2,32,5120]{1,2,0:T(8,128)(2,1)S(1)} fusion(f32[2,32,5120]{1,2,0:T(8,128)S(1)} %fusion.7, f32[2,32,320]{1,2,0:T(8,128)S(1)} %get-tuple-element.30, f32[2,32,320]{1,2,0:T(8,128)S(1)} %get-tuple-element.31, f32[2,1,5120]{1,2,0:T(8,128)S(1)} %get-tuple-element.32, f32[2,1,5120]{1,2,0:T(8,128)S(1)} %get-tuple-element.33), kind=kLoop, calls=%fused_computation.10 | loop fusion | flops 1638400 | bytes 2211840 | tf_op jit(solution)/shard_map/convert_element_type | solution.py:200
  73.2 2.4 %copy.81 = bf16[2,32,5120]{2,1,0:T(8,128)(2,1)} copy(bf16[2,32,5120]{1,2,0:T(8,128)(2,1)S(1)} %add_convert_fusion) | data formatting | bytes 1310720 | tf_op jit(solution)/shard_map/convert_element_type | solution.py:200
  (40 shorter events, 0.2 us)
Async XLA Ops:
  2.0 15.8 %copy-start.2 = (bf16[2,320,512]{2,1,0:T(8,128)(2,1)}, bf16[2,320,512]{2,1,0:T(8,128)(2,1)S(1)}, u32[]{:S(2)}) copy-start(bf16[2,320,512]{2,1,0:T(8,128)(2,1)S(1)} %copy.71.own_ref) | copy-start | bytes 1966084
  2.1 14.6 %collective-permute-start = (bf16[2,320,512]{2,1,0:T(8,128)(2,1)S(1)}, bf16[2,320,512]{2,1,0:T(8,128)(2,1)S(1)}, u32[]{:S(2)}, u32[]{:S(2)}) collective-permute-start(bf16[2,320,512]{2,1,0:T(8,128)(2,1)S(1)} %copy.71.own_ref), channel_id=1, source_target_pairs={{16,32},{32,16},{48,64},{64,48},{80,96},{96,80},{112,128},{128,112... | collective-permute-start | bytes 1966088 | tf_op jit(solution)/shard_map/ppermute | solution.py:117
  4.0 12.6 %collective-permute-start.1 = (bf16[2,320,512]{2,1,0:T(8,128)(2,1)S(1)}, bf16[2,320,512]{2,1,0:T(8,128)(2,1)S(1)}, u32[]{:S(2)}, u32[]{:S(2)}) collective-permute-start(bf16[2,320,512]{2,1,0:T(8,128)(2,1)S(1)} %copy.71.own_ref), channel_id=1, source_target_pairs={{0,16},{16,0},{32,48},{48,32},{64,80},{80,64},{96,112},{112,96},{1... | collective-permute-start | bytes 1966088 | tf_op jit(solution)/shard_map/ppermute | solution.py:117
  12.4 0.6 copy-start.10
  12.4 0.7 copy-start.12
  12.4 18.6 %copy-start.8 = (f32[320]{0:T(512)}, f32[320]{0:T(512)S(1)}, u32[]{:S(2)}) copy-start(f32[320]{0:T(512)S(1)} %get-tuple-element.9) | copy-start | bytes 3844
  28.0 13.1 %collective-permute-start.2 = (bf16[2,1,5120]{2,0,1:T(2,128)(2,1)}, bf16[2,1,5120]{2,0,1:T(2,128)(2,1)}, u32[]{:S(2)}, u32[]{:S(2)}) collective-permute-start(bf16[2,1,5120]{2,0,1:T(2,128)(2,1)} %select_n.104), channel_id=1, source_target_pairs={{0,8},{8,0},{1,9},{9,1},{2,10},{10,2},{3,11},{11,3},{4,12},{12,4},... | collective-permute-start | bytes 61448 | tf_op jit(solution)/shard_map/ppermute | solution.py:117
  32.9 4.2 %copy-start.1 = (bf16[2,320,512]{2,1,0:T(8,128)(2,1)S(1)}, bf16[2,320,512]{2,1,0:T(8,128)(2,1)}, u32[]{:S(2)}) copy-start(bf16[2,320,512]{2,1,0:T(8,128)(2,1)} %shard_map.46) | copy-start | bytes 1966084
  43.9 2.3 %copy-start.3 = (bf16[2,320,32]{2,1,0:T(8,128)(2,1)S(1)}, bf16[2,320,32]{2,1,0:T(8,128)(2,1)}, u32[]{:S(2)}) copy-start(bf16[2,320,32]{2,1,0:T(8,128)(2,1)} %slice.214) | copy-start | bytes 122884
  43.9 7.7 %copy-start = (bf16[2,34,5120]{1,2,0:T(8,128)(2,1)S(1)}, bf16[2,34,5120]{1,2,0:T(8,128)(2,1)}, u32[]{:S(2)}) copy-start(bf16[2,34,5120]{1,2,0:T(8,128)(2,1)} %pad_maximum_fusion.4) | copy-start | bytes 2088964
  43.9 7.7 %copy-start.4 = (f32[5120]{0:T(1024)S(1)}, f32[5120]{0:T(1024)}, u32[]{:S(2)}) copy-start(f32[5120]{0:T(1024)} %tile.56) | copy-start | bytes 61444
  43.9 7.8 %copy-start.5 = (f32[5120]{0:T(1024)S(1)}, f32[5120]{0:T(1024)}, u32[]{:S(2)}) copy-start(f32[5120]{0:T(1024)} %tile.48) | copy-start | bytes 61444
  43.9 7.7 %copy-start.6 = (f32[5120]{0:T(1024)S(1)}, f32[5120]{0:T(1024)}, u32[]{:S(2)}) copy-start(f32[5120]{0:T(1024)} %tile.52) | copy-start | bytes 61444
  43.9 7.7 %copy-start.7 = (f32[5120]{0:T(1024)S(1)}, f32[5120]{0:T(1024)}, u32[]{:S(2)}) copy-start(f32[5120]{0:T(1024)} %tile.50) | copy-start | bytes 61444
  46.5 16.7 %collective-permute-start.3 = (bf16[2,34,320]{1,2,0:T(8,128)(2,1)S(1)}, bf16[2,34,320]{1,2,0:T(8,128)(2,1)S(1)}, u32[]{:S(2)}, u32[]{:S(2)}) collective-permute-start(bf16[2,34,320]{1,2,0:T(8,128)(2,1)S(1)} %get-tuple-element.22), channel_id=1, source_target_pairs={{1,2},{2,1},{3,4},{4,3},{5,6},{6,5},{9,10},{10,9},{11,12},{12,11},... | collective-permute-start | bytes 130568 | tf_op jit(solution)/shard_map/ppermute | solution.py:117
  48.9 14.8 %copy-start.9 = (f32[320]{0:T(512)S(1)}, f32[320]{0:T(512)}, u32[]{:S(2)}) copy-start(f32[320]{0:T(512)} %copy-done.8) | copy-start | bytes 3844
  48.9 14.8 %copy-start.11 = (f32[320]{0:T(512)S(1)}, f32[320]{0:T(512)}, u32[]{:S(2)}) copy-start(f32[320]{0:T(512)} %copy-done.10) | copy-start | bytes 3844
  48.9 14.8 %copy-start.13 = (f32[320]{0:T(512)S(1)}, f32[320]{0:T(512)}, u32[]{:S(2)}) copy-start(f32[320]{0:T(512)} %copy-done.12) | copy-start | bytes 3844
  49.0 14.3 %collective-permute-start.4 = (bf16[2,34,320]{1,2,0:T(8,128)(2,1)S(1)}, bf16[2,34,320]{1,2,0:T(8,128)(2,1)S(1)}, u32[]{:S(2)}, u32[]{:S(2)}) collective-permute-start(bf16[2,34,320]{1,2,0:T(8,128)(2,1)S(1)} %get-tuple-element.23), channel_id=1, source_target_pairs={{0,1},{1,0},{2,3},{3,2},{4,5},{5,4},{6,7},{7,6},{8,9},{9,8},{10,11... | collective-permute-start | bytes 130568 | tf_op jit(solution)/shard_map/ppermute | solution.py:117

commit v10 on v8

--- a/solution.py
+++ b/solution.py
@@ -18,7 +18,17 @@
     return (cent * lax.rsqrt(var + 1e-05)).astype(jnp.bfloat16)
 
 
-def attend_kernel(valid_ref, prev_ref, own_ref, next_ref, wqkv_ref, wout_ref, out_ref):
+def attend_kernel(valid_ref, a_ref, own_ref, b_ref, wqkv_ref, wout_ref, out_ref):
+    @pl.when(valid_ref[6] > 0)
+    def _():
+        attend_body(valid_ref, b_ref, own_ref, a_ref, wqkv_ref, wout_ref, out_ref)
+
+    @pl.when(valid_ref[6] == 0)
+    def _():
+        attend_body(valid_ref, a_ref, own_ref, b_ref, wqkv_ref, wout_ref, out_ref)
+
+
+def attend_body(valid_ref, prev_ref, own_ref, next_ref, wqkv_ref, wout_ref, out_ref):
     chans = wout_ref.shape[0]
     heads = chans // HEAD_DIM
     block = own_ref.shape[2]
@@ -138,12 +148,15 @@
         frames, chans, points
     )
     own_c = cells(latents)
-    x_prev, x_next = exchange(own_c, own_c, "tm")
+    got_a = swap(own_c, own_c, "tm", 0)
+    got_b = swap(own_c, own_c, "tm", 1)
     first = lax.axis_index("tm") * frames
     total = lax.axis_size("tm") * frames
     where_t = first + jnp.arange(6, dtype=jnp.int32) - 2
     valid = ((where_t >= 0) & (where_t < total)).astype(jnp.int32)
-    hidden = attend(valid, x_prev, own_c, x_next, w_qkv, w_out)
+    even = (lax.axis_index("tm") % 2 == 0).astype(jnp.int32)
+    valid = jnp.concatenate([valid, even[None]])
+    hidden = attend(valid, got_a, own_c, got_b, w_qkv, w_out)
     hid = (
         hidden.reshape(frames, chans, rows, cols).transpose(0, 2, 3, 1).reshape(frames, rows, merged)
     )

time: 43.7 us -> 43.7 us (level)
  other arithmetic: 5.53 us -> 4.47 us
  waiting for transfers between devices: 13.5 us -> 14.5 us
  local copies, waits for them, and re-layouts: 6.94 us -> 7.8 us
  starting transfers between devices: 10.5 us -> 9.68 us
    select_n x1 -> x0, other arithmetic: 1.14 us -> none  [exchange(): from_next = jnp.where(even, got_a, got_b)]
    ppermute x5, waiting for transfers between devices: 13.5 us -> 14.5 us  [swap(): return lax.ppermute(payload, axis, pairs)]
    ppermute x5, starting transfers between devices: 10.5 us -> 9.68 us  [swap(): return lax.ppermute(payload, axis, pairs)]
    unnamed x10 -> x14, local copies, waits for them, and re-layouts: 2.04 us -> 2.9 us
    concatenate x0 -> x1, other arithmetic: none -> 0.58 us  [body(): valid = jnp.concatenate([valid, even[None]])]
    convert_element_type x1 -> x0, other arithmetic: 0.51 us -> none  [body(): valid = ((where_t >= 0) & (where_t < total)).astype(jnp.int32)]
where the time goes in v10:
time: 43.7 us; the launch traced here: 43.4 us
  waiting for transfers between devices  14.5 us (33%)
  starting transfers between devices  9.68 us (22%)
  local copies, waits for them, and re-layouts  7.8 us (18%)
  Pallas kernels  6.8 us (16%)
  other arithmetic  4.47 us (10%)
    ppermute x5, waiting for transfers between devices, swap(): return lax.ppermute(payload, axis, pairs)  14.5 us
    ppermute x5, starting transfers between devices, swap(): return lax.ppermute(payload, axis, pairs)  9.68 us
    pallas_call x1, Pallas kernels, attend(): pl.pallas_call(attend_kernel, grid=grid, in_specs=[pl.BlockSpec(memory_sp...  6.8 us
    unnamed x14, local copies, waits for them, and re-layouts  2.9 us
    convert_element_type x1, other arithmetic, body(): return acc.astype(jnp.bfloat16)  2.85 us
    reshape x2, local copies, waits for them, and re-layouts, body(): a.reshape(frames, rows, cols, chans).transpose(0, 3, 1, 2)  2.03 us
    pallas_call x1, local copies, waits for them, and re-layouts, attend(): pl.pallas_call(attend_kernel, grid=grid, in_specs=[pl.BlockSpec(memory_sp...  1.44 us
  transfers between devices with their start and end apart: 5, of which 3 were waited for; matrix products, arithmetic and copies ran while one was open for 8% of the time, Pallas kernels for 0%

profile of v10, /device:TPU:152, one launch (start us, length us, event | category | flops | bytes accessed | tf_op | source)
XLA Modules:
  0.0 43.4 jit_solution(17905882487849807846)
XLA Ops:
  0.0 1.8 %reshape.60 = bf16[2,32,16,320]{3,2,1,0:T(8,128)(2,1)S(1)} reshape(bf16[2,32,5120]{2,1,0:T(8,128)(2,1)} %param.4) | data formatting | bytes 1310720 | tf_op jit(solution)/shard_map/reshape | solution.py:147
  1.8 0.0 copy-start.1
  1.8 0.3 copy.9.own_ref
  2.1 0.0 copy-start
  2.1 0.0 copy-start.4
  2.1 0.1 collective-permute-start
  2.2 2.1 %collective-permute-start.1 = (bf16[2,320,512]{2,1,0:T(8,128)(2,1)S(1)}, bf16[2,320,512]{2,1,0:T(8,128)(2,1)S(1)}, u32[]{:S(2)}, u32[]{:S(2)}) collective-permute-start(bf16[2,320,512]{2,1,0:T(8,128)(2,1)S(1)} %copy.9.own_ref), channel_id=1, source_target_pairs={{16,32},{32,16},{48,64},{64,48},{80,96},{96,80},{112,128},{128,112... | collective-permute-start | bytes 1966088 | tf_op jit(solution)/shard_map/ppermute | solution.py:127
  4.3 0.0 copy-done.1
  4.3 1.2 %copy.11 = bf16[320,960]{0,1:T(8,128)(2,1)} copy(bf16[320,960]{1,0:T(8,128)(2,1)S(1)} %copy-done.1) | data formatting | bytes 1228800 | tf_op args[1]
  5.5 0.0 copy-done.4
  5.5 0.9 %copy.12 = bf16[320,320]{0,1:T(8,128)(2,1)} copy(bf16[320,320]{1,0:T(8,128)(2,1)S(1)} %copy-done.4) | data formatting | bytes 409600 | tf_op args[2]
  6.3 0.0 copy-done
  6.4 0.6 %add_convert_fusion.valid_ref = s32[7]{0:T(128)} fusion(pred[1]{0:T(512)(128)(4,1)} %bitcast, pred[6]{0:T(512)(128)(4,1)S(1)} %compare_and_fusion), kind=kLoop, calls=%fused_computation.25 | loop fusion | flops 14 | bytes 35 | tf_op jit(solution)/shard_map/concatenate | solution.py:158
  6.9 0.0 collective-permute-done.a_ref
  6.9 0.0 copy-start.2
  6.9 8.5 %collective-permute-done.1.b_ref = bf16[2,320,512]{2,1,0:T(8,128)(2,1)S(1)} collective-permute-done((bf16[2,320,512]{2,1,0:T(8,128)(2,1)S(1)}, bf16[2,320,512]{2,1,0:T(8,128)(2,1)S(1)}, u32[]{:S(2)}, u32[]{:S(2)}) %collective-permute-start.1) | collective-permute-done | bytes 655392 | tf_op jit(solution)/shard_map/ppermute | solution.py:127
  15.4 0.0 copy-start.3
  15.4 0.0 copy-done.2
  15.4 0.9 %copy-done.3 = bf16[2,320,512]{2,1,0:T(8,128)(2,1)} copy-done((bf16[2,320,512]{2,1,0:T(8,128)(2,1)}, bf16[2,320,512]{2,1,0:T(8,128)(2,1)S(1)}, u32[]{:S(2)}) %copy-start.3) | copy-done | bytes 655384
  16.3 6.8 %shard_map.46 = bf16[2,320,512]{2,1,0:T(8,128)(2,1)} custom-call(s32[7]{0:T(128)} %add_convert_fusion.valid_ref, bf16[2,320,512]{2,1,0:T(8,128)(2,1)} %copy-done.2, bf16[2,320,512]{2,1,0:T(8,128)(2,1)} %copy-done, bf16[2,320,512]{2,1,0:T(8,128)(2,1)} %copy-done.3, bf16[960,320]{1,0:T(8,128)(2,1)} %bitcast.13, bf16[320,320]{1,0:T(8,128)(2,1)} %bitcast.14), custom_call_target="tpu_custom_call" | custom-call | tf_op jit(solution)/shard_map/pallas_call | solution.py:92
  23.1 1.4 %copy.14 = bf16[2,320,512]{1,2,0:T(8,128)(2,1)S(1)} copy(bf16[2,320,512]{2,1,0:T(8,128)(2,1)} %shard_map.46) | data formatting | bytes 1310720 | tf_op jit(solution)/shard_map/pallas_call | solution.py:92
  24.5 0.6 %reshape.63 = bf16[2,32,5120]{2,1,0:T(8,128)(2,1)S(1)} reshape(bf16[2,32,16,320]{3,2,1,0:T(8,128)(2,1)S(1)} %bitcast.11) | data formatting | bytes 1310720 | tf_op jit(solution)/shard_map/reshape | solution.py:161
  25.2 0.0 copy-start.5
  25.2 0.1 broadcast_select_fusion.2
  25.3 3.1 %collective-permute-start.2 = (bf16[2,1,5120]{2,1,0:T(2,128)(2,1)S(1)}, bf16[2,1,5120]{2,1,0:T(2,128)(2,1)S(1)}, u32[]{:S(2)}, u32[]{:S(2)}) collective-permute-start(bf16[2,1,5120]{2,1,0:T(2,128)(2,1)S(1)} %broadcast_select_fusion.2), channel_id=1, source_target_pairs={{0,8},{8,0},{1,9},{9,1},{2,10},{10,2},{3,11},{11,3},{4,12},{12,4},... | collective-permute-start | bytes 61448 | tf_op jit(solution)/shard_map/ppermute | solution.py:127
  28.4 2.5 %collective-permute-done.2 = bf16[2,1,5120]{2,1,0:T(2,128)(2,1)S(1)} collective-permute-done((bf16[2,1,5120]{2,1,0:T(2,128)(2,1)S(1)}, bf16[2,1,5120]{2,1,0:T(2,128)(2,1)S(1)}, u32[]{:S(2)}, u32[]{:S(2)}) %collective-permute-start.2) | collective-permute-done | bytes 20512 | tf_op jit(solution)/shard_map/ppermute | solution.py:127
  30.9 0.1 broadcast_select_fusion.1
  30.9 0.1 broadcast_select_fusion.6
  31.1 1.8 %collective-permute-start.4 = (bf16[2,34,320]{2,1,0:T(8,128)(2,1)S(1)}, bf16[2,34,320]{2,1,0:T(8,128)(2,1)S(1)}, u32[]{:S(2)}, u32[]{:S(2)}) collective-permute-start(bf16[2,34,320]{2,1,0:T(8,128)(2,1)S(1)} %broadcast_select_fusion.5), channel_id=1, source_target_pairs={{0,1},{1,0},{2,3},{3,2},{4,5},{5,4},{6,7},{7,6},{8,9},{9,8},{10,11... | collective-permute-start | bytes 130568 | tf_op jit(solution)/shard_map/ppermute | solution.py:127
  32.8 2.6 %collective-permute-start.3 = (bf16[2,34,320]{2,1,0:T(8,128)(2,1)S(1)}, bf16[2,34,320]{2,1,0:T(8,128)(2,1)S(1)}, u32[]{:S(2)}, u32[]{:S(2)}) collective-permute-start(bf16[2,34,320]{2,1,0:T(8,128)(2,1)S(1)} %get-tuple-element.14), channel_id=1, source_target_pairs={{1,2},{2,1},{3,4},{4,3},{5,6},{6,5},{9,10},{10,9},{11,12},{12,11},... | collective-permute-start | bytes 130568 | tf_op jit(solution)/shard_map/ppermute | solution.py:127
  35.4 0.0 copy-done.5
  35.4 0.1 slice_reduce_fusion.8
  35.5 0.1 tile.42
  35.6 0.1 tile.44
  35.7 0.1 tile.46
  35.8 0.1 tile.48
  35.8 0.1 tile.50
  35.9 0.1 tile.52
  36.0 0.1 tile.54
  36.1 0.1 tile.56
  36.2 0.1 tile.58
  36.3 0.0 collective-permute-done.4
  36.3 3.6 %collective-permute-done.3 = bf16[2,34,320]{2,1,0:T(8,128)(2,1)S(1)} collective-permute-done((bf16[2,34,320]{2,1,0:T(8,128)(2,1)S(1)}, bf16[2,34,320]{2,1,0:T(8,128)(2,1)S(1)}, u32[]{:S(2)}, u32[]{:S(2)}) %collective-permute-start.3) | collective-permute-done | bytes 43552 | tf_op jit(solution)/shard_map/ppermute | solution.py:127
  39.8 0.8 %maximum_maximum_fusion = (bf16[2,34,5440]{2,1,0:T(8,128)(2,1)S(1)}, bf16[2,34,5440]{2,1,0:T(8,128)(2,1)S(1)}) fusion(bf16[2,1,5120]{2,1,0:T(2,128)(2,1)S(1)} %get-tuple-element.22, bf16[2,32,5120]{2,1,0:T(8,128)(2,1)S(1)} %reshape.63, bf16[2,1,5120]{2,1,0:T(2,128)(2,1)S(1)} %get-tuple-element.21, bf16[2,34,320]{2,1,0:T(8,128)(2,1)S(1)} %get-tuple-element.19, ...), kind=kLoop, calls=%fused_computation.11 | loop fusion | flops 5918720 | bytes 2263040 | tf_op jit(solution)/shard_map/concatenate | solution.py:167
  40.6 2.8 %fusion.8 = bf16[2,32,5120]{2,1,0:T(8,128)(2,1)} fusion(bf16[2,32,5120]{2,1,0:T(8,128)(2,1)S(1)} %reshape.63, bf16[2,34,5440]{2,1,0:T(8,128)(2,1)S(1)} %get-tuple-element.18, bf16[2,1,5120]{2,1,0:T(2,128)(2,1)S(1)} %get-tuple-element.22, bf16[2,34,5440]{2,1,0:T(8,128)(2,1)S(1)} %get-tuple-element.17, bf16[2,1,5120]{2,1,0:T(2,128)(2,1)S(1)} %get-tuple-element.21, ...), kind=kLoop, calls=%fused_computation.10 | loop fusion | flops 11141120 | bytes 5468160 | tf_op jit(solution)/shard_map/convert_element_type | solution.py:179
  (12 shorter events, 0.1 us)
Async XLA Ops:
  1.8 2.6 %copy-start.1 = (bf16[320,960]{1,0:T(8,128)(2,1)S(1)}, bf16[320,960]{1,0:T(8,128)(2,1)}, u32[]{:S(2)}) copy-start(bf16[320,960]{1,0:T(8,128)(2,1)} %param.5) | copy-start | bytes 1843204
  2.1 4.3 %copy-start = (bf16[2,320,512]{2,1,0:T(8,128)(2,1)}, bf16[2,320,512]{2,1,0:T(8,128)(2,1)S(1)}, u32[]{:S(2)}) copy-start(bf16[2,320,512]{2,1,0:T(8,128)(2,1)S(1)} %copy.9.own_ref) | copy-start | bytes 1966084
  2.1 3.4 %copy-start.4 = (bf16[320,320]{1,0:T(8,128)(2,1)S(1)}, bf16[320,320]{1,0:T(8,128)(2,1)}, u32[]{:S(2)}) copy-start(bf16[320,320]{1,0:T(8,128)(2,1)} %param.6) | copy-start | bytes 614404
  2.1 4.9 %collective-permute-start = (bf16[2,320,512]{2,1,0:T(8,128)(2,1)S(1)}, bf16[2,320,512]{2,1,0:T(8,128)(2,1)S(1)}, u32[]{:S(2)}, u32[]{:S(2)}) collective-permute-start(bf16[2,320,512]{2,1,0:T(8,128)(2,1)S(1)} %copy.9.own_ref), channel_id=1, source_target_pairs={{0,16},{16,0},{32,48},{48,32},{64,80},{80,64},{96,112},{112,96},{1... | collective-permute-start | bytes 1966088 | tf_op jit(solution)/shard_map/ppermute | solution.py:127
  2.2 13.2 %collective-permute-start.1 = (bf16[2,320,512]{2,1,0:T(8,128)(2,1)S(1)}, bf16[2,320,512]{2,1,0:T(8,128)(2,1)S(1)}, u32[]{:S(2)}, u32[]{:S(2)}) collective-permute-start(bf16[2,320,512]{2,1,0:T(8,128)(2,1)S(1)} %copy.9.own_ref), channel_id=1, source_target_pairs={{16,32},{32,16},{48,64},{64,48},{80,96},{96,80},{112,128},{128,112... | collective-permute-start | bytes 1966088 | tf_op jit(solution)/shard_map/ppermute | solution.py:127
  6.9 8.5 %copy-start.2 = (bf16[2,320,512]{2,1,0:T(8,128)(2,1)}, bf16[2,320,512]{2,1,0:T(8,128)(2,1)S(1)}, u32[]{:S(2)}) copy-start(bf16[2,320,512]{2,1,0:T(8,128)(2,1)S(1)} %collective-permute-done.a_ref) | copy-start | bytes 1966084
  15.4 0.9 %copy-start.3 = (bf16[2,320,512]{2,1,0:T(8,128)(2,1)}, bf16[2,320,512]{2,1,0:T(8,128)(2,1)S(1)}, u32[]{:S(2)}) copy-start(bf16[2,320,512]{2,1,0:T(8,128)(2,1)S(1)} %collective-permute-done.1.b_ref) | copy-start | bytes 1966084
  25.2 10.3 %copy-start.5 = (f32[9,320]{1,0:T(8,128)S(1)}, f32[9,320]{1,0:T(8,128)}, u32[]{:S(2)}) copy-start(f32[9,320]{1,0:T(8,128)} %param.7) | copy-start | bytes 34564
  25.3 5.6 %collective-permute-start.2 = (bf16[2,1,5120]{2,1,0:T(2,128)(2,1)S(1)}, bf16[2,1,5120]{2,1,0:T(2,128)(2,1)S(1)}, u32[]{:S(2)}, u32[]{:S(2)}) collective-permute-start(bf16[2,1,5120]{2,1,0:T(2,128)(2,1)S(1)} %broadcast_select_fusion.2), channel_id=1, source_target_pairs={{0,8},{8,0},{1,9},{9,1},{2,10},{10,2},{3,11},{11,3},{4,12},{12,4},... | collective-permute-start | bytes 61448 | tf_op jit(solution)/shard_map/ppermute | solution.py:127
  31.1 5.2 %collective-permute-start.4 = (bf16[2,34,320]{2,1,0:T(8,128)(2,1)S(1)}, bf16[2,34,320]{2,1,0:T(8,128)(2,1)S(1)}, u32[]{:S(2)}, u32[]{:S(2)}) collective-permute-start(bf16[2,34,320]{2,1,0:T(8,128)(2,1)S(1)} %broadcast_select_fusion.5), channel_id=1, source_target_pairs={{0,1},{1,0},{2,3},{3,2},{4,5},{5,4},{6,7},{7,6},{8,9},{9,8},{10,11... | collective-permute-start | bytes 130568 | tf_op jit(solution)/shard_map/ppermute | solution.py:127
  32.8 7.0 %collective-permute-start.3 = (bf16[2,34,320]{2,1,0:T(8,128)(2,1)S(1)}, bf16[2,34,320]{2,1,0:T(8,128)(2,1)S(1)}, u32[]{:S(2)}, u32[]{:S(2)}) collective-permute-start(bf16[2,34,320]{2,1,0:T(8,128)(2,1)S(1)} %get-tuple-element.14), channel_id=1, source_target_pairs={{1,2},{2,1},{3,4},{4,3},{5,6},{6,5},{9,10},{10,9},{11,12},{12,11},... | collective-permute-start | bytes 130568 | tf_op jit(solution)/shard_map/ppermute | solution.py:127

commit v11 on v10

--- a/solution.py
+++ b/solution.py
@@ -18,21 +18,24 @@
     return (cent * lax.rsqrt(var + 1e-05)).astype(jnp.bfloat16)
 
 
-def attend_kernel(valid_ref, a_ref, own_ref, b_ref, wqkv_ref, wout_ref, out_ref):
+def attend_kernel(valid_ref, a_ref, own_ref, b0_ref, b1_ref, wqkv_ref, wout_ref, out_ref):
+    near = [a_ref.at[0], a_ref.at[1]]
+    far = [b0_ref.at[0], b1_ref.at[0]]
+
     @pl.when(valid_ref[6] > 0)
     def _():
-        attend_body(valid_ref, b_ref, own_ref, a_ref, wqkv_ref, wout_ref, out_ref)
+        attend_body(valid_ref, far, own_ref, near, wqkv_ref, wout_ref, out_ref)
 
     @pl.when(valid_ref[6] == 0)
     def _():
-        attend_body(valid_ref, a_ref, own_ref, b_ref, wqkv_ref, wout_ref, out_ref)
+        attend_body(valid_ref, near, own_ref, far, wqkv_ref, wout_ref, out_ref)
 
 
-def attend_body(valid_ref, prev_ref, own_ref, next_ref, wqkv_ref, wout_ref, out_ref):
+def attend_body(valid_ref, prev_refs, own_ref, next_refs, wqkv_ref, wout_ref, out_ref):
     chans = wout_ref.shape[0]
     heads = chans // HEAD_DIM
     block = own_ref.shape[2]
-    frames = [prev_ref[0], prev_ref[1], own_ref[0], own_ref[1], next_ref[0], next_ref[1]]
+    frames = [prev_refs[0][...], prev_refs[1][...], own_ref[0], own_ref[1], next_refs[0][...], next_refs[1][...]]
     normed = [layer_norm_t(f.astype(jnp.float32)) for f in frames]
     own_n = jnp.concatenate([normed[2], normed[3]], axis=1)
     qkv = jnp.dot(wqkv_ref[...], own_n, preferred_element_type=jnp.float32).astype(jnp.bfloat16)
@@ -81,11 +84,12 @@
     out_ref[1] = hidden[:, block:]
 
 
-def attend(valid, prev, own, nxt, w_qkv, w_out):
+def attend(valid, prev, own, nxt0, nxt1, w_qkv, w_out):
     frames, chans, points = own.shape
     grid = (points // BLOCK,)
     assert points % BLOCK == 0
     cell_spec = pl.BlockSpec((frames, chans, BLOCK), lambda i: (0, 0, i))
+    frame_spec = pl.BlockSpec((1, chans, BLOCK), lambda i: (0, 0, i))
     full = lambda shape: pl.BlockSpec(shape, lambda i: (0, 0))
     w_qkv = w_qkv.T
     w_out = w_out.T
@@ -96,13 +100,14 @@
             pl.BlockSpec(memory_space=pltpu.SMEM),
             cell_spec,
             cell_spec,
-            cell_spec,
+            frame_spec,
+            frame_spec,
             full(w_qkv.shape),
             full(w_out.shape),
         ],
         out_specs=cell_spec,
         out_shape=jax.ShapeDtypeStruct(own.shape, jnp.bfloat16),
-    )(valid, prev, own, nxt, w_qkv, w_out)
+    )(valid, prev, own, nxt0, nxt1, w_qkv, w_out)
 
 
 def shift(x, axis, step):
@@ -149,14 +154,15 @@
     )
     own_c = cells(latents)
     got_a = swap(own_c, own_c, "tm", 0)
-    got_b = swap(own_c, own_c, "tm", 1)
+    got_b0 = swap(own_c[:1], own_c[:1], "tm", 1)
+    got_b1 = swap(own_c[1:], own_c[1:], "tm", 1)
     first = lax.axis_index("tm") * frames
     total = lax.axis_size("tm") * frames
     where_t = first + jnp.arange(6, dtype=jnp.int32) - 2
     valid = ((where_t >= 0) & (where_t < total)).astype(jnp.int32)
     even = (lax.axis_index("tm") % 2 == 0).astype(jnp.int32)
     valid = jnp.concatenate([valid, even[None]])
-    hidden = attend(valid, got_a, own_c, got_b, w_qkv, w_out)
+    hidden = attend(valid, got_a, own_c, got_b0, got_b1, w_qkv, w_out)
     hid = (
         hidden.reshape(frames, chans, rows, cols).transpose(0, 2, 3, 1).reshape(frames, rows, merged)
     )

time: 43.7 us -> 44.4 us (1.016)
  waiting for transfers between devices: 14.5 us -> 8.61 us
  starting transfers between devices: 9.68 us -> 14.3 us
  local copies, waits for them, and re-layouts: 7.8 us -> 9.68 us
    ppermute x5 -> x6, waiting for transfers between devices: 14.5 us -> 8.61 us  [swap(): return lax.ppermute(payload, axis, pairs)]
    ppermute x5 -> x6, starting transfers between devices: 9.68 us -> 14.3 us  [swap(): return lax.ppermute(payload, axis, pairs)]
    unnamed x14, local copies, waits for them, and re-layouts: 2.9 us -> 4.35 us
  transfers between devices with their start and end apart: 5 -> 6, of which waited for: 3 -> 3; matrix products, arithmetic and copies ran while one was open for 8% -> 11% of each run, Pallas kernels for 0% -> 0%
where the time goes in v11:
time: 44.4 us; the launch traced here: 44.1 us
  starting transfers between devices  14.3 us (32%)
  local copies, waits for them, and re-layouts  9.68 us (22%)
  waiting for transfers between devices  8.61 us (19%)
  Pallas kernels  6.82 us (15%)
  other arithmetic  4.47 us (10%)
    ppermute x6, starting transfers between devices, swap(): return lax.ppermute(payload, axis, pairs)  14.3 us
    ppermute x6, waiting for transfers between devices, swap(): return lax.ppermute(payload, axis, pairs)  8.61 us
    pallas_call x1, Pallas kernels, attend(): pl.pallas_call(attend_kernel, grid=grid, in_specs=[pl.BlockSpec(memory_sp...  6.82 us
    unnamed x14, local copies, waits for them, and re-layouts  4.35 us
    convert_element_type x1, other arithmetic, body(): return acc.astype(jnp.bfloat16)  2.85 us
    reshape x2, local copies, waits for them, and re-layouts, body(): a.reshape(frames, rows, cols, chans).transpose(0, 3, 1, 2)  2.03 us
    pallas_call x1, local copies, waits for them, and re-layouts, attend(): pl.pallas_call(attend_kernel, grid=grid, in_specs=[pl.BlockSpec(memory_sp...  1.44 us
  transfers between devices with their start and end apart: 6, of which 3 were waited for; matrix products, arithmetic and copies ran while one was open for 11% of the time, Pallas kernels for 0%

profile of v11, /device:TPU:152, one launch (start us, length us, event | category | flops | bytes accessed | tf_op | source)
XLA Modules:
  0.0 44.1 jit_solution(9951565118381082253)
XLA Ops:
  0.0 1.8 %reshape.62 = bf16[2,32,16,320]{3,2,1,0:T(8,128)(2,1)S(1)} reshape(bf16[2,32,5120]{2,1,0:T(8,128)(2,1)} %param.4) | data formatting | bytes 1310720 | tf_op jit(solution)/shard_map/reshape | solution.py:152
  1.8 0.3 copy.9.own_ref
  2.0 0.0 copy-start
  2.1 0.1 collective-permute-start
  2.2 0.1 fusion.9
  2.2 0.0 copy-start.1
  2.3 0.2 copy.10
  2.4 0.4 %copy-done = bf16[2,320,512]{2,1,0:T(8,128)(2,1)} copy-done((bf16[2,320,512]{2,1,0:T(8,128)(2,1)}, bf16[2,320,512]{2,1,0:T(8,128)(2,1)S(1)}, u32[]{:S(2)}) %copy-start) | copy-done | bytes 655384
  2.9 1.9 %collective-permute-start.1 = (bf16[1,320,512]{2,1,0:T(8,128)(2,1)S(1)}, bf16[1,320,512]{2,1,0:T(8,128)(2,1)S(1)}, u32[]{:S(2)}, u32[]{:S(2)}) collective-permute-start(bf16[1,320,512]{2,1,0:T(8,128)(2,1)S(1)} %copy.10), channel_id=1, source_target_pairs={{16,32},{32,16},{48,64},{64,48},{80,96},{96,80},{112,128},{128,112... | collective-permute-start | bytes 983048 | tf_op jit(solution)/shard_map/ppermute | solution.py:132
  4.8 0.2 copy.11
  5.0 4.9 %collective-permute-start.2 = (bf16[1,320,512]{2,1,0:T(8,128)(2,1)S(1)}, bf16[1,320,512]{2,1,0:T(8,128)(2,1)S(1)}, u32[]{:S(2)}, u32[]{:S(2)}) collective-permute-start(bf16[1,320,512]{2,1,0:T(8,128)(2,1)S(1)} %copy.11), channel_id=1, source_target_pairs={{16,32},{32,16},{48,64},{64,48},{80,96},{96,80},{112,128},{128,112... | collective-permute-start | bytes 983048 | tf_op jit(solution)/shard_map/ppermute | solution.py:132
  9.9 0.0 copy-done.1
  9.9 1.2 %copy.12 = bf16[320,960]{0,1:T(8,128)(2,1)} copy(bf16[320,960]{1,0:T(8,128)(2,1)S(1)} %copy-done.1) | data formatting | bytes 1228800 | tf_op args[1]
  11.0 1.8 %copy.13 = bf16[320,320]{0,1:T(8,128)(2,1)} copy(bf16[320,320]{1,0:T(8,128)(2,1)} %param.6) | data formatting | bytes 409600 | tf_op args[2]
  12.8 0.6 %add_convert_fusion.valid_ref = s32[7]{0:T(128)} fusion(pred[1]{0:T(512)(128)(4,1)} %bitcast, pred[6]{0:T(512)(128)(4,1)S(1)} %compare_and_fusion), kind=kLoop, calls=%fused_computation.25 | loop fusion | flops 14 | bytes 35 | tf_op jit(solution)/shard_map/concatenate | solution.py:164
  13.4 0.0 collective-permute-done.1.b0_ref
  13.4 0.0 copy-start.3
  13.4 2.6 %collective-permute-done.2.b1_ref = bf16[1,320,512]{2,1,0:T(8,128)(2,1)S(1)} collective-permute-done((bf16[1,320,512]{2,1,0:T(8,128)(2,1)S(1)}, bf16[1,320,512]{2,1,0:T(8,128)(2,1)S(1)}, u32[]{:S(2)}, u32[]{:S(2)}) %collective-permute-start.2) | collective-permute-done | bytes 327712 | tf_op jit(solution)/shard_map/ppermute | solution.py:132
  16.0 0.0 collective-permute-done.a_ref
  16.0 0.0 copy-done.3
  16.0 0.7 %copy-done.4 = bf16[1,320,512]{2,1,0:T(8,128)(2,1)} copy-done((bf16[1,320,512]{2,1,0:T(8,128)(2,1)}, bf16[1,320,512]{2,1,0:T(8,128)(2,1)S(1)}, u32[]{:S(2)}) %copy-start.4) | copy-done | bytes 327704
  16.7 0.2 copy-done.2
  16.9 6.8 %shard_map.46 = bf16[2,320,512]{2,1,0:T(8,128)(2,1)} custom-call(s32[7]{0:T(128)} %add_convert_fusion.valid_ref, bf16[2,320,512]{2,1,0:T(8,128)(2,1)} %copy-done.2, bf16[2,320,512]{2,1,0:T(8,128)(2,1)} %copy-done, bf16[1,320,512]{2,1,0:T(8,128)(2,1)} %copy-done.3, bf16[1,320,512]{2,1,0:T(8,128)(2,1)} %copy-done.4, bf16[960,320]{1,0:T(8,128)(2,1)} %bitcast.16, ...), custom_call_target="tpu_custom_call" | custom-call | tf_op jit(solution)/shard_map/pallas_call | solution.py:96
  23.7 1.4 %copy.15 = bf16[2,320,512]{1,2,0:T(8,128)(2,1)S(1)} copy(bf16[2,320,512]{2,1,0:T(8,128)(2,1)} %shard_map.46) | data formatting | bytes 1310720 | tf_op jit(solution)/shard_map/pallas_call | solution.py:96
  25.2 0.6 %reshape.65 = bf16[2,32,5120]{2,1,0:T(8,128)(2,1)S(1)} reshape(bf16[2,32,16,320]{3,2,1,0:T(8,128)(2,1)S(1)} %bitcast.15) | data formatting | bytes 1310720 | tf_op jit(solution)/shard_map/reshape | solution.py:167
  25.8 0.0 copy-start.5
  25.8 0.1 broadcast_select_fusion.2
  25.9 3.3 %collective-permute-start.3 = (bf16[2,1,5120]{2,1,0:T(2,128)(2,1)S(1)}, bf16[2,1,5120]{2,1,0:T(2,128)(2,1)S(1)}, u32[]{:S(2)}, u32[]{:S(2)}) collective-permute-start(bf16[2,1,5120]{2,1,0:T(2,128)(2,1)S(1)} %broadcast_select_fusion.2), channel_id=1, source_target_pairs={{0,8},{8,0},{1,9},{9,1},{2,10},{10,2},{3,11},{11,3},{4,12},{12,4},... | collective-permute-start | bytes 61448 | tf_op jit(solution)/shard_map/ppermute | solution.py:132
  29.2 2.5 %collective-permute-done.3 = bf16[2,1,5120]{2,1,0:T(2,128)(2,1)S(1)} collective-permute-done((bf16[2,1,5120]{2,1,0:T(2,128)(2,1)S(1)}, bf16[2,1,5120]{2,1,0:T(2,128)(2,1)S(1)}, u32[]{:S(2)}, u32[]{:S(2)}) %collective-permute-start.3) | collective-permute-done | bytes 20512 | tf_op jit(solution)/shard_map/ppermute | solution.py:132
  31.7 0.1 broadcast_select_fusion.1
  31.8 0.1 broadcast_select_fusion.6
  31.9 1.6 %collective-permute-start.5 = (bf16[2,34,320]{2,1,0:T(8,128)(2,1)S(1)}, bf16[2,34,320]{2,1,0:T(8,128)(2,1)S(1)}, u32[]{:S(2)}, u32[]{:S(2)}) collective-permute-start(bf16[2,34,320]{2,1,0:T(8,128)(2,1)S(1)} %broadcast_select_fusion.5), channel_id=1, source_target_pairs={{0,1},{1,0},{2,3},{3,2},{4,5},{5,4},{6,7},{7,6},{8,9},{9,8},{10,11... | collective-permute-start | bytes 130568 | tf_op jit(solution)/shard_map/ppermute | solution.py:132
  33.5 2.6 %collective-permute-start.4 = (bf16[2,34,320]{2,1,0:T(8,128)(2,1)S(1)}, bf16[2,34,320]{2,1,0:T(8,128)(2,1)S(1)}, u32[]{:S(2)}, u32[]{:S(2)}) collective-permute-start(bf16[2,34,320]{2,1,0:T(8,128)(2,1)S(1)} %get-tuple-element.14), channel_id=1, source_target_pairs={{1,2},{2,1},{3,4},{4,3},{5,6},{6,5},{9,10},{10,9},{11,12},{12,11},... | collective-permute-start | bytes 130568 | tf_op jit(solution)/shard_map/ppermute | solution.py:132
  36.1 0.0 copy-done.5
  36.1 0.1 slice_reduce_fusion.8
  36.2 0.1 tile.42
  36.3 0.1 tile.44
  36.3 0.1 tile.46
  36.4 0.1 tile.48
  36.5 0.1 tile.50
  36.6 0.1 tile.52
  36.7 0.1 tile.54
  36.8 0.1 tile.56
  36.8 0.1 tile.58
  36.9 0.0 collective-permute-done.5
  36.9 3.6 %collective-permute-done.4 = bf16[2,34,320]{2,1,0:T(8,128)(2,1)S(1)} collective-permute-done((bf16[2,34,320]{2,1,0:T(8,128)(2,1)S(1)}, bf16[2,34,320]{2,1,0:T(8,128)(2,1)S(1)}, u32[]{:S(2)}, u32[]{:S(2)}) %collective-permute-start.4) | collective-permute-done | bytes 43552 | tf_op jit(solution)/shard_map/ppermute | solution.py:132
  40.5 0.8 %maximum_maximum_fusion = (bf16[2,34,5440]{2,1,0:T(8,128)(2,1)S(1)}, bf16[2,34,5440]{2,1,0:T(8,128)(2,1)S(1)}) fusion(bf16[2,1,5120]{2,1,0:T(2,128)(2,1)S(1)} %get-tuple-element.24, bf16[2,32,5120]{2,1,0:T(8,128)(2,1)S(1)} %reshape.65, bf16[2,1,5120]{2,1,0:T(2,128)(2,1)S(1)} %get-tuple-element.23, bf16[2,34,320]{2,1,0:T(8,128)(2,1)S(1)} %get-tuple-element.21, ...), kind=kLoop, calls=%fused_computation.11 | loop fusion | flops 5918720 | bytes 2263040 | tf_op jit(solution)/shard_map/concatenate | solution.py:173
  41.3 2.8 %fusion.8 = bf16[2,32,5120]{2,1,0:T(8,128)(2,1)} fusion(bf16[2,32,5120]{2,1,0:T(8,128)(2,1)S(1)} %reshape.65, bf16[2,34,5440]{2,1,0:T(8,128)(2,1)S(1)} %get-tuple-element.20, bf16[2,1,5120]{2,1,0:T(2,128)(2,1)S(1)} %get-tuple-element.24, bf16[2,34,5440]{2,1,0:T(8,128)(2,1)S(1)} %get-tuple-element.19, bf16[2,1,5120]{2,1,0:T(2,128)(2,1)S(1)} %get-tuple-element.23, ...), kind=kLoop, calls=%fused_computation.10 | loop fusion | flops 11141120 | bytes 5468160 | tf_op jit(solution)/shard_map/convert_element_type | solution.py:185
  (14 shorter events, 0.1 us)
Async XLA Ops:
  2.0 0.8 %copy-start = (bf16[2,320,512]{2,1,0:T(8,128)(2,1)}, bf16[2,320,512]{2,1,0:T(8,128)(2,1)S(1)}, u32[]{:S(2)}) copy-start(bf16[2,320,512]{2,1,0:T(8,128)(2,1)S(1)} %copy.9.own_ref) | copy-start | bytes 1966084
  2.1 13.9 %collective-permute-start = (bf16[2,320,512]{2,1,0:T(8,128)(2,1)S(1)}, bf16[2,320,512]{2,1,0:T(8,128)(2,1)S(1)}, u32[]{:S(2)}, u32[]{:S(2)}) collective-permute-start(bf16[2,320,512]{2,1,0:T(8,128)(2,1)S(1)} %copy.9.own_ref), channel_id=1, source_target_pairs={{0,16},{16,0},{32,48},{48,32},{64,80},{80,64},{96,112},{112,96},{1... | collective-permute-start | bytes 1966088 | tf_op jit(solution)/shard_map/ppermute | solution.py:132
  2.2 7.6 %copy-start.1 = (bf16[320,960]{1,0:T(8,128)(2,1)S(1)}, bf16[320,960]{1,0:T(8,128)(2,1)}, u32[]{:S(2)}) copy-start(bf16[320,960]{1,0:T(8,128)(2,1)} %param.5) | copy-start | bytes 1843204
  2.9 10.5 %collective-permute-start.1 = (bf16[1,320,512]{2,1,0:T(8,128)(2,1)S(1)}, bf16[1,320,512]{2,1,0:T(8,128)(2,1)S(1)}, u32[]{:S(2)}, u32[]{:S(2)}) collective-permute-start(bf16[1,320,512]{2,1,0:T(8,128)(2,1)S(1)} %copy.10), channel_id=1, source_target_pairs={{16,32},{32,16},{48,64},{64,48},{80,96},{96,80},{112,128},{128,112... | collective-permute-start | bytes 983048 | tf_op jit(solution)/shard_map/ppermute | solution.py:132
  5.0 11.0 %collective-permute-start.2 = (bf16[1,320,512]{2,1,0:T(8,128)(2,1)S(1)}, bf16[1,320,512]{2,1,0:T(8,128)(2,1)S(1)}, u32[]{:S(2)}, u32[]{:S(2)}) collective-permute-start(bf16[1,320,512]{2,1,0:T(8,128)(2,1)S(1)} %copy.11), channel_id=1, source_target_pairs={{16,32},{32,16},{48,64},{64,48},{80,96},{96,80},{112,128},{128,112... | collective-permute-start | bytes 983048 | tf_op jit(solution)/shard_map/ppermute | solution.py:132
  13.4 2.6 %copy-start.3 = (bf16[1,320,512]{2,1,0:T(8,128)(2,1)}, bf16[1,320,512]{2,1,0:T(8,128)(2,1)S(1)}, u32[]{:S(2)}) copy-start(bf16[1,320,512]{2,1,0:T(8,128)(2,1)S(1)} %collective-permute-done.1.b0_ref) | copy-start | bytes 983044
  16.0 0.7 %copy-start.4 = (bf16[1,320,512]{2,1,0:T(8,128)(2,1)}, bf16[1,320,512]{2,1,0:T(8,128)(2,1)S(1)}, u32[]{:S(2)}) copy-start(bf16[1,320,512]{2,1,0:T(8,128)(2,1)S(1)} %collective-permute-done.2.b1_ref) | copy-start | bytes 983044
  16.0 0.9 %copy-start.2 = (bf16[2,320,512]{2,1,0:T(8,128)(2,1)}, bf16[2,320,512]{2,1,0:T(8,128)(2,1)S(1)}, u32[]{:S(2)}) copy-start(bf16[2,320,512]{2,1,0:T(8,128)(2,1)S(1)} %collective-permute-done.a_ref) | copy-start | bytes 1966084
  25.8 10.3 %copy-start.5 = (f32[9,320]{1,0:T(8,128)S(1)}, f32[9,320]{1,0:T(8,128)}, u32[]{:S(2)}) copy-start(f32[9,320]{1,0:T(8,128)} %param.7) | copy-start | bytes 34564
  25.9 5.8 %collective-permute-start.3 = (bf16[2,1,5120]{2,1,0:T(2,128)(2,1)S(1)}, bf16[2,1,5120]{2,1,0:T(2,128)(2,1)S(1)}, u32[]{:S(2)}, u32[]{:S(2)}) collective-permute-start(bf16[2,1,5120]{2,1,0:T(2,128)(2,1)S(1)} %broadcast_select_fusion.2), channel_id=1, source_target_pairs={{0,8},{8,0},{1,9},{9,1},{2,10},{10,2},{3,11},{11,3},{4,12},{12,4},... | collective-permute-start | bytes 61448 | tf_op jit(solution)/shard_map/ppermute | solution.py:132
  31.9 5.0 %collective-permute-start.5 = (bf16[2,34,320]{2,1,0:T(8,128)(2,1)S(1)}, bf16[2,34,320]{2,1,0:T(8,128)(2,1)S(1)}, u32[]{:S(2)}, u32[]{:S(2)}) collective-permute-start(bf16[2,34,320]{2,1,0:T(8,128)(2,1)S(1)} %broadcast_select_fusion.5), channel_id=1, source_target_pairs={{0,1},{1,0},{2,3},{3,2},{4,5},{5,4},{6,7},{7,6},{8,9},{9,8},{10,11... | collective-permute-start | bytes 130568 | tf_op jit(solution)/shard_map/ppermute | solution.py:132
  33.5 7.0 %collective-permute-start.4 = (bf16[2,34,320]{2,1,0:T(8,128)(2,1)S(1)}, bf16[2,34,320]{2,1,0:T(8,128)(2,1)S(1)}, u32[]{:S(2)}, u32[]{:S(2)}) collective-permute-start(bf16[2,34,320]{2,1,0:T(8,128)(2,1)S(1)} %get-tuple-element.14), channel_id=1, source_target_pairs={{1,2},{2,1},{3,4},{4,3},{5,6},{6,5},{9,10},{10,9},{11,12},{12,11},... | collective-permute-start | bytes 130568 | tf_op jit(solution)/shard_map/ppermute | solution.py:132

commit v12 on v10

--- a/solution.py
+++ b/solution.py
@@ -83,9 +83,8 @@
 
 def attend(valid, prev, own, nxt, w_qkv, w_out):
     frames, chans, points = own.shape
-    grid = (points // BLOCK,)
-    assert points % BLOCK == 0
-    cell_spec = pl.BlockSpec((frames, chans, BLOCK), lambda i: (0, 0, i))
+    grid = (1,)
+    cell_spec = pl.BlockSpec((frames, chans, points), lambda i: (0, 0, i))
     full = lambda shape: pl.BlockSpec(shape, lambda i: (0, 0))
     w_qkv = w_qkv.T
     w_out = w_out.T
@@ -144,10 +143,14 @@
     chans = w_out.shape[0]
     cols = merged // chans
     points = rows * cols
-    cells = lambda a: a.reshape(frames, rows, cols, chans).transpose(0, 3, 1, 2).reshape(
-        frames, chans, points
+    assert lax.axis_size("row") == 2
+    upper = lax.axis_index("row") == 0
+    edge_x = jnp.where(upper, latents[:, rows - 1 :], latents[:, :1])
+    halo_x = lax.ppermute(edge_x, "row", [(0, 1), (1, 0)])
+    ext = jnp.concatenate([latents, halo_x], axis=1)
+    own_c = ext.reshape(frames, rows + 1, cols, chans).transpose(0, 3, 1, 2).reshape(
+        frames, chans, points + cols
     )
-    own_c = cells(latents)
     got_a = swap(own_c, own_c, "tm", 0)
     got_b = swap(own_c, own_c, "tm", 1)
     first = lax.axis_index("tm") * frames
@@ -158,10 +161,15 @@
     valid = jnp.concatenate([valid, even[None]])
     hidden = attend(valid, got_a, own_c, got_b, w_qkv, w_out)
     hid = (
-        hidden.reshape(frames, chans, rows, cols).transpose(0, 2, 3, 1).reshape(frames, rows, merged)
+        hidden[:, :, :points]
+        .reshape(frames, chans, rows, cols)
+        .transpose(0, 2, 3, 1)
+        .reshape(frames, rows, merged)
     )
-
-    halo_top, halo_bot = exchange(hid[:, rows - 1 :, :], hid[:, :1, :], "row")
+    hrow = hidden[:, :, points:].transpose(0, 2, 1).reshape(frames, 1, merged)
+    zero = jnp.zeros_like(hrow)
+    halo_top = jnp.where(upper, zero, hrow)
+    halo_bot = jnp.where(upper, hrow, zero)
     tall = jnp.concatenate([halo_top, hid, halo_bot], axis=1)
     halo_left, halo_right = exchange(tall[:, :, merged - chans :], tall[:, :, :chans], "col")
     padded = jnp.concatenate([halo_left, tall, halo_right], axis=2)

time: 43.7 us -> 49 us (1.12)
  local copies, waits for them, and re-layouts: 7.8 us -> 10 us
  other arithmetic: 4.47 us -> 6.64 us
  Pallas kernels: 6.8 us -> 8.95 us
  waiting for transfers between devices: 14.5 us -> 13.5 us
    ppermute x5 -> x4, waiting for transfers between devices: 14.5 us -> 11 us  [swap(): return lax.ppermute(payload, axis, pairs)]
    ppermute x5 -> x4, starting transfers between devices: 9.68 us -> 6.39 us  [swap(): return lax.ppermute(payload, axis, pairs)]
    ppermute x0 -> x1, starting transfers between devices: none -> 3.11 us  [body(): halo_x = lax.ppermute(edge_x, 'row', [(0, 1), (1, 0)])]
    ppermute x0 -> x2, local copies, waits for them, and re-layouts: none -> 2.52 us  [swap(): return lax.ppermute(payload, axis, pairs)]
    ppermute x0 -> x1, waiting for transfers between devices: none -> 2.48 us  [body(): halo_x = lax.ppermute(edge_x, 'row', [(0, 1), (1, 0)])]
    pallas_call x1, Pallas kernels: 6.8 us -> 8.95 us  [attend(): pl.pallas_call(attend_kernel, grid=grid, in_specs=[pl.BlockSpec(memory_sp...]
    pallas_call x1 -> x0, local copies, waits for them, and re-layouts: 1.44 us -> none  [attend(): pl.pallas_call(attend_kernel, grid=grid, in_specs=[pl.BlockSpec(memory_sp...]
    concatenate x0 -> x1, other arithmetic: none -> 1.16 us  [body(): ext = jnp.concatenate([latents, halo_x], axis=1)]
  transfers between devices with their start and end apart: 5 -> 5, of which waited for: 3 -> 3; matrix products, arithmetic and copies ran while one was open for 8% -> 12% of each run, Pallas kernels for 0% -> 0%
where the time goes in v12:
time: 49 us; the launch traced here: 48.8 us
  waiting for transfers between devices  13.5 us (28%)
  local copies, waits for them, and re-layouts  10 us (20%)
  starting transfers between devices  9.5 us (19%)
  Pallas kernels  8.95 us (18%)
  other arithmetic  6.64 us (14%)
    ppermute x4, waiting for transfers between devices, swap(): return lax.ppermute(payload, axis, pairs)  11 us
    pallas_call x1, Pallas kernels, attend(): pl.pallas_call(attend_kernel, grid=grid, in_specs=[pl.BlockSpec(memory_sp...  8.95 us
    ppermute x4, starting transfers between devices, swap(): return lax.ppermute(payload, axis, pairs)  6.39 us
    unnamed x10, local copies, waits for them, and re-layouts  3.17 us
    ppermute x1, starting transfers between devices, body(): halo_x = lax.ppermute(edge_x, 'row', [(0, 1), (1, 0)])  3.11 us
    convert_element_type x1, other arithmetic, body(): return acc.astype(jnp.bfloat16)  2.85 us
    ppermute x2, local copies, waits for them, and re-layouts, swap(): return lax.ppermute(payload, axis, pairs)  2.52 us
    ppermute x1, waiting for transfers between devices, body(): halo_x = lax.ppermute(edge_x, 'row', [(0, 1), (1, 0)])  2.48 us
  transfers between devices with their start and end apart: 5, of which 3 were waited for; matrix products, arithmetic and copies ran while one was open for 12% of the time, Pallas kernels for 0%

profile of v12, /device:TPU:152, one launch (start us, length us, event | category | flops | bytes accessed | tf_op | source)
XLA Modules:
  0.0 48.8 jit_solution(1973684724738949749)
XLA Ops:
  0.0 1.1 %broadcast_select_fusion = bf16[2,1,5120]{2,1,0:T(2,128)(2,1)S(1)} fusion(pred[]{:T(512)S(6)} %eq.21, bf16[2,32,5120]{2,1,0:T(8,128)(2,1)} %param.4), kind=kLoop, calls=%fused_computation.18 | loop fusion | flops 10240 | bytes 61441 | tf_op jit(solution)/shard_map/jit(_where)/select_n | solution.py:148
  1.1 3.1 %collective-permute-start = (bf16[2,1,5120]{2,1,0:T(2,128)(2,1)S(1)}, bf16[2,1,5120]{2,1,0:T(2,128)(2,1)S(1)}, u32[]{:S(2)}, u32[]{:S(2)}) collective-permute-start(bf16[2,1,5120]{2,1,0:T(2,128)(2,1)S(1)} %broadcast_select_fusion), channel_id=1, source_target_pairs={{0,8},{8,0},{1,9},{9,1},{2,10},{10,2},{3,11},{11,3},{4,12},{12,4},... | collective-permute-start | bytes 61448 | tf_op jit(solution)/shard_map/ppermute | solution.py:149
  4.2 2.5 %collective-permute-done = bf16[2,1,5120]{2,1,0:T(2,128)(2,1)S(1)} collective-permute-done((bf16[2,1,5120]{2,1,0:T(2,128)(2,1)S(1)}, bf16[2,1,5120]{2,1,0:T(2,128)(2,1)S(1)}, u32[]{:S(2)}, u32[]{:S(2)}) %collective-permute-start) | collective-permute-done | bytes 20512 | tf_op jit(solution)/shard_map/ppermute | solution.py:149
  6.7 1.2 %pad_maximum_fusion.1 = bf16[2,33,5120]{2,1,0:T(8,128)(2,1)S(1)} fusion(bf16[2,1,5120]{2,1,0:T(2,128)(2,1)S(1)} %collective-permute-done, bf16[2,32,5120]{2,1,0:T(8,128)(2,1)} %param.4), kind=kLoop, calls=%fused_computation.13 | loop fusion | flops 1351680 | bytes 1351680 | tf_op jit(solution)/shard_map/concatenate | solution.py:150
  7.8 0.0 copy-start.1
  7.8 0.7 %reshape.91 = bf16[2,33,16,320]{3,2,1,0:T(8,128)(2,1)S(1)} reshape(bf16[2,33,5120]{2,1,0:T(8,128)(2,1)S(1)} %pad_maximum_fusion.1) | data formatting | bytes 1351680 | tf_op jit(solution)/shard_map/reshape | solution.py:151
  8.5 0.0 copy-start.2
  8.5 0.1 collective-permute-start.1
  8.6 2.1 %collective-permute-start.2 = (bf16[2,320,528]{1,2,0:T(8,128)(2,1)S(1)}, bf16[2,320,528]{1,2,0:T(8,128)(2,1)S(1)}, u32[]{:S(2)}, u32[]{:S(2)}) collective-permute-start(bf16[2,320,528]{1,2,0:T(8,128)(2,1)S(1)} %bitcast.16), channel_id=1, source_target_pairs={{16,32},{32,16},{48,64},{64,48},{80,96},{96,80},{112,128},{128,112... | collective-permute-start | bytes 2027528 | tf_op jit(solution)/shard_map/ppermute | solution.py:126
  10.8 0.0 copy-done.1
  10.8 1.1 %copy.21 = bf16[320,960]{0,1:T(8,128)(2,1)} copy(bf16[320,960]{1,0:T(8,128)(2,1)S(1)} %copy-done.1) | data formatting | bytes 1228800 | tf_op args[1]
  11.9 0.0 copy-done.2
  11.9 0.9 %copy.22 = bf16[320,320]{0,1:T(8,128)(2,1)} copy(bf16[320,320]{1,0:T(8,128)(2,1)S(1)} %copy-done.2) | data formatting | bytes 409600 | tf_op args[2]
  12.8 0.6 %add_convert_fusion.valid_ref = s32[7]{0:T(128)} fusion(pred[1]{0:T(512)(128)(4,1)} %bitcast, pred[6]{0:T(512)(128)(4,1)S(1)} %compare_and_fusion), kind=kLoop, calls=%fused_computation.26 | loop fusion | flops 14 | bytes 35 | tf_op jit(solution)/shard_map/concatenate | solution.py:161
  13.4 1.3 %copy.24.own_ref = bf16[2,320,528]{2,1,0:T(8,128)(2,1)} copy(bf16[2,320,528]{1,2,0:T(8,128)(2,1)S(1)} %bitcast.17) | data formatting | bytes 1351680 | tf_op jit(solution)/shard_map/reshape | solution.py:151
  14.7 0.0 collective-permute-done.1
  14.7 1.2 %copy.23.a_ref = bf16[2,320,528]{2,1,0:T(8,128)(2,1)} copy(bf16[2,320,528]{1,2,0:T(8,128)(2,1)S(1)} %collective-permute-done.1) | data formatting | bytes 1351680 | tf_op jit(solution)/shard_map/ppermute | solution.py:126
  15.9 7.5 %collective-permute-done.2 = bf16[2,320,528]{1,2,0:T(8,128)(2,1)S(1)} collective-permute-done((bf16[2,320,528]{1,2,0:T(8,128)(2,1)S(1)}, bf16[2,320,528]{1,2,0:T(8,128)(2,1)S(1)}, u32[]{:S(2)}, u32[]{:S(2)}) %collective-permute-start.2) | collective-permute-done | bytes 675872 | tf_op jit(solution)/shard_map/ppermute | solution.py:126
  23.4 1.3 %copy.25.b_ref = bf16[2,320,528]{2,1,0:T(8,128)(2,1)} copy(bf16[2,320,528]{1,2,0:T(8,128)(2,1)S(1)} %collective-permute-done.2) | data formatting | bytes 1351680 | tf_op jit(solution)/shard_map/ppermute | solution.py:126
  24.7 8.9 %shard_map.46 = bf16[2,320,528]{2,1,0:T(8,128)(2,1)} custom-call(s32[7]{0:T(128)} %add_convert_fusion.valid_ref, bf16[2,320,528]{2,1,0:T(8,128)(2,1)} %copy.23.a_ref, bf16[2,320,528]{2,1,0:T(8,128)(2,1)} %copy.24.own_ref, bf16[2,320,528]{2,1,0:T(8,128)(2,1)} %copy.25.b_ref, bf16[960,320]{1,0:T(8,128)(2,1)} %bitcast.19, bf16[320,320]{1,0:T(8,128)(2,1)} %bitcast.20), custom_call_target="tpu_custom_call" | custom-call | tf_op jit(solution)/shard_map/pallas_call | solution.py:91
  33.6 0.0 copy-start
  33.6 1.1 %copy-done = bf16[2,320,528]{2,1,0:T(8,128)(2,1)S(1)} copy-done((bf16[2,320,528]{2,1,0:T(8,128)(2,1)S(1)}, bf16[2,320,528]{2,1,0:T(8,128)(2,1)}, u32[]{:S(2)}) %copy-start) | copy-done | bytes 675864
  34.8 0.2 slice-done
  35.0 0.4 copy.26
  35.3 0.6 %reshape.94 = bf16[2,32,5120]{2,1,0:T(8,128)(2,1)S(1)} reshape(bf16[2,32,16,320]{3,2,1,0:T(8,128)(2,1)S(1)} %bitcast.18) | data formatting | bytes 1310720 | tf_op jit(solution)/shard_map/reshape | solution.py:167
  36.0 0.0 copy-start.3
  36.0 0.1 copy.27
  36.1 0.1 select_n.107
  36.2 0.1 copy.28
  36.3 0.1 select_n.108
  36.4 0.1 broadcast_select_fusion.4
  36.6 1.6 %collective-permute-start.4 = (bf16[2,34,320]{2,1,0:T(8,128)(2,1)S(1)}, bf16[2,34,320]{2,1,0:T(8,128)(2,1)S(1)}, u32[]{:S(2)}, u32[]{:S(2)}) collective-permute-start(bf16[2,34,320]{2,1,0:T(8,128)(2,1)S(1)} %broadcast_select_fusion.3), channel_id=1, source_target_pairs={{0,1},{1,0},{2,3},{3,2},{4,5},{5,4},{6,7},{7,6},{8,9},{9,8},{10,11... | collective-permute-start | bytes 130568 | tf_op jit(solution)/shard_map/ppermute | solution.py:126
  38.2 2.6 %collective-permute-start.3 = (bf16[2,34,320]{2,1,0:T(8,128)(2,1)S(1)}, bf16[2,34,320]{2,1,0:T(8,128)(2,1)S(1)}, u32[]{:S(2)}, u32[]{:S(2)}) collective-permute-start(bf16[2,34,320]{2,1,0:T(8,128)(2,1)S(1)} %get-tuple-element.14), channel_id=1, source_target_pairs={{1,2},{2,1},{3,4},{4,3},{5,6},{6,5},{9,10},{10,9},{11,12},{12,11},... | collective-permute-start | bytes 130568 | tf_op jit(solution)/shard_map/ppermute | solution.py:126
  40.8 0.0 copy-done.3
  40.8 0.1 slice_reduce_fusion.8
  40.9 0.1 tile.42
  40.9 0.1 tile.44
  41.0 0.1 tile.46
  41.1 0.1 tile.48
  41.2 0.1 tile.50
  41.3 0.1 tile.52
  41.4 0.1 tile.54
  41.4 0.1 tile.56
  41.5 0.1 tile.58
  41.6 0.0 collective-permute-done.4
  41.6 3.6 %collective-permute-done.3 = bf16[2,34,320]{2,1,0:T(8,128)(2,1)S(1)} collective-permute-done((bf16[2,34,320]{2,1,0:T(8,128)(2,1)S(1)}, bf16[2,34,320]{2,1,0:T(8,128)(2,1)S(1)}, u32[]{:S(2)}, u32[]{:S(2)}) %collective-permute-start.3) | collective-permute-done | bytes 43552 | tf_op jit(solution)/shard_map/ppermute | solution.py:126
  45.2 0.8 %maximum_maximum_fusion = (bf16[2,34,5440]{2,1,0:T(8,128)(2,1)S(1)}, bf16[2,34,5440]{2,1,0:T(8,128)(2,1)S(1)}) fusion(bf16[2,1,5120]{2,1,0:T(2,128)(2,1)S(1)} %select_n.108, bf16[2,32,5120]{2,1,0:T(8,128)(2,1)S(1)} %reshape.94, bf16[2,1,5120]{2,1,0:T(2,128)(2,1)S(1)} %select_n.107, bf16[2,34,320]{2,1,0:T(8,128)(2,1)S(1)} %get-tuple-element.21, ...), kind=kLoop, calls=%fused_computation.11 | loop fusion | flops 5918720 | bytes 2263040 | tf_op jit(solution)/shard_map/concatenate | solution.py:175
  46.0 2.8 %fusion.8 = bf16[2,32,5120]{2,1,0:T(8,128)(2,1)} fusion(bf16[2,32,5120]{2,1,0:T(8,128)(2,1)S(1)} %reshape.94, bf16[2,34,5440]{2,1,0:T(8,128)(2,1)S(1)} %get-tuple-element.20, bf16[2,1,5120]{2,1,0:T(2,128)(2,1)S(1)} %select_n.108, bf16[2,34,5440]{2,1,0:T(8,128)(2,1)S(1)} %get-tuple-element.19, bf16[2,1,5120]{2,1,0:T(2,128)(2,1)S(1)} %select_n.107, ...), kind=kLoop, calls=%fused_computation.10 | loop fusion | flops 11141120 | bytes 5468160 | tf_op jit(solution)/shard_map/convert_element_type | solution.py:187
  (14 shorter events, 0.1 us)
Async XLA Ops:
  1.1 5.6 %collective-permute-start = (bf16[2,1,5120]{2,1,0:T(2,128)(2,1)S(1)}, bf16[2,1,5120]{2,1,0:T(2,128)(2,1)S(1)}, u32[]{:S(2)}, u32[]{:S(2)}) collective-permute-start(bf16[2,1,5120]{2,1,0:T(2,128)(2,1)S(1)} %broadcast_select_fusion), channel_id=1, source_target_pairs={{0,8},{8,0},{1,9},{9,1},{2,10},{10,2},{3,11},{11,3},{4,12},{12,4},... | collective-permute-start | bytes 61448 | tf_op jit(solution)/shard_map/ppermute | solution.py:149
  7.8 2.9 %copy-start.1 = (bf16[320,960]{1,0:T(8,128)(2,1)S(1)}, bf16[320,960]{1,0:T(8,128)(2,1)}, u32[]{:S(2)}) copy-start(bf16[320,960]{1,0:T(8,128)(2,1)} %param.5) | copy-start | bytes 1843204
  8.5 3.4 %copy-start.2 = (bf16[320,320]{1,0:T(8,128)(2,1)S(1)}, bf16[320,320]{1,0:T(8,128)(2,1)}, u32[]{:S(2)}) copy-start(bf16[320,320]{1,0:T(8,128)(2,1)} %param.6) | copy-start | bytes 614404
  8.5 6.2 %collective-permute-start.1 = (bf16[2,320,528]{1,2,0:T(8,128)(2,1)S(1)}, bf16[2,320,528]{1,2,0:T(8,128)(2,1)S(1)}, u32[]{:S(2)}, u32[]{:S(2)}) collective-permute-start(bf16[2,320,528]{1,2,0:T(8,128)(2,1)S(1)} %bitcast.15), channel_id=1, source_target_pairs={{0,16},{16,0},{32,48},{48,32},{64,80},{80,64},{96,112},{112,96},{1... | collective-permute-start | bytes 2027528 | tf_op jit(solution)/shard_map/ppermute | solution.py:126
  8.6 14.8 %collective-permute-start.2 = (bf16[2,320,528]{1,2,0:T(8,128)(2,1)S(1)}, bf16[2,320,528]{1,2,0:T(8,128)(2,1)S(1)}, u32[]{:S(2)}, u32[]{:S(2)}) collective-permute-start(bf16[2,320,528]{1,2,0:T(8,128)(2,1)S(1)} %bitcast.16), channel_id=1, source_target_pairs={{16,32},{32,16},{48,64},{64,48},{80,96},{96,80},{112,128},{128,112... | collective-permute-start | bytes 2027528 | tf_op jit(solution)/shard_map/ppermute | solution.py:126
  33.6 1.1 %copy-start = (bf16[2,320,528]{2,1,0:T(8,128)(2,1)S(1)}, bf16[2,320,528]{2,1,0:T(8,128)(2,1)}, u32[]{:S(2)}) copy-start(bf16[2,320,528]{2,1,0:T(8,128)(2,1)} %shard_map.46) | copy-start | bytes 2027524
  33.6 1.3 %slice-start = ((bf16[2,320,528]{2,1,0:T(8,128)(2,1)}), bf16[2,320,512]{2,1,0:T(8,128)(2,1)S(1)}, s32[]{:S(2)}) async-start(bf16[2,320,528]{2,1,0:T(8,128)(2,1)} %shard_map.46), calls=%async_computation | async-start | bytes 1310720 | tf_op jit(solution)/shard_map/slice | solution.py:164
  36.0 4.8 %copy-start.3 = (f32[9,320]{1,0:T(8,128)S(1)}, f32[9,320]{1,0:T(8,128)}, u32[]{:S(2)}) copy-start(f32[9,320]{1,0:T(8,128)} %param.7) | copy-start | bytes 34564
  36.6 5.0 %collective-permute-start.4 = (bf16[2,34,320]{2,1,0:T(8,128)(2,1)S(1)}, bf16[2,34,320]{2,1,0:T(8,128)(2,1)S(1)}, u32[]{:S(2)}, u32[]{:S(2)}) collective-permute-start(bf16[2,34,320]{2,1,0:T(8,128)(2,1)S(1)} %broadcast_select_fusion.3), channel_id=1, source_target_pairs={{0,1},{1,0},{2,3},{3,2},{4,5},{5,4},{6,7},{7,6},{8,9},{9,8},{10,11... | collective-permute-start | bytes 130568 | tf_op jit(solution)/shard_map/ppermute | solution.py:126
  38.2 7.0 %collective-permute-start.3 = (bf16[2,34,320]{2,1,0:T(8,128)(2,1)S(1)}, bf16[2,34,320]{2,1,0:T(8,128)(2,1)S(1)}, u32[]{:S(2)}, u32[]{:S(2)}) collective-permute-start(bf16[2,34,320]{2,1,0:T(8,128)(2,1)S(1)} %get-tuple-element.14), channel_id=1, source_target_pairs={{1,2},{2,1},{3,4},{4,3},{5,6},{6,5},{9,10},{10,9},{11,12},{12,11},... | collective-permute-start | bytes 130568 | tf_op jit(solution)/shard_map/ppermute | solution.py:126

commit v13 on v10

--- a/solution.py
+++ b/solution.py
@@ -147,9 +147,10 @@
     cells = lambda a: a.reshape(frames, rows, cols, chans).transpose(0, 3, 1, 2).reshape(
         frames, chans, points
     )
+    raw_b = swap(latents, latents, "tm", 1)
     own_c = cells(latents)
     got_a = swap(own_c, own_c, "tm", 0)
-    got_b = swap(own_c, own_c, "tm", 1)
+    got_b = cells(raw_b)
     first = lax.axis_index("tm") * frames
     total = lax.axis_size("tm") * frames
     where_t = first + jnp.arange(6, dtype=jnp.int32) - 2

time: 43.7 us -> 43.3 us (level)
  waiting for transfers between devices: 14.5 us -> 11.5 us
  local copies, waits for them, and re-layouts: 7.8 us -> 9.55 us
  starting transfers between devices: 9.68 us -> 10.6 us
    ppermute x5, waiting for transfers between devices: 14.5 us -> 11.5 us  [swap(): return lax.ppermute(payload, axis, pairs)]
    reshape x2 -> x4, local copies, waits for them, and re-layouts: 2.03 us -> 3.8 us  [body(): a.reshape(frames, rows, cols, chans).transpose(0, 3, 1, 2)]
    ppermute x5, starting transfers between devices: 9.68 us -> 10.6 us  [swap(): return lax.ppermute(payload, axis, pairs)]
    unnamed x14 -> x12, local copies, waits for them, and re-layouts: 2.9 us -> 2.88 us
  transfers between devices with their start and end apart: 5 -> 5, of which waited for: 3 -> 3; matrix products, arithmetic and copies ran while one was open for 8% -> 17% of each run, Pallas kernels for 0% -> 0%
where the time goes in v13:
time: 43.3 us; the launch traced here: 43.1 us
  waiting for transfers between devices  11.5 us (27%)
  starting transfers between devices  10.6 us (24%)
  local copies, waits for them, and re-layouts  9.55 us (22%)
  Pallas kernels  6.79 us (16%)
  other arithmetic  4.47 us (10%)
    ppermute x5, waiting for transfers between devices, swap(): return lax.ppermute(payload, axis, pairs)  11.5 us
    ppermute x5, starting transfers between devices, swap(): return lax.ppermute(payload, axis, pairs)  10.6 us
    pallas_call x1, Pallas kernels, attend(): pl.pallas_call(attend_kernel, grid=grid, in_specs=[pl.BlockSpec(memory_sp...  6.79 us
    reshape x4, local copies, waits for them, and re-layouts, body(): a.reshape(frames, rows, cols, chans).transpose(0, 3, 1, 2)  3.8 us
    unnamed x12, local copies, waits for them, and re-layouts  2.88 us
    convert_element_type x1, other arithmetic, body(): return acc.astype(jnp.bfloat16)  2.85 us
    pallas_call x1, local copies, waits for them, and re-layouts, attend(): pl.pallas_call(attend_kernel, grid=grid, in_specs=[pl.BlockSpec(memory_sp...  1.44 us
  transfers between devices with their start and end apart: 5, of which 3 were waited for; matrix products, arithmetic and copies ran while one was open for 17% of the time, Pallas kernels for 0%

profile of v13, /device:TPU:152, one launch (start us, length us, event | category | flops | bytes accessed | tf_op | source)
XLA Modules:
  0.0 43.1 jit_solution(5789578295755840708)
XLA Ops:
  0.0 1.9 %collective-permute-start.1 = (bf16[2,32,5120]{2,1,0:T(8,128)(2,1)}, bf16[2,32,5120]{2,1,0:T(8,128)(2,1)S(1)}, u32[]{:S(2)}, u32[]{:S(2)}) collective-permute-start(bf16[2,32,5120]{2,1,0:T(8,128)(2,1)} %param.4), channel_id=1, source_target_pairs={{16,32},{32,16},{48,64},{64,48},{80,96},{96,80},{112,128},{128,112... | collective-permute-start | bytes 1966088 | tf_op jit(solution)/shard_map/ppermute | solution.py:127
  1.9 1.8 %reshape.66 = bf16[2,32,16,320]{3,2,1,0:T(8,128)(2,1)S(1)} reshape(bf16[2,32,5120]{2,1,0:T(8,128)(2,1)} %param.4) | data formatting | bytes 1310720 | tf_op jit(solution)/shard_map/reshape | solution.py:147
  3.7 0.0 copy-start.1
  3.7 0.3 copy.10.own_ref
  4.0 0.0 copy-start
  4.0 0.0 copy-start.3
  4.0 1.2 %collective-permute-start = (bf16[2,320,512]{2,1,0:T(8,128)(2,1)S(1)}, bf16[2,320,512]{2,1,0:T(8,128)(2,1)S(1)}, u32[]{:S(2)}, u32[]{:S(2)}) collective-permute-start(bf16[2,320,512]{2,1,0:T(8,128)(2,1)S(1)} %copy.10.own_ref), channel_id=1, source_target_pairs={{0,16},{16,0},{32,48},{48,32},{64,80},{80,64},{96,112},{112,96},{1... | collective-permute-start | bytes 1966088 | tf_op jit(solution)/shard_map/ppermute | solution.py:127
  5.2 0.0 copy-done.1
  5.2 1.2 %copy.11 = bf16[320,960]{0,1:T(8,128)(2,1)} copy(bf16[320,960]{1,0:T(8,128)(2,1)S(1)} %copy-done.1) | data formatting | bytes 1228800 | tf_op args[1]
  6.4 0.0 copy-done.3
  6.4 0.9 %copy.12 = bf16[320,320]{0,1:T(8,128)(2,1)} copy(bf16[320,320]{1,0:T(8,128)(2,1)S(1)} %copy-done.3) | data formatting | bytes 409600 | tf_op args[2]
  7.2 0.0 copy-done
  7.3 0.6 %add_convert_fusion.valid_ref = s32[7]{0:T(128)} fusion(pred[1]{0:T(512)(128)(4,1)} %bitcast, pred[6]{0:T(512)(128)(4,1)S(1)} %compare_and_fusion), kind=kLoop, calls=%fused_computation.25 | loop fusion | flops 14 | bytes 35 | tf_op jit(solution)/shard_map/concatenate | solution.py:159
  7.8 5.5 %collective-permute-done.1 = bf16[2,32,5120]{2,1,0:T(8,128)(2,1)S(1)} collective-permute-done((bf16[2,32,5120]{2,1,0:T(8,128)(2,1)}, bf16[2,32,5120]{2,1,0:T(8,128)(2,1)S(1)}, u32[]{:S(2)}, u32[]{:S(2)}) %collective-permute-start.1) | collective-permute-done | bytes 655392 | tf_op jit(solution)/shard_map/ppermute | solution.py:127
  13.3 0.6 %reshape.68 = bf16[2,32,16,320]{3,2,1,0:T(8,128)(2,1)S(1)} reshape(bf16[2,32,5120]{2,1,0:T(8,128)(2,1)S(1)} %collective-permute-done.1) | data formatting | bytes 1310720 | tf_op jit(solution)/shard_map/reshape | solution.py:147
  13.9 1.1 %copy.14.b_ref = bf16[2,320,512]{2,1,0:T(8,128)(2,1)} copy(bf16[2,320,512]{1,2,0:T(8,128)(2,1)S(1)} %bitcast.14) | data formatting | bytes 1310720 | tf_op jit(solution)/shard_map/reshape | solution.py:147
  15.1 0.0 collective-permute-done.a_ref
  15.1 0.0 copy-start.2
  15.1 0.8 %copy-done.2 = bf16[2,320,512]{2,1,0:T(8,128)(2,1)} copy-done((bf16[2,320,512]{2,1,0:T(8,128)(2,1)}, bf16[2,320,512]{2,1,0:T(8,128)(2,1)S(1)}, u32[]{:S(2)}) %copy-start.2) | copy-done | bytes 655384
  15.9 6.8 %shard_map.46 = bf16[2,320,512]{2,1,0:T(8,128)(2,1)} custom-call(s32[7]{0:T(128)} %add_convert_fusion.valid_ref, bf16[2,320,512]{2,1,0:T(8,128)(2,1)} %copy-done.2, bf16[2,320,512]{2,1,0:T(8,128)(2,1)} %copy-done, bf16[2,320,512]{2,1,0:T(8,128)(2,1)} %copy.14.b_ref, bf16[960,320]{1,0:T(8,128)(2,1)} %bitcast.17, bf16[320,320]{1,0:T(8,128)(2,1)} %bitcast.18), custom_call_target="tpu_custom_call" | custom-call | tf_op jit(solution)/shard_map/pallas_call | solution.py:92
  22.7 1.4 %copy.15 = bf16[2,320,512]{1,2,0:T(8,128)(2,1)S(1)} copy(bf16[2,320,512]{2,1,0:T(8,128)(2,1)} %shard_map.46) | data formatting | bytes 1310720 | tf_op jit(solution)/shard_map/pallas_call | solution.py:92
  24.2 0.6 %reshape.71 = bf16[2,32,5120]{2,1,0:T(8,128)(2,1)S(1)} reshape(bf16[2,32,16,320]{3,2,1,0:T(8,128)(2,1)S(1)} %bitcast.15) | data formatting | bytes 1310720 | tf_op jit(solution)/shard_map/reshape | solution.py:162
  24.8 0.0 copy-start.4
  24.8 0.1 broadcast_select_fusion.2
  24.9 3.3 %collective-permute-start.2 = (bf16[2,1,5120]{2,1,0:T(2,128)(2,1)S(1)}, bf16[2,1,5120]{2,1,0:T(2,128)(2,1)S(1)}, u32[]{:S(2)}, u32[]{:S(2)}) collective-permute-start(bf16[2,1,5120]{2,1,0:T(2,128)(2,1)S(1)} %broadcast_select_fusion.2), channel_id=1, source_target_pairs={{0,8},{8,0},{1,9},{9,1},{2,10},{10,2},{3,11},{11,3},{4,12},{12,4},... | collective-permute-start | bytes 61448 | tf_op jit(solution)/shard_map/ppermute | solution.py:127
  28.2 2.5 %collective-permute-done.2 = bf16[2,1,5120]{2,1,0:T(2,128)(2,1)S(1)} collective-permute-done((bf16[2,1,5120]{2,1,0:T(2,128)(2,1)S(1)}, bf16[2,1,5120]{2,1,0:T(2,128)(2,1)S(1)}, u32[]{:S(2)}, u32[]{:S(2)}) %collective-permute-start.2) | collective-permute-done | bytes 20512 | tf_op jit(solution)/shard_map/ppermute | solution.py:127
  30.7 0.1 broadcast_select_fusion.1
  30.7 0.1 broadcast_select_fusion.6
  30.9 1.6 %collective-permute-start.4 = (bf16[2,34,320]{2,1,0:T(8,128)(2,1)S(1)}, bf16[2,34,320]{2,1,0:T(8,128)(2,1)S(1)}, u32[]{:S(2)}, u32[]{:S(2)}) collective-permute-start(bf16[2,34,320]{2,1,0:T(8,128)(2,1)S(1)} %broadcast_select_fusion.5), channel_id=1, source_target_pairs={{0,1},{1,0},{2,3},{3,2},{4,5},{5,4},{6,7},{7,6},{8,9},{9,8},{10,11... | collective-permute-start | bytes 130568 | tf_op jit(solution)/shard_map/ppermute | solution.py:127
  32.5 2.6 %collective-permute-start.3 = (bf16[2,34,320]{2,1,0:T(8,128)(2,1)S(1)}, bf16[2,34,320]{2,1,0:T(8,128)(2,1)S(1)}, u32[]{:S(2)}, u32[]{:S(2)}) collective-permute-start(bf16[2,34,320]{2,1,0:T(8,128)(2,1)S(1)} %get-tuple-element.14), channel_id=1, source_target_pairs={{1,2},{2,1},{3,4},{4,3},{5,6},{6,5},{9,10},{10,9},{11,12},{12,11},... | collective-permute-start | bytes 130568 | tf_op jit(solution)/shard_map/ppermute | solution.py:127
  35.1 0.0 copy-done.4
  35.1 0.1 slice_reduce_fusion.8
  35.1 0.1 tile.42
  35.2 0.1 tile.44
  35.3 0.1 tile.46
  35.4 0.1 tile.48
  35.5 0.1 tile.50
  35.6 0.1 tile.52
  35.6 0.1 tile.54
  35.7 0.1 tile.56
  35.8 0.1 tile.58
  35.9 0.0 collective-permute-done.4
  35.9 3.6 %collective-permute-done.3 = bf16[2,34,320]{2,1,0:T(8,128)(2,1)S(1)} collective-permute-done((bf16[2,34,320]{2,1,0:T(8,128)(2,1)S(1)}, bf16[2,34,320]{2,1,0:T(8,128)(2,1)S(1)}, u32[]{:S(2)}, u32[]{:S(2)}) %collective-permute-start.3) | collective-permute-done | bytes 43552 | tf_op jit(solution)/shard_map/ppermute | solution.py:127
  39.5 0.8 %maximum_maximum_fusion = (bf16[2,34,5440]{2,1,0:T(8,128)(2,1)S(1)}, bf16[2,34,5440]{2,1,0:T(8,128)(2,1)S(1)}) fusion(bf16[2,1,5120]{2,1,0:T(2,128)(2,1)S(1)} %get-tuple-element.22, bf16[2,32,5120]{2,1,0:T(8,128)(2,1)S(1)} %reshape.71, bf16[2,1,5120]{2,1,0:T(2,128)(2,1)S(1)} %get-tuple-element.21, bf16[2,34,320]{2,1,0:T(8,128)(2,1)S(1)} %get-tuple-element.19, ...), kind=kLoop, calls=%fused_computation.11 | loop fusion | flops 5918720 | bytes 2263040 | tf_op jit(solution)/shard_map/concatenate | solution.py:168
  40.2 2.8 %fusion.8 = bf16[2,32,5120]{2,1,0:T(8,128)(2,1)} fusion(bf16[2,32,5120]{2,1,0:T(8,128)(2,1)S(1)} %reshape.71, bf16[2,34,5440]{2,1,0:T(8,128)(2,1)S(1)} %get-tuple-element.18, bf16[2,1,5120]{2,1,0:T(2,128)(2,1)S(1)} %get-tuple-element.22, bf16[2,34,5440]{2,1,0:T(8,128)(2,1)S(1)} %get-tuple-element.17, bf16[2,1,5120]{2,1,0:T(2,128)(2,1)S(1)} %get-tuple-element.21, ...), kind=kLoop, calls=%fused_computation.10 | loop fusion | flops 11141120 | bytes 5468160 | tf_op jit(solution)/shard_map/convert_element_type | solution.py:180
  (12 shorter events, 0.1 us)
Async XLA Ops:
  0.0 13.3 %collective-permute-start.1 = (bf16[2,32,5120]{2,1,0:T(8,128)(2,1)}, bf16[2,32,5120]{2,1,0:T(8,128)(2,1)S(1)}, u32[]{:S(2)}, u32[]{:S(2)}) collective-permute-start(bf16[2,32,5120]{2,1,0:T(8,128)(2,1)} %param.4), channel_id=1, source_target_pairs={{16,32},{32,16},{48,64},{64,48},{80,96},{96,80},{112,128},{128,112... | collective-permute-start | bytes 1966088 | tf_op jit(solution)/shard_map/ppermute | solution.py:127
  3.7 1.5 %copy-start.1 = (bf16[320,960]{1,0:T(8,128)(2,1)S(1)}, bf16[320,960]{1,0:T(8,128)(2,1)}, u32[]{:S(2)}) copy-start(bf16[320,960]{1,0:T(8,128)(2,1)} %param.5) | copy-start | bytes 1843204
  4.0 3.3 %copy-start = (bf16[2,320,512]{2,1,0:T(8,128)(2,1)}, bf16[2,320,512]{2,1,0:T(8,128)(2,1)S(1)}, u32[]{:S(2)}) copy-start(bf16[2,320,512]{2,1,0:T(8,128)(2,1)S(1)} %copy.10.own_ref) | copy-start | bytes 1966084
  4.0 2.4 %copy-start.3 = (bf16[320,320]{1,0:T(8,128)(2,1)S(1)}, bf16[320,320]{1,0:T(8,128)(2,1)}, u32[]{:S(2)}) copy-start(bf16[320,320]{1,0:T(8,128)(2,1)} %param.6) | copy-start | bytes 614404
  4.0 11.1 %collective-permute-start = (bf16[2,320,512]{2,1,0:T(8,128)(2,1)S(1)}, bf16[2,320,512]{2,1,0:T(8,128)(2,1)S(1)}, u32[]{:S(2)}, u32[]{:S(2)}) collective-permute-start(bf16[2,320,512]{2,1,0:T(8,128)(2,1)S(1)} %copy.10.own_ref), channel_id=1, source_target_pairs={{0,16},{16,0},{32,48},{48,32},{64,80},{80,64},{96,112},{112,96},{1... | collective-permute-start | bytes 1966088 | tf_op jit(solution)/shard_map/ppermute | solution.py:127
  15.1 0.8 %copy-start.2 = (bf16[2,320,512]{2,1,0:T(8,128)(2,1)}, bf16[2,320,512]{2,1,0:T(8,128)(2,1)S(1)}, u32[]{:S(2)}) copy-start(bf16[2,320,512]{2,1,0:T(8,128)(2,1)S(1)} %collective-permute-done.a_ref) | copy-start | bytes 1966084
  24.8 10.3 %copy-start.4 = (f32[9,320]{1,0:T(8,128)S(1)}, f32[9,320]{1,0:T(8,128)}, u32[]{:S(2)}) copy-start(f32[9,320]{1,0:T(8,128)} %param.7) | copy-start | bytes 34564
  24.9 5.8 %collective-permute-start.2 = (bf16[2,1,5120]{2,1,0:T(2,128)(2,1)S(1)}, bf16[2,1,5120]{2,1,0:T(2,128)(2,1)S(1)}, u32[]{:S(2)}, u32[]{:S(2)}) collective-permute-start(bf16[2,1,5120]{2,1,0:T(2,128)(2,1)S(1)} %broadcast_select_fusion.2), channel_id=1, source_target_pairs={{0,8},{8,0},{1,9},{9,1},{2,10},{10,2},{3,11},{11,3},{4,12},{12,4},... | collective-permute-start | bytes 61448 | tf_op jit(solution)/shard_map/ppermute | solution.py:127
  30.9 5.0 %collective-permute-start.4 = (bf16[2,34,320]{2,1,0:T(8,128)(2,1)S(1)}, bf16[2,34,320]{2,1,0:T(8,128)(2,1)S(1)}, u32[]{:S(2)}, u32[]{:S(2)}) collective-permute-start(bf16[2,34,320]{2,1,0:T(8,128)(2,1)S(1)} %broadcast_select_fusion.5), channel_id=1, source_target_pairs={{0,1},{1,0},{2,3},{3,2},{4,5},{5,4},{6,7},{7,6},{8,9},{9,8},{10,11... | collective-permute-start | bytes 130568 | tf_op jit(solution)/shard_map/ppermute | solution.py:127
  32.5 7.0 %collective-permute-start.3 = (bf16[2,34,320]{2,1,0:T(8,128)(2,1)S(1)}, bf16[2,34,320]{2,1,0:T(8,128)(2,1)S(1)}, u32[]{:S(2)}, u32[]{:S(2)}) collective-permute-start(bf16[2,34,320]{2,1,0:T(8,128)(2,1)S(1)} %get-tuple-element.14), channel_id=1, source_target_pairs={{1,2},{2,1},{3,4},{4,3},{5,6},{6,5},{9,10},{10,9},{11,12},{12,11},... | collective-permute-start | bytes 130568 | tf_op jit(solution)/shard_map/ppermute | solution.py:127

commit v14 on v13

--- a/solution.py
+++ b/solution.py
@@ -162,7 +162,9 @@
         hidden.reshape(frames, chans, rows, cols).transpose(0, 2, 3, 1).reshape(frames, rows, merged)
     )
 
-    halo_top, halo_bot = exchange(hid[:, rows - 1 :, :], hid[:, :1, :], "row")
+    as_row = lambda a: a.transpose(0, 2, 1).reshape(frames, 1, merged)
+    edge_top, edge_bot = exchange(hidden[:, :, points - cols :], hidden[:, :, :cols], "row")
+    halo_top, halo_bot = as_row(edge_top), as_row(edge_bot)
     tall = jnp.concatenate([halo_top, hid, halo_bot], axis=1)
     halo_left, halo_right = exchange(tall[:, :, merged - chans :], tall[:, :, :chans], "col")
     padded = jnp.concatenate([halo_left, tall, halo_right], axis=2)

time: 43.3 us -> 44 us (1.016)
  other arithmetic: 4.47 us -> 5.47 us
  waiting for transfers between devices: 11.5 us -> 10.8 us
  local copies, waits for them, and re-layouts: 9.55 us -> 10 us
    select_n x2, other arithmetic: 0.08 us -> 1.12 us  [swap(): payload = jnp.where(even, send_even, send_odd)]
    ppermute x5, waiting for transfers between devices: 11.5 us -> 10.8 us  [swap(): return lax.ppermute(payload, axis, pairs)]
  transfers between devices with their start and end apart: 5 -> 5, of which waited for: 3 -> 3; matrix products, arithmetic and copies ran while one was open for 17% -> 21% of each run, Pallas kernels for 0% -> 0%
where the time goes in v14:
time: 44 us; the launch traced here: 43.8 us
  waiting for transfers between devices  10.8 us (25%)
  starting transfers between devices  10.6 us (24%)
  local copies, waits for them, and re-layouts  10 us (23%)
  Pallas kernels  6.79 us (15%)
  other arithmetic  5.47 us (12%)
    ppermute x5, waiting for transfers between devices, swap(): return lax.ppermute(payload, axis, pairs)  10.8 us
    ppermute x5, starting transfers between devices, swap(): return lax.ppermute(payload, axis, pairs)  10.6 us
    pallas_call x1, Pallas kernels, attend(): pl.pallas_call(attend_kernel, grid=grid, in_specs=[pl.BlockSpec(memory_sp...  6.79 us
    reshape x4, local copies, waits for them, and re-layouts, body(): a.reshape(frames, rows, cols, chans).transpose(0, 3, 1, 2)  3.8 us
    unnamed x12, local copies, waits for them, and re-layouts  2.88 us
    convert_element_type x1, other arithmetic, body(): return acc.astype(jnp.bfloat16)  2.85 us
    pallas_call x1, local copies, waits for them, and re-layouts, attend(): pl.pallas_call(attend_kernel, grid=grid, in_specs=[pl.BlockSpec(memory_sp...  1.44 us
    select_n x2, other arithmetic, swap(): payload = jnp.where(even, send_even, send_odd)  1.12 us
  transfers between devices with their start and end apart: 5, of which 3 were waited for; matrix products, arithmetic and copies ran while one was open for 21% of the time, Pallas kernels for 0%

profile of v14, /device:TPU:152, one launch (start us, length us, event | category | flops | bytes accessed | tf_op | source)
XLA Modules:
  0.0 43.8 jit_solution(7720870891062508486)
XLA Ops:
  0.0 1.9 %collective-permute-start.1 = (bf16[2,32,5120]{2,1,0:T(8,128)(2,1)}, bf16[2,32,5120]{2,1,0:T(8,128)(2,1)S(1)}, u32[]{:S(2)}, u32[]{:S(2)}) collective-permute-start(bf16[2,32,5120]{2,1,0:T(8,128)(2,1)} %param.4), channel_id=1, source_target_pairs={{16,32},{32,16},{48,64},{64,48},{80,96},{96,80},{112,128},{128,112... | collective-permute-start | bytes 1966088 | tf_op jit(solution)/shard_map/ppermute | solution.py:127
  1.9 1.8 %reshape.72 = bf16[2,32,16,320]{3,2,1,0:T(8,128)(2,1)S(1)} reshape(bf16[2,32,5120]{2,1,0:T(8,128)(2,1)} %param.4) | data formatting | bytes 1310720 | tf_op jit(solution)/shard_map/reshape | solution.py:147
  3.7 0.0 copy-start.1
  3.7 0.3 copy.10.own_ref
  4.0 0.0 copy-start
  4.0 0.0 copy-start.3
  4.0 1.2 %collective-permute-start = (bf16[2,320,512]{2,1,0:T(8,128)(2,1)S(1)}, bf16[2,320,512]{2,1,0:T(8,128)(2,1)S(1)}, u32[]{:S(2)}, u32[]{:S(2)}) collective-permute-start(bf16[2,320,512]{2,1,0:T(8,128)(2,1)S(1)} %copy.10.own_ref), channel_id=1, source_target_pairs={{0,16},{16,0},{32,48},{48,32},{64,80},{80,64},{96,112},{112,96},{1... | collective-permute-start | bytes 1966088 | tf_op jit(solution)/shard_map/ppermute | solution.py:127
  5.2 0.0 copy-done.1
  5.2 1.2 %copy.11 = bf16[320,960]{0,1:T(8,128)(2,1)} copy(bf16[320,960]{1,0:T(8,128)(2,1)S(1)} %copy-done.1) | data formatting | bytes 1228800 | tf_op args[1]
  6.4 0.0 copy-done.3
  6.4 0.9 %copy.12 = bf16[320,320]{0,1:T(8,128)(2,1)} copy(bf16[320,320]{1,0:T(8,128)(2,1)S(1)} %copy-done.3) | data formatting | bytes 409600 | tf_op args[2]
  7.2 0.0 copy-done
  7.3 0.6 %add_convert_fusion.valid_ref = s32[7]{0:T(128)} fusion(pred[1]{0:T(512)(128)(4,1)} %bitcast, pred[6]{0:T(512)(128)(4,1)S(1)} %compare_and_fusion), kind=kLoop, calls=%fused_computation.25 | loop fusion | flops 14 | bytes 35 | tf_op jit(solution)/shard_map/concatenate | solution.py:159
  7.8 5.5 %collective-permute-done.1 = bf16[2,32,5120]{2,1,0:T(8,128)(2,1)S(1)} collective-permute-done((bf16[2,32,5120]{2,1,0:T(8,128)(2,1)}, bf16[2,32,5120]{2,1,0:T(8,128)(2,1)S(1)}, u32[]{:S(2)}, u32[]{:S(2)}) %collective-permute-start.1) | collective-permute-done | bytes 655392 | tf_op jit(solution)/shard_map/ppermute | solution.py:127
  13.3 0.6 %reshape.74 = bf16[2,32,16,320]{3,2,1,0:T(8,128)(2,1)S(1)} reshape(bf16[2,32,5120]{2,1,0:T(8,128)(2,1)S(1)} %collective-permute-done.1) | data formatting | bytes 1310720 | tf_op jit(solution)/shard_map/reshape | solution.py:147
  13.9 1.1 %copy.14.b_ref = bf16[2,320,512]{2,1,0:T(8,128)(2,1)} copy(bf16[2,320,512]{1,2,0:T(8,128)(2,1)S(1)} %bitcast.18) | data formatting | bytes 1310720 | tf_op jit(solution)/shard_map/reshape | solution.py:147
  15.1 0.0 collective-permute-done.a_ref
  15.1 0.0 copy-start.2
  15.1 0.8 %copy-done.2 = bf16[2,320,512]{2,1,0:T(8,128)(2,1)} copy-done((bf16[2,320,512]{2,1,0:T(8,128)(2,1)}, bf16[2,320,512]{2,1,0:T(8,128)(2,1)S(1)}, u32[]{:S(2)}) %copy-start.2) | copy-done | bytes 655384
  15.9 6.8 %shard_map.46 = bf16[2,320,512]{2,1,0:T(8,128)(2,1)} custom-call(s32[7]{0:T(128)} %add_convert_fusion.valid_ref, bf16[2,320,512]{2,1,0:T(8,128)(2,1)} %copy-done.2, bf16[2,320,512]{2,1,0:T(8,128)(2,1)} %copy-done, bf16[2,320,512]{2,1,0:T(8,128)(2,1)} %copy.14.b_ref, bf16[960,320]{1,0:T(8,128)(2,1)} %bitcast.21, bf16[320,320]{1,0:T(8,128)(2,1)} %bitcast.22), custom_call_target="tpu_custom_call" | custom-call | tf_op jit(solution)/shard_map/pallas_call | solution.py:92
  22.7 1.1 %slice_select_fusion = bf16[2,320,16]{2,1,0:T(8,128)(2,1)S(1)} fusion(bf16[2,320,512]{2,1,0:T(8,128)(2,1)} %shard_map.46, pred[]{:T(512)S(6)} %eq.25), kind=kLoop, calls=%fused_computation.15 | loop fusion | flops 10240 | bytes 61441 | tf_op jit(solution)/shard_map/jit(_where)/select_n | solution.py:126
  23.8 3.3 %collective-permute-start.2 = (bf16[2,320,16]{2,1,0:T(8,128)(2,1)S(1)}, bf16[2,320,16]{2,1,0:T(8,128)(2,1)S(1)}, u32[]{:S(2)}, u32[]{:S(2)}) collective-permute-start(bf16[2,320,16]{2,1,0:T(8,128)(2,1)S(1)} %slice_select_fusion), channel_id=1, source_target_pairs={{0,8},{8,0},{1,9},{9,1},{2,10},{10,2},{3,11},{11,3},{4,12},{12,4},... | collective-permute-start | bytes 61448 | tf_op jit(solution)/shard_map/ppermute | solution.py:127
  27.1 1.4 %copy.15 = bf16[2,320,512]{1,2,0:T(8,128)(2,1)S(1)} copy(bf16[2,320,512]{2,1,0:T(8,128)(2,1)} %shard_map.46) | data formatting | bytes 1310720 | tf_op jit(solution)/shard_map/pallas_call | solution.py:92
  28.6 0.6 %reshape.77 = bf16[2,32,5120]{2,1,0:T(8,128)(2,1)S(1)} reshape(bf16[2,32,16,320]{3,2,1,0:T(8,128)(2,1)S(1)} %bitcast.19) | data formatting | bytes 1310720 | tf_op jit(solution)/shard_map/reshape | solution.py:162
  29.2 1.7 %collective-permute-done.2 = bf16[2,320,16]{2,1,0:T(8,128)(2,1)S(1)} collective-permute-done((bf16[2,320,16]{2,1,0:T(8,128)(2,1)S(1)}, bf16[2,320,16]{2,1,0:T(8,128)(2,1)S(1)}, u32[]{:S(2)}, u32[]{:S(2)}) %collective-permute-start.2) | collective-permute-done | bytes 20512 | tf_op jit(solution)/shard_map/ppermute | solution.py:127
  31.0 0.0 copy-start.4
  31.0 0.1 copy.16
  31.1 0.1 reshape.80
  31.2 0.1 copy.17
  31.3 0.1 reshape.81
  31.4 0.1 broadcast_select_fusion.3
  31.6 1.6 %collective-permute-start.4 = (bf16[2,34,320]{2,1,0:T(8,128)(2,1)S(1)}, bf16[2,34,320]{2,1,0:T(8,128)(2,1)S(1)}, u32[]{:S(2)}, u32[]{:S(2)}) collective-permute-start(bf16[2,34,320]{2,1,0:T(8,128)(2,1)S(1)} %broadcast_select_fusion.2), channel_id=1, source_target_pairs={{0,1},{1,0},{2,3},{3,2},{4,5},{5,4},{6,7},{7,6},{8,9},{9,8},{10,11... | collective-permute-start | bytes 130568 | tf_op jit(solution)/shard_map/ppermute | solution.py:127
  33.2 2.6 %collective-permute-start.3 = (bf16[2,34,320]{2,1,0:T(8,128)(2,1)S(1)}, bf16[2,34,320]{2,1,0:T(8,128)(2,1)S(1)}, u32[]{:S(2)}, u32[]{:S(2)}) collective-permute-start(bf16[2,34,320]{2,1,0:T(8,128)(2,1)S(1)} %get-tuple-element.14), channel_id=1, source_target_pairs={{1,2},{2,1},{3,4},{4,3},{5,6},{6,5},{9,10},{10,9},{11,12},{12,11},... | collective-permute-start | bytes 130568 | tf_op jit(solution)/shard_map/ppermute | solution.py:127
  35.8 0.0 copy-done.4
  35.8 0.1 slice_reduce_fusion.8
  35.8 0.1 tile.42
  35.9 0.1 tile.44
  36.0 0.1 tile.46
  36.1 0.1 tile.48
  36.2 0.1 tile.50
  36.3 0.1 tile.52
  36.3 0.1 tile.54
  36.4 0.1 tile.56
  36.5 0.1 tile.58
  36.6 0.0 collective-permute-done.4
  36.6 3.6 %collective-permute-done.3 = bf16[2,34,320]{2,1,0:T(8,128)(2,1)S(1)} collective-permute-done((bf16[2,34,320]{2,1,0:T(8,128)(2,1)S(1)}, bf16[2,34,320]{2,1,0:T(8,128)(2,1)S(1)}, u32[]{:S(2)}, u32[]{:S(2)}) %collective-permute-start.3) | collective-permute-done | bytes 43552 | tf_op jit(solution)/shard_map/ppermute | solution.py:127
  40.2 0.8 %maximum_maximum_fusion = (bf16[2,34,5440]{2,1,0:T(8,128)(2,1)S(1)}, bf16[2,34,5440]{2,1,0:T(8,128)(2,1)S(1)}) fusion(bf16[2,1,5120]{2,1,0:T(2,128)(2,1)S(1)} %reshape.81, bf16[2,32,5120]{2,1,0:T(8,128)(2,1)S(1)} %reshape.77, bf16[2,1,5120]{2,1,0:T(2,128)(2,1)S(1)} %reshape.80, bf16[2,34,320]{2,1,0:T(8,128)(2,1)S(1)} %get-tuple-element.21, ...), kind=kLoop, calls=%fused_computation.11 | loop fusion | flops 5918720 | bytes 2263040 | tf_op jit(solution)/shard_map/concatenate | solution.py:170
  40.9 2.8 %fusion.8 = bf16[2,32,5120]{2,1,0:T(8,128)(2,1)} fusion(bf16[2,32,5120]{2,1,0:T(8,128)(2,1)S(1)} %reshape.77, bf16[2,34,5440]{2,1,0:T(8,128)(2,1)S(1)} %get-tuple-element.18, bf16[2,1,5120]{2,1,0:T(2,128)(2,1)S(1)} %reshape.81, bf16[2,34,5440]{2,1,0:T(8,128)(2,1)S(1)} %get-tuple-element.17, bf16[2,1,5120]{2,1,0:T(2,128)(2,1)S(1)} %reshape.80, ...), kind=kLoop, calls=%fused_computation.10 | loop fusion | flops 11141120 | bytes 5468160 | tf_op jit(solution)/shard_map/convert_element_type | solution.py:182
  (13 shorter events, 0.1 us)
Async XLA Ops:
  0.0 13.3 %collective-permute-start.1 = (bf16[2,32,5120]{2,1,0:T(8,128)(2,1)}, bf16[2,32,5120]{2,1,0:T(8,128)(2,1)S(1)}, u32[]{:S(2)}, u32[]{:S(2)}) collective-permute-start(bf16[2,32,5120]{2,1,0:T(8,128)(2,1)} %param.4), channel_id=1, source_target_pairs={{16,32},{32,16},{48,64},{64,48},{80,96},{96,80},{112,128},{128,112... | collective-permute-start | bytes 1966088 | tf_op jit(solution)/shard_map/ppermute | solution.py:127
  3.7 1.5 %copy-start.1 = (bf16[320,960]{1,0:T(8,128)(2,1)S(1)}, bf16[320,960]{1,0:T(8,128)(2,1)}, u32[]{:S(2)}) copy-start(bf16[320,960]{1,0:T(8,128)(2,1)} %param.5) | copy-start | bytes 1843204
  4.0 3.3 %copy-start = (bf16[2,320,512]{2,1,0:T(8,128)(2,1)}, bf16[2,320,512]{2,1,0:T(8,128)(2,1)S(1)}, u32[]{:S(2)}) copy-start(bf16[2,320,512]{2,1,0:T(8,128)(2,1)S(1)} %copy.10.own_ref) | copy-start | bytes 1966084
  4.0 2.4 %copy-start.3 = (bf16[320,320]{1,0:T(8,128)(2,1)S(1)}, bf16[320,320]{1,0:T(8,128)(2,1)}, u32[]{:S(2)}) copy-start(bf16[320,320]{1,0:T(8,128)(2,1)} %param.6) | copy-start | bytes 614404
  4.0 11.1 %collective-permute-start = (bf16[2,320,512]{2,1,0:T(8,128)(2,1)S(1)}, bf16[2,320,512]{2,1,0:T(8,128)(2,1)S(1)}, u32[]{:S(2)}, u32[]{:S(2)}) collective-permute-start(bf16[2,320,512]{2,1,0:T(8,128)(2,1)S(1)} %copy.10.own_ref), channel_id=1, source_target_pairs={{0,16},{16,0},{32,48},{48,32},{64,80},{80,64},{96,112},{112,96},{1... | collective-permute-start | bytes 1966088 | tf_op jit(solution)/shard_map/ppermute | solution.py:127
  15.1 0.8 %copy-start.2 = (bf16[2,320,512]{2,1,0:T(8,128)(2,1)}, bf16[2,320,512]{2,1,0:T(8,128)(2,1)S(1)}, u32[]{:S(2)}) copy-start(bf16[2,320,512]{2,1,0:T(8,128)(2,1)S(1)} %collective-permute-done.a_ref) | copy-start | bytes 1966084
  23.8 7.1 %collective-permute-start.2 = (bf16[2,320,16]{2,1,0:T(8,128)(2,1)S(1)}, bf16[2,320,16]{2,1,0:T(8,128)(2,1)S(1)}, u32[]{:S(2)}, u32[]{:S(2)}) collective-permute-start(bf16[2,320,16]{2,1,0:T(8,128)(2,1)S(1)} %slice_select_fusion), channel_id=1, source_target_pairs={{0,8},{8,0},{1,9},{9,1},{2,10},{10,2},{3,11},{11,3},{4,12},{12,4},... | collective-permute-start | bytes 61448 | tf_op jit(solution)/shard_map/ppermute | solution.py:127
  31.0 4.8 %copy-start.4 = (f32[9,320]{1,0:T(8,128)S(1)}, f32[9,320]{1,0:T(8,128)}, u32[]{:S(2)}) copy-start(f32[9,320]{1,0:T(8,128)} %param.7) | copy-start | bytes 34564
  31.6 5.0 %collective-permute-start.4 = (bf16[2,34,320]{2,1,0:T(8,128)(2,1)S(1)}, bf16[2,34,320]{2,1,0:T(8,128)(2,1)S(1)}, u32[]{:S(2)}, u32[]{:S(2)}) collective-permute-start(bf16[2,34,320]{2,1,0:T(8,128)(2,1)S(1)} %broadcast_select_fusion.2), channel_id=1, source_target_pairs={{0,1},{1,0},{2,3},{3,2},{4,5},{5,4},{6,7},{7,6},{8,9},{9,8},{10,11... | collective-permute-start | bytes 130568 | tf_op jit(solution)/shard_map/ppermute | solution.py:127
  33.2 7.0 %collective-permute-start.3 = (bf16[2,34,320]{2,1,0:T(8,128)(2,1)S(1)}, bf16[2,34,320]{2,1,0:T(8,128)(2,1)S(1)}, u32[]{:S(2)}, u32[]{:S(2)}) collective-permute-start(bf16[2,34,320]{2,1,0:T(8,128)(2,1)S(1)} %get-tuple-element.14), channel_id=1, source_target_pairs={{1,2},{2,1},{3,4},{4,3},{5,6},{6,5},{9,10},{10,9},{11,12},{12,11},... | collective-permute-start | bytes 130568 | tf_op jit(solution)/shard_map/ppermute | solution.py:127

commit v15 on v13

--- a/solution.py
+++ b/solution.py
@@ -162,10 +162,10 @@
         hidden.reshape(frames, chans, rows, cols).transpose(0, 2, 3, 1).reshape(frames, rows, merged)
     )
 
-    halo_top, halo_bot = exchange(hid[:, rows - 1 :, :], hid[:, :1, :], "row")
-    tall = jnp.concatenate([halo_top, hid, halo_bot], axis=1)
-    halo_left, halo_right = exchange(tall[:, :, merged - chans :], tall[:, :, :chans], "col")
-    padded = jnp.concatenate([halo_left, tall, halo_right], axis=2)
+    halo_left, halo_right = exchange(hid[:, :, merged - chans :], hid[:, :, :chans], "col")
+    wide = jnp.concatenate([halo_left, hid, halo_right], axis=2)
+    halo_top, halo_bot = exchange(wide[:, rows - 1 :, :], wide[:, :1, :], "row")
+    padded = jnp.concatenate([halo_top, wide, halo_bot], axis=1)
     taps = jnp.tile(conv_weight, (1, cols))
     acc = hid.astype(jnp.float32)
     for tap_a in range(3):

time: 43.3 us -> 44.6 us (1.030)
  other arithmetic: 4.47 us -> 5.51 us
  starting transfers between devices: 10.6 us -> 9.8 us
  local copies, waits for them, and re-layouts: 9.55 us -> 10.3 us
    convert_element_type x1, other arithmetic: 2.85 us -> 4.65 us  [body(): return acc.astype(jnp.bfloat16)]
    ppermute x5, starting transfers between devices: 10.6 us -> 9.8 us  [swap(): return lax.ppermute(payload, axis, pairs)]
    concatenate x0 -> x1, local copies, waits for them, and re-layouts: none -> 0.78 us  [body(): wide = jnp.concatenate([halo_left, hid, halo_right], axis=2)]
    concatenate x1 -> x0, other arithmetic: 0.75 us -> none  [body(): padded = jnp.concatenate([halo_left, tall, halo_right], axis=2)]
  transfers between devices with their start and end apart: 5 -> 5, of which waited for: 3 -> 4; matrix products, arithmetic and copies ran while one was open for 17% -> 16% of each run, Pallas kernels for 0% -> 0%
where the time goes in v15:
time: 44.6 us; the launch traced here: 44.1 us
  waiting for transfers between devices  11.6 us (26%)
  local copies, waits for them, and re-layouts  10.3 us (23%)
  starting transfers between devices  9.8 us (22%)
  Pallas kernels  6.79 us (15%)
  other arithmetic  5.51 us (12%)
    ppermute x5, waiting for transfers between devices, swap(): return lax.ppermute(payload, axis, pairs)  11.6 us
    ppermute x5, starting transfers between devices, swap(): return lax.ppermute(payload, axis, pairs)  9.8 us
    pallas_call x1, Pallas kernels, attend(): pl.pallas_call(attend_kernel, grid=grid, in_specs=[pl.BlockSpec(memory_sp...  6.79 us
    convert_element_type x1, other arithmetic, body(): return acc.astype(jnp.bfloat16)  4.65 us
    reshape x4, local copies, waits for them, and re-layouts, body(): a.reshape(frames, rows, cols, chans).transpose(0, 3, 1, 2)  3.8 us
    unnamed x12, local copies, waits for them, and re-layouts  2.88 us
    pallas_call x1, local copies, waits for them, and re-layouts, attend(): pl.pallas_call(attend_kernel, grid=grid, in_specs=[pl.BlockSpec(memory_sp...  1.44 us
  transfers between devices with their start and end apart: 5, of which 4 were waited for; matrix products, arithmetic and copies ran while one was open for 16% of the time, Pallas kernels for 0%

profile of v15, /device:TPU:152, one launch (start us, length us, event | category | flops | bytes accessed | tf_op | source)
XLA Modules:
  0.0 44.1 jit_solution(1201413178801766397)
XLA Ops:
  0.0 1.9 %collective-permute-start.1 = (bf16[2,32,5120]{2,1,0:T(8,128)(2,1)}, bf16[2,32,5120]{2,1,0:T(8,128)(2,1)S(1)}, u32[]{:S(2)}, u32[]{:S(2)}) collective-permute-start(bf16[2,32,5120]{2,1,0:T(8,128)(2,1)} %param.4), channel_id=1, source_target_pairs={{16,32},{32,16},{48,64},{64,48},{80,96},{96,80},{112,128},{128,112... | collective-permute-start | bytes 1966088 | tf_op jit(solution)/shard_map/ppermute | solution.py:127
  1.9 1.8 %reshape.66 = bf16[2,32,16,320]{3,2,1,0:T(8,128)(2,1)S(1)} reshape(bf16[2,32,5120]{2,1,0:T(8,128)(2,1)} %param.4) | data formatting | bytes 1310720 | tf_op jit(solution)/shard_map/reshape | solution.py:147
  3.7 0.0 copy-start.1
  3.7 0.3 copy.10.own_ref
  4.0 0.0 copy-start
  4.0 0.0 copy-start.3
  4.0 1.2 %collective-permute-start = (bf16[2,320,512]{2,1,0:T(8,128)(2,1)S(1)}, bf16[2,320,512]{2,1,0:T(8,128)(2,1)S(1)}, u32[]{:S(2)}, u32[]{:S(2)}) collective-permute-start(bf16[2,320,512]{2,1,0:T(8,128)(2,1)S(1)} %copy.10.own_ref), channel_id=1, source_target_pairs={{0,16},{16,0},{32,48},{48,32},{64,80},{80,64},{96,112},{112,96},{1... | collective-permute-start | bytes 1966088 | tf_op jit(solution)/shard_map/ppermute | solution.py:127
  5.2 0.0 copy-done.1
  5.2 1.2 %copy.11 = bf16[320,960]{0,1:T(8,128)(2,1)} copy(bf16[320,960]{1,0:T(8,128)(2,1)S(1)} %copy-done.1) | data formatting | bytes 1228800 | tf_op args[1]
  6.4 0.0 copy-done.3
  6.4 0.9 %copy.12 = bf16[320,320]{0,1:T(8,128)(2,1)} copy(bf16[320,320]{1,0:T(8,128)(2,1)S(1)} %copy-done.3) | data formatting | bytes 409600 | tf_op args[2]
  7.2 0.0 copy-done
  7.3 0.6 %add_convert_fusion.valid_ref = s32[7]{0:T(128)} fusion(pred[1]{0:T(512)(128)(4,1)} %bitcast, pred[6]{0:T(512)(128)(4,1)S(1)} %compare_and_fusion), kind=kLoop, calls=%fused_computation.34 | loop fusion | flops 14 | bytes 35 | tf_op jit(solution)/shard_map/concatenate | solution.py:159
  7.8 5.5 %collective-permute-done.1 = bf16[2,32,5120]{2,1,0:T(8,128)(2,1)S(1)} collective-permute-done((bf16[2,32,5120]{2,1,0:T(8,128)(2,1)}, bf16[2,32,5120]{2,1,0:T(8,128)(2,1)S(1)}, u32[]{:S(2)}, u32[]{:S(2)}) %collective-permute-start.1) | collective-permute-done | bytes 655392 | tf_op jit(solution)/shard_map/ppermute | solution.py:127
  13.3 0.6 %reshape.68 = bf16[2,32,16,320]{3,2,1,0:T(8,128)(2,1)S(1)} reshape(bf16[2,32,5120]{2,1,0:T(8,128)(2,1)S(1)} %collective-permute-done.1) | data formatting | bytes 1310720 | tf_op jit(solution)/shard_map/reshape | solution.py:147
  13.9 1.1 %copy.14.b_ref = bf16[2,320,512]{2,1,0:T(8,128)(2,1)} copy(bf16[2,320,512]{1,2,0:T(8,128)(2,1)S(1)} %bitcast.14) | data formatting | bytes 1310720 | tf_op jit(solution)/shard_map/reshape | solution.py:147
  15.1 0.0 collective-permute-done.a_ref
  15.1 0.0 copy-start.2
  15.1 0.8 %copy-done.2 = bf16[2,320,512]{2,1,0:T(8,128)(2,1)} copy-done((bf16[2,320,512]{2,1,0:T(8,128)(2,1)}, bf16[2,320,512]{2,1,0:T(8,128)(2,1)S(1)}, u32[]{:S(2)}) %copy-start.2) | copy-done | bytes 655384
  15.9 6.8 %shard_map.46 = bf16[2,320,512]{2,1,0:T(8,128)(2,1)} custom-call(s32[7]{0:T(128)} %add_convert_fusion.valid_ref, bf16[2,320,512]{2,1,0:T(8,128)(2,1)} %copy-done.2, bf16[2,320,512]{2,1,0:T(8,128)(2,1)} %copy-done, bf16[2,320,512]{2,1,0:T(8,128)(2,1)} %copy.14.b_ref, bf16[960,320]{1,0:T(8,128)(2,1)} %bitcast.17, bf16[320,320]{1,0:T(8,128)(2,1)} %bitcast.18), custom_call_target="tpu_custom_call" | custom-call | tf_op jit(solution)/shard_map/pallas_call | solution.py:92
  22.7 1.4 %copy.15 = bf16[2,320,512]{1,2,0:T(8,128)(2,1)S(1)} copy(bf16[2,320,512]{2,1,0:T(8,128)(2,1)} %shard_map.46) | data formatting | bytes 1310720 | tf_op jit(solution)/shard_map/pallas_call | solution.py:92
  24.2 0.6 %reshape.71 = bf16[2,32,5120]{2,1,0:T(8,128)(2,1)S(1)} reshape(bf16[2,32,16,320]{3,2,1,0:T(8,128)(2,1)S(1)} %bitcast.15) | data formatting | bytes 1310720 | tf_op jit(solution)/shard_map/reshape | solution.py:162
  24.8 0.1 broadcast_select_fusion.5
  24.9 3.6 %collective-permute-start.2 = (bf16[2,32,320]{2,1,0:T(8,128)(2,1)S(1)}, bf16[2,32,320]{2,1,0:T(8,128)(2,1)S(1)}, u32[]{:S(2)}, u32[]{:S(2)}) collective-permute-start(bf16[2,32,320]{2,1,0:T(8,128)(2,1)S(1)} %get-tuple-element.15), channel_id=1, source_target_pairs={{1,2},{2,1},{3,4},{4,3},{5,6},{6,5},{9,10},{10,9},{11,12},{12,11},... | collective-permute-start | bytes 122888 | tf_op jit(solution)/shard_map/ppermute | solution.py:127
  28.5 0.3 collective-permute-start.3
  28.8 3.0 %collective-permute-done.2 = bf16[2,32,320]{2,1,0:T(8,128)(2,1)S(1)} collective-permute-done((bf16[2,32,320]{2,1,0:T(8,128)(2,1)S(1)}, bf16[2,32,320]{2,1,0:T(8,128)(2,1)S(1)}, u32[]{:S(2)}, u32[]{:S(2)}) %collective-permute-start.2) | collective-permute-done | bytes 40992 | tf_op jit(solution)/shard_map/ppermute | solution.py:127
  31.8 1.1 %collective-permute-done.3 = bf16[2,32,320]{2,1,0:T(8,128)(2,1)S(1)} collective-permute-done((bf16[2,32,320]{2,1,0:T(8,128)(2,1)S(1)}, bf16[2,32,320]{2,1,0:T(8,128)(2,1)S(1)}, u32[]{:S(2)}, u32[]{:S(2)}) %collective-permute-start.3) | collective-permute-done | bytes 40992 | tf_op jit(solution)/shard_map/ppermute | solution.py:127
  32.9 0.0 copy-start.4
  32.9 0.8 %concatenate.27 = bf16[2,32,5760]{2,1,0:T(8,128)(2,1)S(1)} concatenate(bf16[2,32,320]{2,1,0:T(8,128)(2,1)S(1)} %get-tuple-element.17, bf16[2,32,5120]{2,1,0:T(8,128)(2,1)S(1)} %reshape.71, bf16[2,32,320]{2,1,0:T(8,128)(2,1)S(1)} %get-tuple-element.16), dimensions={2} | concatenate | bytes 1474560 | tf_op jit(solution)/shard_map/concatenate | solution.py:166
  33.7 0.1 broadcast_select_fusion.2
  33.7 2.8 %collective-permute-start.4 = (bf16[2,1,5760]{2,1,0:T(2,128)(2,1)S(1)}, bf16[2,1,5760]{2,1,0:T(2,128)(2,1)S(1)}, u32[]{:S(2)}, u32[]{:S(2)}) collective-permute-start(bf16[2,1,5760]{2,1,0:T(2,128)(2,1)S(1)} %broadcast_select_fusion.2), channel_id=1, source_target_pairs={{0,8},{8,0},{1,9},{9,1},{2,10},{10,2},{3,11},{11,3},{4,12},{12,4},... | collective-permute-start | bytes 69128 | tf_op jit(solution)/shard_map/ppermute | solution.py:127
  36.6 0.0 copy-done.4
  36.6 0.1 slice_reduce_fusion.8
  36.6 0.1 tile.42
  36.7 0.1 tile.44
  36.8 0.1 tile.46
  36.9 0.1 tile.48
  37.0 0.1 tile.50
  37.0 0.1 tile.52
  37.1 0.1 tile.54
  37.2 0.1 tile.56
  37.3 0.1 tile.58
  37.4 2.0 %collective-permute-done.4 = bf16[2,1,5760]{2,1,0:T(2,128)(2,1)S(1)} collective-permute-done((bf16[2,1,5760]{2,1,0:T(2,128)(2,1)S(1)}, bf16[2,1,5760]{2,1,0:T(2,128)(2,1)S(1)}, u32[]{:S(2)}, u32[]{:S(2)}) %collective-permute-start.4) | collective-permute-done | bytes 23072 | tf_op jit(solution)/shard_map/ppermute | solution.py:127
  39.4 0.1 broadcast_select_fusion.1
  39.5 4.7 %fusion.8 = bf16[2,32,5120]{2,1,0:T(8,128)(2,1)} fusion(bf16[2,32,5120]{2,1,0:T(8,128)(2,1)S(1)} %reshape.71, bf16[2,32,5760]{2,1,0:T(8,128)(2,1)S(1)} %concatenate.27, bf16[2,1,5760]{2,1,0:T(2,128)(2,1)S(1)} %get-tuple-element.19, bf16[2,1,5760]{2,1,0:T(2,128)(2,1)S(1)} %get-tuple-element.18, bf16[2,32,320]{2,1,0:T(8,128)(2,1)S(1)} %get-tuple-element.16, ...), kind=kLoop, calls=%fused_computation.10 | loop fusion | flops 17039360 | bytes 2360320 | tf_op jit(solution)/shard_map/convert_element_type | solution.py:180
  (11 shorter events, 0.0 us)
Async XLA Ops:
  0.0 13.3 %collective-permute-start.1 = (bf16[2,32,5120]{2,1,0:T(8,128)(2,1)}, bf16[2,32,5120]{2,1,0:T(8,128)(2,1)S(1)}, u32[]{:S(2)}, u32[]{:S(2)}) collective-permute-start(bf16[2,32,5120]{2,1,0:T(8,128)(2,1)} %param.4), channel_id=1, source_target_pairs={{16,32},{32,16},{48,64},{64,48},{80,96},{96,80},{112,128},{128,112... | collective-permute-start | bytes 1966088 | tf_op jit(solution)/shard_map/ppermute | solution.py:127
  3.7 1.5 %copy-start.1 = (bf16[320,960]{1,0:T(8,128)(2,1)S(1)}, bf16[320,960]{1,0:T(8,128)(2,1)}, u32[]{:S(2)}) copy-start(bf16[320,960]{1,0:T(8,128)(2,1)} %param.5) | copy-start | bytes 1843204
  4.0 3.3 %copy-start = (bf16[2,320,512]{2,1,0:T(8,128)(2,1)}, bf16[2,320,512]{2,1,0:T(8,128)(2,1)S(1)}, u32[]{:S(2)}) copy-start(bf16[2,320,512]{2,1,0:T(8,128)(2,1)S(1)} %copy.10.own_ref) | copy-start | bytes 1966084
  4.0 2.4 %copy-start.3 = (bf16[320,320]{1,0:T(8,128)(2,1)S(1)}, bf16[320,320]{1,0:T(8,128)(2,1)}, u32[]{:S(2)}) copy-start(bf16[320,320]{1,0:T(8,128)(2,1)} %param.6) | copy-start | bytes 614404
  4.0 11.1 %collective-permute-start = (bf16[2,320,512]{2,1,0:T(8,128)(2,1)S(1)}, bf16[2,320,512]{2,1,0:T(8,128)(2,1)S(1)}, u32[]{:S(2)}, u32[]{:S(2)}) collective-permute-start(bf16[2,320,512]{2,1,0:T(8,128)(2,1)S(1)} %copy.10.own_ref), channel_id=1, source_target_pairs={{0,16},{16,0},{32,48},{48,32},{64,80},{80,64},{96,112},{112,96},{1... | collective-permute-start | bytes 1966088 | tf_op jit(solution)/shard_map/ppermute | solution.py:127
  15.1 0.8 %copy-start.2 = (bf16[2,320,512]{2,1,0:T(8,128)(2,1)}, bf16[2,320,512]{2,1,0:T(8,128)(2,1)S(1)}, u32[]{:S(2)}) copy-start(bf16[2,320,512]{2,1,0:T(8,128)(2,1)S(1)} %collective-permute-done.a_ref) | copy-start | bytes 1966084
  24.9 6.9 %collective-permute-start.2 = (bf16[2,32,320]{2,1,0:T(8,128)(2,1)S(1)}, bf16[2,32,320]{2,1,0:T(8,128)(2,1)S(1)}, u32[]{:S(2)}, u32[]{:S(2)}) collective-permute-start(bf16[2,32,320]{2,1,0:T(8,128)(2,1)S(1)} %get-tuple-element.15), channel_id=1, source_target_pairs={{1,2},{2,1},{3,4},{4,3},{5,6},{6,5},{9,10},{10,9},{11,12},{12,11},... | collective-permute-start | bytes 122888 | tf_op jit(solution)/shard_map/ppermute | solution.py:127
  28.5 4.4 %collective-permute-start.3 = (bf16[2,32,320]{2,1,0:T(8,128)(2,1)S(1)}, bf16[2,32,320]{2,1,0:T(8,128)(2,1)S(1)}, u32[]{:S(2)}, u32[]{:S(2)}) collective-permute-start(bf16[2,32,320]{2,1,0:T(8,128)(2,1)S(1)} %get-tuple-element.14), channel_id=1, source_target_pairs={{0,1},{1,0},{2,3},{3,2},{4,5},{5,4},{6,7},{7,6},{8,9},{9,8},{10,11... | collective-permute-start | bytes 122888 | tf_op jit(solution)/shard_map/ppermute | solution.py:127
  32.9 3.7 %copy-start.4 = (f32[9,320]{1,0:T(8,128)S(1)}, f32[9,320]{1,0:T(8,128)}, u32[]{:S(2)}) copy-start(f32[9,320]{1,0:T(8,128)} %param.7) | copy-start | bytes 34564
  33.7 5.6 %collective-permute-start.4 = (bf16[2,1,5760]{2,1,0:T(2,128)(2,1)S(1)}, bf16[2,1,5760]{2,1,0:T(2,128)(2,1)S(1)}, u32[]{:S(2)}, u32[]{:S(2)}) collective-permute-start(bf16[2,1,5760]{2,1,0:T(2,128)(2,1)S(1)} %broadcast_select_fusion.2), channel_id=1, source_target_pairs={{0,8},{8,0},{1,9},{9,1},{2,10},{10,2},{3,11},{11,3},{4,12},{12,4},... | collective-permute-start | bytes 69128 | tf_op jit(solution)/shard_map/ppermute | solution.py:127
